TPU v7x, 256 devices: a whole 4x4x8 slice. The times are simulated.
256 devices in a mesh: lon: 64 (over x_hi, z, y), lat: 4 (over x_lo, core).
Axes of the slice: x: 4 (x_hi: 2, x_lo: 2; x = x_hi * 2 + x_lo), y: 4, z: 8, core: 2. Of those that a mesh axis runs over, the one named last changes fastest.
Arguments:
- adjoint_final: float32 [10, 256, 16384], P(None, 'lat', 'lon'), may hold values from -6 to 6
- stored_tracer: float32 [4, 10, 256, 16384], P(None, None, 'lat', 'lon'), may hold values from -4 to 4
- stored_zonal: float32 [4, 10, 256, 16384], P(None, None, 'lat', 'lon'), may hold values from -4 to 4
- stored_meridional: float32 [4, 10, 256, 16384], P(None, None, 'lat', 'lon'), may hold values from -4 to 4
- diffusivity: float32 [256, 16384], P('lat', 'lon'), may hold values from 0.02 to 0.2
- level_mixing: float32 [10, 10], replicated, may hold values from -2 to 2
- wet_tiles: int32 [4, 128], P('lat', 'lon'), may hold values 0 or 1
- state_index: int32 [2], replicated, may hold values from 0 to 3, as said below
Outputs:
- adjoint_start: float32 [10, 256, 16384], P(None, 'lat', 'lon')
Inputs may be any that keep to these rules, and one draw needn't show every extreme that they name: The entries of state_index are distinct stored states, and one of them is the last stored state.
All inputs are finite; a program needn't handle non-finite values. No bound on the sum of `wet_tiles` on one device may be relied on, other than what follows from the above.
Results may differ from a plain program's by a relative error of at most 0.0001.
Values sent between devices are 32-bit elements; how exact they have to be, the bound alone decides.
No kernel may reach another device: no remote copies, remote signals or barrier semaphores. Data moves between devices by JAX's collectives and lax.ppermute only.
A program may use at most 64 MiB of HBM per device.

v0:
```python
import jax
import jax.numpy as jnp
from jax import lax
from jax.sharding import PartitionSpec as P

TLON = 128
STEPS = 2


advect_scale = 0.25
damping = 0.3


def partner(array, axis, distance):
    return lax.ppermute(array, axis, [(i, i ^ 1 << distance) for i in range(lax.axis_size(axis))])


def with_halo(block, sides, width, periodic):
    for axis, dim in sides:
        count = lax.axis_size(axis)
        forward = [(i, i + 1) for i in range(count - 1)]
        if periodic:
            forward.append((count - 1, 0))
        backward = [(target, source) for source, target in forward]
        low = lax.ppermute(
            lax.slice_in_dim(block, block.shape[dim] - width, None, axis=dim), axis, forward
        )
        high = lax.ppermute(lax.slice_in_dim(block, 0, width, axis=dim), axis, backward)
        block = jnp.concatenate([low, block, high], axis=dim)
    return block


def folded_rows(top_rows):
    bit_count = lax.axis_size("lon").bit_length() - 1
    moved = top_rows
    for bit_index in range(bit_count):
        moved = partner(moved, "lon", bit_index)
    return moved[..., ::-1]


def shards(
    adjoint_final,
    stored_tracer,
    stored_zonal,
    stored_meridional,
    diffusivity,
    level_mixing,
    wet_tiles,
    state_index,
):
    wet = jnp.repeat(wet_tiles[0], TLON).astype(jnp.float32)[None, None, :]
    is_top = lax.axis_index("lat") == lax.axis_size("lat") - 1
    adjoint = adjoint_final * wet
    for back in range(STEPS):
        chosen = state_index[STEPS - 1 - back]
        tracer = stored_tracer[chosen]
        zonal = stored_zonal[chosen]
        merid = stored_meridional[chosen]
        spread = diffusivity[None] * adjoint
        zonal_flux = zonal * adjoint
        merid_flux = merid * adjoint
        along_lon = with_halo(jnp.stack([spread, zonal_flux]), (("lon", 3),), 1, True)
        along_lat_src = jnp.stack([spread, merid_flux])
        along_lat = with_halo(along_lat_src, (("lat", 2),), 1, False)
        mirrored = folded_rows(along_lat_src[:, :, -1, :])
        last_north = jnp.where(is_top, mirrored, along_lat[:, :, -1, :])
        north_side = jnp.concatenate([along_lat[:, :, 2:-1, :], last_north[:, :, None, :]], axis=2)
        south_side = along_lat[:, :, :-2, :]
        east_side = along_lon[..., 2:]
        west_side = along_lon[..., :-2]
        nearby = east_side[0] + west_side[0] + north_side[0] + south_side[0]
        advect = east_side[1] - west_side[1] + north_side[1] - south_side[1]
        vertical = jnp.einsum("ml,mab->lab", level_mixing, adjoint, precision=lax.Precision.HIGHEST)
        adjoint = wet * (
            adjoint
            - 4.0 * spread
            + nearby
            + advect_scale * advect
            + vertical
            - damping * tracer * tracer * adjoint
        )
    return adjoint


def solution(mesh):
    return jax.shard_map(
        shards,
        mesh=mesh,
        in_specs=(
            P(None, "lat", "lon"),
            P(None, None, "lat", "lon"),
            P(None, None, "lat", "lon"),
            P(None, None, "lat", "lon"),
            P("lat", "lon"),
            P(),
            P("lat", "lon"),
            P(),
        ),
        out_specs=P(None, "lat", "lon"),
        check_vma=False,
    )
```

profile of v0, /device:TPU:1, one launch (start us, length us, event | category | flops | bytes accessed | tf_op | source)
XLA Modules:
  0.0 111.9 jit_solution(12171805550112810583)
XLA Ops:
  5.9 3.1 %constant_dynamic-slice_fusion.1 = (f32[1,10,64,256]{3,2,1,0:T(8,128)}, f32[1,10,64,256]{3,2,1,0:T(8,128)S(1)}, f32[1,10,64,256]{3,2,1,0:T(8,128)S(1)}, f32[1,10,64,256]{3,2,1,0:T(8,128)}) fusion(f32[4,10,64,256]{3,2,1,0:T(8,128)} %param.11, s32[]{:T(128)S(6)} %select_n.25, s32[]{:T(128)S(6)} %select_n.22, f32[4,10,64,256]{3,2,1,0:T(8,128)} %param.10), kind=kLoop, calls=%fused_computation.99 | loop fusion | bytes 5242888 | tf_op jit(solution)/shard_map/dynamic_slice | solution.py:58
  10.2 2.2 %collective-permute-start.2 = (f32[2,10,256]{2,1,0:T(8,128)S(1)}, f32[2,10,256]{2,1,0:T(8,128)S(1)}, u32[]{:S(2)}, u32[]{:S(2)}) collective-permute-start(f32[2,10,256]{2,1,0:T(8,128)S(1)} %bitcast.111), channel_id=1, source_target_pairs={{0,4},{4,0},{8,12},{12,8},{16,20},{20,16},{24,28},{28,24},{32,36},... | collective-permute-start | bytes 61448 | tf_op jit(solution)/shard_map/ppermute | solution.py:15
  13.7 3.1 %collective-permute-start.3 = (f32[2,10,256]{2,1,0:T(8,128)S(1)}, f32[2,10,256]{2,1,0:T(8,128)S(1)}, u32[]{:S(2)}, u32[]{:S(2)}) collective-permute-start(f32[2,10,256]{2,1,0:T(8,128)S(1)} %collective-permute-done.2), channel_id=1, source_target_pairs={{0,8},{4,12},{8,0},{12,4},{16,24},{20,28},{24,16},{28,20},{32,40},... | collective-permute-start | bytes 61448 | tf_op jit(solution)/shard_map/ppermute | solution.py:15
  18.1 1.7 %collective-permute-start.4 = (f32[2,10,256]{2,1,0:T(8,128)S(1)}, f32[2,10,256]{2,1,0:T(8,128)S(1)}, u32[]{:S(2)}, u32[]{:S(2)}) collective-permute-start(f32[2,10,256]{2,1,0:T(8,128)S(1)} %collective-permute-done.3), channel_id=1, source_target_pairs={{0,16},{4,20},{8,24},{12,28},{16,0},{20,4},{24,8},{28,12},{32,48},... | collective-permute-start | bytes 61448 | tf_op jit(solution)/shard_map/ppermute | solution.py:15
  19.8 6.2 %collective-permute-start.9 = (f32[2,10,1,256]{3,1,0,2:T(8,128)S(1)}, f32[2,10,1,256]{3,1,0,2:T(8,128)S(1)}, u32[]{:S(2)}, u32[]{:S(2)}) collective-permute-start(f32[2,10,1,256]{3,1,0,2:T(8,128)S(1)} %bitcast.112), channel_id=1, source_target_pairs={{0,1},{1,2},{2,3},{4,5},{5,6},{6,7},{8,9},{9,10},{10,11},{12,13},{... | collective-permute-start | bytes 61448 | tf_op jit(solution)/shard_map/ppermute | solution.py:25
  26.1 1.9 %collective-permute-start.8 = (f32[2,10,1,256]{3,1,0,2:T(8,128)S(1)}, f32[2,10,1,256]{3,1,0,2:T(8,128)S(1)}, u32[]{:S(2)}, u32[]{:S(2)}) collective-permute-start(f32[2,10,1,256]{3,1,0,2:T(8,128)S(1)} %get-tuple-element.17), channel_id=1, source_target_pairs={{1,0},{2,1},{3,2},{5,4},{6,5},{7,6},{9,8},{10,9},{11,10},{13,12},{... | collective-permute-start | bytes 61448 | tf_op jit(solution)/shard_map/ppermute | solution.py:28
  28.0 3.1 %collective-permute-start.5 = (f32[2,10,256]{2,1,0:T(8,128)S(1)}, f32[2,10,256]{2,1,0:T(8,128)S(1)}, u32[]{:S(2)}, u32[]{:S(2)}) collective-permute-start(f32[2,10,256]{2,1,0:T(8,128)S(1)} %collective-permute-done.4), channel_id=1, source_target_pairs={{0,32},{4,36},{8,40},{12,44},{16,48},{20,52},{24,56},{28,60},{32,0... | collective-permute-start | bytes 61448 | tf_op jit(solution)/shard_map/ppermute | solution.py:15
  32.4 1.5 %copy.30 = f32[2,10,64,1]{2,0,3,1:T(2,128)S(1)} copy(f32[2,10,64,1]{3,1,2,0:T(8,128)} %get-tuple-element.16) | data formatting | bytes 10240 | tf_op jit(solution)/shard_map/slice | solution.py:26
  35.6 6.2 %collective-permute-start = (f32[2,10,64,1]{2,0,3,1:T(2,128)S(1)}, f32[2,10,64,1]{2,0,3,1:T(2,128)S(1)}, u32[]{:S(2)}, u32[]{:S(2)}) collective-permute-start(f32[2,10,64,1]{2,0,3,1:T(2,128)S(1)} %copy.28), channel_id=1, source_target_pairs={{4,0},{8,4},{12,8},{16,12},{20,16},{24,20},{28,24},{32,28},{36,32}... | collective-permute-start | bytes 15368 | tf_op jit(solution)/shard_map/ppermute | solution.py:28
  41.9 1.5 %collective-permute-start.6 = (f32[2,10,256]{2,1,0:T(8,128)S(1)}, f32[2,10,256]{2,1,0:T(8,128)S(1)}, u32[]{:S(2)}, u32[]{:S(2)}) collective-permute-start(f32[2,10,256]{2,1,0:T(8,128)S(1)} %collective-permute-done.5), channel_id=1, source_target_pairs={{0,64},{4,68},{8,72},{12,76},{16,80},{20,84},{24,88},{28,92},{32,9... | collective-permute-start | bytes 61448 | tf_op jit(solution)/shard_map/ppermute | solution.py:15
  43.4 1.6 %fusion.1 = f32[2,10,63,256]{3,1,2,0:T(8,128)} fusion(f32[1,10,64,256]{3,1,2,0:T(8,128)S(1)} %get-tuple-element.23, f32[1,10,64,256]{3,1,2,0:T(8,128)S(1)} %get-tuple-element.24), kind=kLoop, calls=%fused_computation.17 | loop fusion | flops 322560 | bytes 2600960 | tf_op jit(solution)/shard_map/stack | solution.py:63
  45.0 3.6 %collective-permute-done.6 = f32[2,10,256]{2,1,0:T(8,128)S(1)} collective-permute-done((f32[2,10,256]{2,1,0:T(8,128)S(1)}, f32[2,10,256]{2,1,0:T(8,128)S(1)}, u32[]{:S(2)}, u32[]{:S(2)}) %collective-permute-start.6) | collective-permute-done | bytes 20512 | tf_op jit(solution)/shard_map/ppermute | solution.py:15
  48.6 2.2 %collective-permute-start.7 = (f32[2,10,256]{2,1,0:T(8,128)S(1)}, f32[2,10,256]{2,1,0:T(8,128)S(1)}, u32[]{:S(2)}, u32[]{:S(2)}) collective-permute-start(f32[2,10,256]{2,1,0:T(8,128)S(1)} %collective-permute-done.6), channel_id=1, source_target_pairs={{0,128},{4,132},{8,136},{12,140},{16,144},{20,148},{24,152},{28,15... | collective-permute-start | bytes 61448 | tf_op jit(solution)/shard_map/ppermute | solution.py:15
  55.0 6.1 %fusion.7 = f32[10,64,256]{2,0,1:T(8,128)S(1)} fusion(f32[2,10,63,256]{3,1,2,0:T(8,128)} %fusion.1, f32[2,10,1,256]{3,1,2,0:T(8,128)S(1)} %fusion.47, f32[2,10,1,256]{3,1,2,0:T(8,128)S(1)} %bitcast.115, f32[1,10,64,256]{3,1,2,0:T(8,128)S(1)} %get-tuple-element.23, f32[1,10,64,256]{3,1,2,0:T(8,128)S(1)} %get-tuple-element.24, f32[2,10,64,1]{3,1,2,0:T(8,128)} %copy.31, ...), kind=kOutput, calls=%fused_computation.27 | convolution fusion | flops 25231360 | bytes 10070016 | tf_op jit(solution)/shard_map/ml,mab->lab/dot_general | solution.py:73
  62.2 2.8 %collective-permute-done.12 = f32[2,10,256]{2,1,0:T(8,128)S(1)} collective-permute-done((f32[2,10,256]{2,1,0:T(8,128)S(1)}, f32[2,10,256]{2,1,0:T(8,128)S(1)}, u32[]{:S(2)}, u32[]{:S(2)}) %collective-permute-start.12) | collective-permute-done | bytes 20512 | tf_op jit(solution)/shard_map/ppermute | solution.py:15
  65.0 4.3 %collective-permute-done.13 = f32[2,10,256]{2,1,0:T(8,128)S(1)} collective-permute-done((f32[2,10,256]{2,1,0:T(8,128)S(1)}, f32[2,10,256]{2,1,0:T(8,128)S(1)}, u32[]{:S(2)}, u32[]{:S(2)}) %collective-permute-start.13) | collective-permute-done | bytes 20512 | tf_op jit(solution)/shard_map/ppermute | solution.py:15
  69.3 2.8 %collective-permute-done.14 = f32[2,10,256]{2,1,0:T(8,128)S(1)} collective-permute-done((f32[2,10,256]{2,1,0:T(8,128)S(1)}, f32[2,10,256]{2,1,0:T(8,128)S(1)}, u32[]{:S(2)}, u32[]{:S(2)}) %collective-permute-start.14) | collective-permute-done | bytes 20512 | tf_op jit(solution)/shard_map/ppermute | solution.py:15
  72.0 6.0 %collective-permute-start.18 = (f32[2,10,1,256]{3,1,2,0:T(8,128)S(1)}, f32[2,10,1,256]{3,1,2,0:T(8,128)S(1)}, u32[]{:S(2)}, u32[]{:S(2)}) collective-permute-start(f32[2,10,1,256]{3,1,2,0:T(8,128)S(1)} %get-tuple-element.13), channel_id=1, source_target_pairs={{1,0},{2,1},{3,2},{5,4},{6,5},{7,6},{9,8},{10,9},{11,10},{13,12},{... | collective-permute-start | bytes 61448 | tf_op jit(solution)/shard_map/ppermute | solution.py:28
  78.1 1.9 %collective-permute-start.16 = (f32[2,10,256]{2,1,0:T(8,128)S(1)}, f32[2,10,256]{2,1,0:T(8,128)S(1)}, u32[]{:S(2)}, u32[]{:S(2)}) collective-permute-start(f32[2,10,256]{2,1,0:T(8,128)S(1)} %collective-permute-done.15), channel_id=1, source_target_pairs={{0,64},{4,68},{8,72},{12,76},{16,80},{20,84},{24,88},{28,92},{32,9... | collective-permute-start | bytes 61448 | tf_op jit(solution)/shard_map/ppermute | solution.py:15
  81.3 1.5 %copy.40 = f32[2,10,64,1]{2,0,3,1:T(2,128)S(1)} copy(f32[2,10,64,1]{3,1,2,0:T(8,128)} %get-tuple-element.11) | data formatting | bytes 10240 | tf_op jit(solution)/shard_map/slice | solution.py:28
  83.3 7.2 %collective-permute-start.10 = (f32[2,10,64,1]{2,0,3,1:T(2,128)S(1)}, f32[2,10,64,1]{2,0,3,1:T(2,128)S(1)}, u32[]{:S(2)}, u32[]{:S(2)}) collective-permute-start(f32[2,10,64,1]{2,0,3,1:T(2,128)S(1)} %copy.40), channel_id=1, source_target_pairs={{4,0},{8,4},{12,8},{16,12},{20,16},{24,20},{28,24},{32,28},{36,32}... | collective-permute-start | bytes 15368 | tf_op jit(solution)/shard_map/ppermute | solution.py:28
  91.9 1.6 %fusion = f32[2,10,63,256]{3,1,2,0:T(8,128)} fusion(f32[1,10,64,256]{3,1,2,0:T(8,128)S(1)} %get-tuple-element.20, f32[1,10,64,256]{3,1,2,0:T(8,128)S(1)} %get-tuple-element.21), kind=kLoop, calls=%fused_computation.16 | loop fusion | flops 322560 | bytes 2600960 | tf_op jit(solution)/shard_map/stack | solution.py:63
  93.4 8.6 %collective-permute-start.19 = (f32[2,10,1,256]{3,1,0,2:T(8,128)S(1)}, f32[2,10,1,256]{3,1,0,2:T(8,128)S(1)}, u32[]{:S(2)}, u32[]{:S(2)}) collective-permute-start(f32[2,10,1,256]{3,1,0,2:T(8,128)S(1)} %bitcast.114), channel_id=1, source_target_pairs={{0,1},{1,2},{2,3},{4,5},{5,6},{6,7},{8,9},{9,10},{10,11},{12,13},{... | collective-permute-start | bytes 61448 | tf_op jit(solution)/shard_map/ppermute | solution.py:25
  105.2 5.5 %fusion.4 = f32[10,64,256]{2,0,1:T(8,128)S(1)} fusion(f32[10,64,256]{2,0,1:T(8,128)} %copy-done.7, f32[2,10,63,256]{3,1,2,0:T(8,128)} %fusion, f32[2,10,1,256]{3,1,2,0:T(8,128)S(1)} %fusion.46, f32[2,10,1,256]{3,1,2,0:T(8,128)S(1)} %bitcast.116, f32[1,10,64,256]{3,1,2,0:T(8,128)S(1)} %get-tuple-element.20, f32[1,10,64,256]{3,1,2,0:T(8,128)S(1)} %get-tuple-element.21, ...), kind=kOutput, calls=%fused_computation.23 | convolution fusion | flops 24903680 | bytes 9643408 | tf_op jit(solution)/shard_map/ml,mab->lab/dot_general | solution.py:73
  (66 shorter events, 21.7 us)
Async XLA Ops:
  0.0 55.0 %copy-start = (f32[10,10]{1,0:T(8,128)S(1)}, f32[10,10]{1,0:T(8,128)}, u32[]{:S(2)}) copy-start(f32[10,10]{1,0:T(8,128)} %param.13) | copy-start | bytes 1204
  10.2 22.2 %copy-start.1 = (f32[1,10,64,256]{3,1,2,0:T(8,128)}, f32[1,10,64,256]{3,1,2,0:T(8,128)S(1)}, u32[]{:S(2)}) copy-start(f32[1,10,64,256]{3,1,2,0:T(8,128)S(1)} %get-tuple-element.22) | copy-start | bytes 1966084
  10.2 3.5 %collective-permute-start.2 = (f32[2,10,256]{2,1,0:T(8,128)S(1)}, f32[2,10,256]{2,1,0:T(8,128)S(1)}, u32[]{:S(2)}, u32[]{:S(2)}) collective-permute-start(f32[2,10,256]{2,1,0:T(8,128)S(1)} %bitcast.111), channel_id=1, source_target_pairs={{0,4},{4,0},{8,12},{12,8},{16,20},{20,16},{24,28},{28,24},{32,36},... | collective-permute-start | bytes 61448 | tf_op jit(solution)/shard_map/ppermute | solution.py:15
  13.7 4.4 %collective-permute-start.3 = (f32[2,10,256]{2,1,0:T(8,128)S(1)}, f32[2,10,256]{2,1,0:T(8,128)S(1)}, u32[]{:S(2)}, u32[]{:S(2)}) collective-permute-start(f32[2,10,256]{2,1,0:T(8,128)S(1)} %collective-permute-done.2), channel_id=1, source_target_pairs={{0,8},{4,12},{8,0},{12,4},{16,24},{20,28},{24,16},{28,20},{32,40},... | collective-permute-start | bytes 61448 | tf_op jit(solution)/shard_map/ppermute | solution.py:15
  18.1 9.9 %collective-permute-start.4 = (f32[2,10,256]{2,1,0:T(8,128)S(1)}, f32[2,10,256]{2,1,0:T(8,128)S(1)}, u32[]{:S(2)}, u32[]{:S(2)}) collective-permute-start(f32[2,10,256]{2,1,0:T(8,128)S(1)} %collective-permute-done.3), channel_id=1, source_target_pairs={{0,16},{4,20},{8,24},{12,28},{16,0},{20,4},{24,8},{28,12},{32,48},... | collective-permute-start | bytes 61448 | tf_op jit(solution)/shard_map/ppermute | solution.py:15
  19.8 35.2 %collective-permute-start.9 = (f32[2,10,1,256]{3,1,0,2:T(8,128)S(1)}, f32[2,10,1,256]{3,1,0,2:T(8,128)S(1)}, u32[]{:S(2)}, u32[]{:S(2)}) collective-permute-start(f32[2,10,1,256]{3,1,0,2:T(8,128)S(1)} %bitcast.112), channel_id=1, source_target_pairs={{0,1},{1,2},{2,3},{4,5},{5,6},{6,7},{8,9},{9,10},{10,11},{12,13},{... | collective-permute-start | bytes 61448 | tf_op jit(solution)/shard_map/ppermute | solution.py:25
  26.1 28.9 %collective-permute-start.8 = (f32[2,10,1,256]{3,1,0,2:T(8,128)S(1)}, f32[2,10,1,256]{3,1,0,2:T(8,128)S(1)}, u32[]{:S(2)}, u32[]{:S(2)}) collective-permute-start(f32[2,10,1,256]{3,1,0,2:T(8,128)S(1)} %get-tuple-element.17), channel_id=1, source_target_pairs={{1,0},{2,1},{3,2},{5,4},{6,5},{7,6},{9,8},{10,9},{11,10},{13,12},{... | collective-permute-start | bytes 61448 | tf_op jit(solution)/shard_map/ppermute | solution.py:28
  28.0 13.9 %collective-permute-start.5 = (f32[2,10,256]{2,1,0:T(8,128)S(1)}, f32[2,10,256]{2,1,0:T(8,128)S(1)}, u32[]{:S(2)}, u32[]{:S(2)}) collective-permute-start(f32[2,10,256]{2,1,0:T(8,128)S(1)} %collective-permute-done.4), channel_id=1, source_target_pairs={{0,32},{4,36},{8,40},{12,44},{16,48},{20,52},{24,56},{28,60},{32,0... | collective-permute-start | bytes 61448 | tf_op jit(solution)/shard_map/ppermute | solution.py:15
  34.0 19.4 %collective-permute-start.1 = (f32[2,10,64,1]{2,0,3,1:T(2,128)S(1)}, f32[2,10,64,1]{2,0,3,1:T(2,128)S(1)}, u32[]{:S(2)}, u32[]{:S(2)}) collective-permute-start(f32[2,10,64,1]{2,0,3,1:T(2,128)S(1)} %copy.30), channel_id=1, source_target_pairs={{0,4},{4,8},{8,12},{12,16},{16,20},{20,24},{24,28},{28,32},{32,36}... | collective-permute-start | bytes 15368 | tf_op jit(solution)/shard_map/ppermute | solution.py:25
  35.6 15.1 %copy-start.8 = (f32[4,10,64,256]{3,2,1,0:T(8,128)S(1)}, f32[4,10,64,256]{3,2,1,0:T(8,128)}, u32[]{:S(2)}) copy-start(f32[4,10,64,256]{3,2,1,0:T(8,128)} %param.9) | copy-start | bytes 7864324
  35.6 16.2 %collective-permute-start = (f32[2,10,64,1]{2,0,3,1:T(2,128)S(1)}, f32[2,10,64,1]{2,0,3,1:T(2,128)S(1)}, u32[]{:S(2)}, u32[]{:S(2)}) collective-permute-start(f32[2,10,64,1]{2,0,3,1:T(2,128)S(1)} %copy.28), channel_id=1, source_target_pairs={{4,0},{8,4},{12,8},{16,12},{20,16},{24,20},{28,24},{32,28},{36,32}... | collective-permute-start | bytes 15368 | tf_op jit(solution)/shard_map/ppermute | solution.py:28
  41.9 6.7 %collective-permute-start.6 = (f32[2,10,256]{2,1,0:T(8,128)S(1)}, f32[2,10,256]{2,1,0:T(8,128)S(1)}, u32[]{:S(2)}, u32[]{:S(2)}) collective-permute-start(f32[2,10,256]{2,1,0:T(8,128)S(1)} %collective-permute-done.5), channel_id=1, source_target_pairs={{0,64},{4,68},{8,72},{12,76},{16,80},{20,84},{24,88},{28,92},{32,9... | collective-permute-start | bytes 61448 | tf_op jit(solution)/shard_map/ppermute | solution.py:15
  48.6 6.2 %collective-permute-start.7 = (f32[2,10,256]{2,1,0:T(8,128)S(1)}, f32[2,10,256]{2,1,0:T(8,128)S(1)}, u32[]{:S(2)}, u32[]{:S(2)}) collective-permute-start(f32[2,10,256]{2,1,0:T(8,128)S(1)} %collective-permute-done.6), channel_id=1, source_target_pairs={{0,128},{4,132},{8,136},{12,140},{16,144},{20,148},{24,152},{28,15... | collective-permute-start | bytes 61448 | tf_op jit(solution)/shard_map/ppermute | solution.py:15
  62.1 19.2 %copy-start.3 = (f32[1,10,64,256]{3,1,2,0:T(8,128)}, f32[1,10,64,256]{3,1,2,0:T(8,128)S(1)}, u32[]{:S(2)}) copy-start(f32[1,10,64,256]{3,1,2,0:T(8,128)S(1)} %get-tuple-element.19) | copy-start | bytes 1966084
  62.1 2.9 %collective-permute-start.12 = (f32[2,10,256]{2,1,0:T(8,128)S(1)}, f32[2,10,256]{2,1,0:T(8,128)S(1)}, u32[]{:S(2)}, u32[]{:S(2)}) collective-permute-start(f32[2,10,256]{2,1,0:T(8,128)S(1)} %bitcast.113), channel_id=1, source_target_pairs={{0,4},{4,0},{8,12},{12,8},{16,20},{20,16},{24,28},{28,24},{32,36},... | collective-permute-start | bytes 61448 | tf_op jit(solution)/shard_map/ppermute | solution.py:15
  65.0 4.3 %collective-permute-start.13 = (f32[2,10,256]{2,1,0:T(8,128)S(1)}, f32[2,10,256]{2,1,0:T(8,128)S(1)}, u32[]{:S(2)}, u32[]{:S(2)}) collective-permute-start(f32[2,10,256]{2,1,0:T(8,128)S(1)} %collective-permute-done.12), channel_id=1, source_target_pairs={{0,8},{4,12},{8,0},{12,4},{16,24},{20,28},{24,16},{28,20},{32,40},... | collective-permute-start | bytes 61448 | tf_op jit(solution)/shard_map/ppermute | solution.py:15
  69.3 2.8 %collective-permute-start.14 = (f32[2,10,256]{2,1,0:T(8,128)S(1)}, f32[2,10,256]{2,1,0:T(8,128)S(1)}, u32[]{:S(2)}, u32[]{:S(2)}) collective-permute-start(f32[2,10,256]{2,1,0:T(8,128)S(1)} %collective-permute-done.13), channel_id=1, source_target_pairs={{0,16},{4,20},{8,24},{12,28},{16,0},{20,4},{24,8},{28,12},{32,48},... | collective-permute-start | bytes 61448 | tf_op jit(solution)/shard_map/ppermute | solution.py:15
  72.0 6.0 %collective-permute-start.15 = (f32[2,10,256]{2,1,0:T(8,128)S(1)}, f32[2,10,256]{2,1,0:T(8,128)S(1)}, u32[]{:S(2)}, u32[]{:S(2)}) collective-permute-start(f32[2,10,256]{2,1,0:T(8,128)S(1)} %collective-permute-done.14), channel_id=1, source_target_pairs={{0,32},{4,36},{8,40},{12,44},{16,48},{20,52},{24,56},{28,60},{32,0... | collective-permute-start | bytes 61448 | tf_op jit(solution)/shard_map/ppermute | solution.py:15
  72.0 33.1 %collective-permute-start.18 = (f32[2,10,1,256]{3,1,2,0:T(8,128)S(1)}, f32[2,10,1,256]{3,1,2,0:T(8,128)S(1)}, u32[]{:S(2)}, u32[]{:S(2)}) collective-permute-start(f32[2,10,1,256]{3,1,2,0:T(8,128)S(1)} %get-tuple-element.13), channel_id=1, source_target_pairs={{1,0},{2,1},{3,2},{5,4},{6,5},{7,6},{9,8},{10,9},{11,10},{13,12},{... | collective-permute-start | bytes 61448 | tf_op jit(solution)/shard_map/ppermute | solution.py:28
  78.1 12.4 %collective-permute-start.16 = (f32[2,10,256]{2,1,0:T(8,128)S(1)}, f32[2,10,256]{2,1,0:T(8,128)S(1)}, u32[]{:S(2)}, u32[]{:S(2)}) collective-permute-start(f32[2,10,256]{2,1,0:T(8,128)S(1)} %collective-permute-done.15), channel_id=1, source_target_pairs={{0,64},{4,68},{8,72},{12,76},{16,80},{20,84},{24,88},{28,92},{32,9... | collective-permute-start | bytes 61448 | tf_op jit(solution)/shard_map/ppermute | solution.py:15
  83.2 20.3 %collective-permute-start.11 = (f32[2,10,64,1]{2,0,3,1:T(2,128)S(1)}, f32[2,10,64,1]{2,0,3,1:T(2,128)S(1)}, u32[]{:S(2)}, u32[]{:S(2)}) collective-permute-start(f32[2,10,64,1]{2,0,3,1:T(2,128)S(1)} %copy.42), channel_id=1, source_target_pairs={{0,4},{4,8},{8,12},{12,16},{16,20},{20,24},{24,28},{28,32},{32,36}... | collective-permute-start | bytes 15368 | tf_op jit(solution)/shard_map/ppermute | solution.py:25
  83.3 18.8 %collective-permute-start.10 = (f32[2,10,64,1]{2,0,3,1:T(2,128)S(1)}, f32[2,10,64,1]{2,0,3,1:T(2,128)S(1)}, u32[]{:S(2)}, u32[]{:S(2)}) collective-permute-start(f32[2,10,64,1]{2,0,3,1:T(2,128)S(1)} %copy.40), channel_id=1, source_target_pairs={{4,0},{8,4},{12,8},{16,12},{20,16},{24,20},{28,24},{32,28},{36,32}... | collective-permute-start | bytes 15368 | tf_op jit(solution)/shard_map/ppermute | solution.py:28
  90.5 14.5 %collective-permute-start.17 = (f32[2,10,256]{2,1,0:T(8,128)S(1)}, f32[2,10,256]{2,1,0:T(8,128)S(1)}, u32[]{:S(2)}, u32[]{:S(2)}) collective-permute-start(f32[2,10,256]{2,1,0:T(8,128)S(1)} %collective-permute-done.16), channel_id=1, source_target_pairs={{0,128},{4,132},{8,136},{12,140},{16,144},{20,148},{24,152},{28,15... | collective-permute-start | bytes 61448 | tf_op jit(solution)/shard_map/ppermute | solution.py:15
  93.4 11.7 %collective-permute-start.19 = (f32[2,10,1,256]{3,1,0,2:T(8,128)S(1)}, f32[2,10,1,256]{3,1,0,2:T(8,128)S(1)}, u32[]{:S(2)}, u32[]{:S(2)}) collective-permute-start(f32[2,10,1,256]{3,1,0,2:T(8,128)S(1)} %bitcast.114), channel_id=1, source_target_pairs={{0,1},{1,2},{2,3},{4,5},{5,6},{6,7},{8,9},{9,10},{10,11},{12,13},{... | collective-permute-start | bytes 61448 | tf_op jit(solution)/shard_map/ppermute | solution.py:25
  (7 other events, 41.3 us)
where the time goes:
time: 112 us
  starting transfers between devices  54.7 us (49%)
  local copies, waits for them, and re-layouts  16.9 us (15%)
  waiting for transfers between devices  16 us (14%)
  matrix products  11.6 us (10%)
  other arithmetic  8.58 us (8%)
  between operations  4.07 us (4%)
    ppermute x4, starting transfers between devices, with_halo(): lax.ppermute(lax.slice_in_dim(block, 0, width, axis=dim), axis, backward)  21.3 us
    ppermute x12, starting transfers between devices, partner(): lax.ppermute(array, axis, [(i, i ^ 1 << distance) for i in range(lax.axis...  17.1 us
    ppermute x4, starting transfers between devices, with_halo(): lax.ppermute(lax.slice_in_dim(block, block.shape[dim] - width, None, axis...  16.3 us
    ppermute x12, waiting for transfers between devices, partner(): lax.ppermute(array, axis, [(i, i ^ 1 << distance) for i in range(lax.axis...  16 us
    dot_general x2, matrix products, shards(): jnp.einsum('ml,mab->lab', level_mixing, adjoint, precision=lax.Precision....  11.6 us
    another operation x4, other arithmetic, shards(): jnp.stack([spread, zonal_flux])  4.75 us
    another operation x3, other arithmetic, shards(): along_lat_src = jnp.stack([spread, merid_flux])  3.15 us
    dynamic_slice x1, local copies, waits for them, and re-layouts, shards(): merid = stored_meridional[chosen]  3.1 us
  transfers between devices with their start and end apart: 20, of which 6 were waited for; matrix products, arithmetic and copies ran while one was open for 15% of the time, Pallas kernels for 0%

commit v1 on v0

v1 whole, which is shorter than its diff:
```python
import functools

import jax
import jax.numpy as jnp
from jax import lax
from jax.experimental import pallas as pl
from jax.experimental.pallas import tpu as pltpu
from jax.sharding import PartitionSpec as P

TLON = 128
STEPS = 2


advect_scale = 0.25
damping = 0.3


def shift_pairs(count, delta, periodic):
    pairs = []
    for i in range(count):
        j = i + delta
        if periodic:
            pairs.append((i, j % count))
        elif 0 <= j < count:
            pairs.append((i, j))
    return pairs


def as_column(row, size):
    spread_rows = jnp.broadcast_to(row, (size, size))
    r = lax.broadcasted_iota(jnp.int32, (size, size), 0)
    c = lax.broadcasted_iota(jnp.int32, (size, size), 1)
    return jnp.sum(jnp.where(r == c, spread_rows, 0.0), axis=1, keepdims=True)


def step_kernel(
    first,
    si_ref,
    wt_ref,
    flag_ref,
    lm_ref,
    adj_ref,
    d_ref,
    t_ref,
    u_ref,
    v_ref,
    he_ref,
    hw_ref,
    hn_ref,
    hf_ref,
    hs_ref,
    out_ref,
):
    del si_ref
    l = pl.program_id(0)
    levels, rows, width = adj_ref.shape
    lane = lax.broadcasted_iota(jnp.int32, (rows, width), 1)
    row = lax.broadcasted_iota(jnp.int32, (rows, width), 0)

    wet_i = jnp.zeros((rows, width), jnp.int32)
    for t in range(width // TLON):
        inside = (lane >= t * TLON) & (lane < (t + 1) * TLON)
        wet_i = jnp.where(inside, wt_ref[t], wet_i)
    wet = wet_i.astype(jnp.float32)

    def level(m):
        a_m = adj_ref[m]
        return a_m * wet if first else a_m

    a = level(l)
    vertical = lm_ref[0, l] * level(0)
    for m in range(1, levels):
        vertical = vertical + lm_ref[m, l] * level(m)

    s = d_ref[...] * a
    zf = u_ref[...] * a
    mf = v_ref[...] * a
    east_src = s + advect_scale * zf
    west_src = s - advect_scale * zf
    north_src = s + advect_scale * mf
    south_src = s - advect_scale * mf

    east_col = as_column(he_ref[pl.ds(l, 1), :], rows)
    west_col = as_column(hw_ref[pl.ds(l, 1), :], rows)
    top = flag_ref[0] == 1
    north_row = jnp.where(top, hf_ref[pl.ds(l, 1), :], hn_ref[pl.ds(l, 1), :])
    south_row = hs_ref[pl.ds(l, 1), :]

    east = jnp.where(lane == width - 1, east_col, pltpu.roll(east_src, width - 1, 1))
    west = jnp.where(lane == 0, west_col, pltpu.roll(west_src, 1, 1))
    north = jnp.where(row == rows - 1, north_row, pltpu.roll(north_src, rows - 1, 0))
    south = jnp.where(row == 0, south_row, pltpu.roll(south_src, 1, 0))

    t = t_ref[...]
    out_ref[...] = wet * (
        a - 4.0 * s + east + west + north + south + vertical - damping * t * t * a
    )


def run_step(k, first, si, wt, flags, lm, adj, d, tracer, zonal, merid, he, hw, hn, hf, hs):
    levels, rows, width = adj.shape
    full3 = pl.BlockSpec((levels, rows, width), lambda l, *_: (0, 0, 0))
    full2 = pl.BlockSpec((rows, width), lambda l, *_: (0, 0))
    state = pl.BlockSpec((None, None, rows, width), lambda l, si, *_: (si[k], l, 0, 0))
    lon_halo = pl.BlockSpec((levels, rows), lambda l, *_: (0, 0))
    lat_halo = pl.BlockSpec((levels, width), lambda l, *_: (0, 0))
    n = levels * rows * width
    return pl.pallas_call(
        functools.partial(step_kernel, first),
        out_shape=jax.ShapeDtypeStruct(adj.shape, jnp.float32),
        grid_spec=pltpu.PrefetchScalarGridSpec(
            num_scalar_prefetch=3,
            grid=(levels,),
            in_specs=[
                pl.BlockSpec(memory_space=pltpu.SMEM),
                full3,
                full2,
                state,
                state,
                state,
                lon_halo,
                lon_halo,
                lat_halo,
                lat_halo,
                lat_halo,
            ],
            out_specs=pl.BlockSpec((None, rows, width), lambda l, *_: (l, 0, 0)),
        ),
        cost_estimate=pl.CostEstimate(flops=60 * n, bytes_accessed=24 * n, transcendentals=0),
    )(si, wt, flags, lm, adj, d, tracer, zonal, merid, he, hw, hn, hf, hs)


def shards(
    adjoint_final,
    stored_tracer,
    stored_zonal,
    stored_meridional,
    diffusivity,
    level_mixing,
    wet_tiles,
    state_index,
):
    n_lat = lax.axis_size("lat")
    n_lon = lax.axis_size("lon")
    levels, rows, width = adjoint_final.shape
    wt = wet_tiles.reshape(-1)
    wet_row = jnp.repeat(wt, TLON).astype(jnp.float32)
    is_top = lax.axis_index("lat") == n_lat - 1
    flags = is_top.astype(jnp.int32).reshape(1)

    to_west = shift_pairs(n_lon, -1, True)
    to_east = shift_pairs(n_lon, 1, True)
    to_south = shift_pairs(n_lat, -1, False)
    to_north = shift_pairs(n_lat, 1, False)
    top = n_lat - 1
    fold = [(j * n_lat + top, (n_lon - 1 - j) * n_lat + top) for j in range(n_lon)]

    adj = adjoint_final
    for back in range(STEPS):
        k = STEPS - 1 - back
        first = back == 0
        chosen = state_index[k]
        a = adj * wet_row if first else adj
        zonal = lax.dynamic_index_in_dim(stored_zonal, chosen, 0, keepdims=False)
        merid = lax.dynamic_index_in_dim(stored_meridional, chosen, 0, keepdims=False)
        a_w, a_e = a[:, :, 0], a[:, :, width - 1]
        a_s, a_n = a[:, 0, :], a[:, rows - 1, :]
        east_payload = diffusivity[:, 0] * a_w + advect_scale * (zonal[:, :, 0] * a_w)
        west_payload = diffusivity[:, width - 1] * a_e - advect_scale * (zonal[:, :, width - 1] * a_e)
        north_payload = diffusivity[0] * a_s + advect_scale * (merid[:, 0, :] * a_s)
        south_payload = diffusivity[rows - 1] * a_n - advect_scale * (merid[:, rows - 1, :] * a_n)
        fold_payload = (diffusivity[rows - 1] * a_n + advect_scale * (merid[:, rows - 1, :] * a_n))[:, ::-1]

        he = lax.ppermute(east_payload, "lon", to_west)
        hw = lax.ppermute(west_payload, "lon", to_east)
        hn = lax.ppermute(north_payload, "lat", to_south)
        hs = lax.ppermute(south_payload, "lat", to_north)
        hf = lax.ppermute(fold_payload, ("lon", "lat"), fold)
        adj = run_step(
            k, first, state_index, wt, flags, level_mixing, adj, diffusivity,
            stored_tracer, stored_zonal, stored_meridional, he, hw, hn, hf, hs,
        )
    return adj


def solution(mesh):
    return jax.shard_map(
        shards,
        mesh=mesh,
        in_specs=(
            P(None, "lat", "lon"),
            P(None, None, "lat", "lon"),
            P(None, None, "lat", "lon"),
            P(None, None, "lat", "lon"),
            P("lat", "lon"),
            P(),
            P("lat", "lon"),
            P(),
        ),
        out_specs=P(None, "lat", "lon"),
        check_vma=False,
    )
```

time: 112 us -> 87.6 us (0.78)
  the two profiles are of different devices: /device:TPU:1 before, /device:TPU:2 now
where the time goes in v1:
time: 87.6 us; the launch traced here: 86.4 us
  starting transfers between devices  42.5 us (49%)
  local copies, waits for them, and re-layouts  19.1 us (22%)
  Pallas kernels  16 us (18%)
  between operations  3.93 us (4%)
  other arithmetic  3.16 us (4%)
  waiting for transfers between devices  1.65 us (2%)
    ppermute x2, starting transfers between devices, shards(): hs = lax.ppermute(south_payload, 'lat', to_north)  21.8 us
    pallas_call x2, Pallas kernels, run_step(): pl.pallas_call(functools.partial(step_kernel, first), out_shape=jax.Shape...  16 us
    ppermute x2, starting transfers between devices, shards(): he = lax.ppermute(east_payload, 'lon', to_west)  15.3 us
    dynamic_slice x3, local copies, waits for them, and re-layouts, shards(): lax.dynamic_index_in_dim(stored_meridional, chosen, 0, keepdims=False)  4.61 us
    ppermute x2, starting transfers between devices, shards(): hn = lax.ppermute(north_payload, 'lat', to_south)  3.84 us
    slice x4, local copies, waits for them, and re-layouts, shards(): a_w, a_e = (a[:, :, 0], a[:, :, width - 1])  3.79 us
    dynamic_slice x2, local copies, waits for them, and re-layouts, shards(): zonal = lax.dynamic_index_in_dim(stored_zonal, chosen, 0, keepdims=False)  3.78 us
    unnamed x36, local copies, waits for them, and re-layouts  2.23 us
  transfers between devices with their start and end apart: 10, of which 1 were waited for; matrix products, arithmetic and copies ran while one was open for 11% of the time, Pallas kernels for 0%

profile of v1, /device:TPU:2, one launch (start us, length us, event | category | flops | bytes accessed | tf_op | source)
XLA Modules:
  0.0 86.4 jit_solution(3636686450821019693)
XLA Ops:
  0.0 1.3 %fusion.33 = (s32[1]{0:T(128)}, s32[1]{0:T(128)}) fusion(s32[2]{0:T(128)} %si_ref.3), kind=kLoop, calls=%fused_computation.60 | loop fusion | bytes 16 | tf_op jit(solution)/shard_map/slice | solution.py:162
  3.7 0.7 bitcast_convert_fusion
  4.5 0.7 fusion.32
  6.4 2.8 %constant_dynamic-slice_fusion = (f32[1,10,64,256]{3,2,1,0:T(8,128)S(1)}, f32[1,10,64,256]{3,2,1,0:T(8,128)S(1)}, f32[1,10,64,256]{3,2,1,0:T(8,128)}, f32[1,10,64,256]{3,2,1,0:T(8,128)S(1)}) fusion(f32[4,10,64,256]{3,2,1,0:T(8,128)} %v_ref.3, s32[]{:T(128)S(6)} %select_n.10, s32[]{:T(128)S(6)} %select_n.9, f32[4,10,64,256]{3,2,1,0:T(8,128)} %u_ref.3), kind=kLoop, calls=%fused_computation.50 | loop fusion | bytes 5242888 | tf_op jit(solution)/shard_map/jit(dynamic_index_in_dim)/dynamic_slice | solution.py:165
  10.7 0.7 rev.6
  12.1 12.6 %collective-permute-start.4 = (f32[10,256]{1,0:T(8,128)}, f32[10,256]{1,0:T(8,128)}, u32[]{:S(2)}, u32[]{:S(2)}) collective-permute-start(f32[10,256]{1,0:T(8,128)} %get-tuple-element.11), channel_id=1, source_target_pairs={{0,1},{1,2},{2,3},{4,5},{5,6},{6,7},{8,9},{9,10},{10,11},{12,13},{... | collective-permute-start | bytes 30728 | tf_op jit(solution)/shard_map/ppermute | solution.py:177
  24.7 1.9 %collective-permute-start.2 = (f32[10,256]{1,0:T(8,128)}, f32[10,256]{1,0:T(8,128)}, u32[]{:S(2)}, u32[]{:S(2)}) collective-permute-start(f32[10,256]{1,0:T(8,128)} %get-tuple-element.15), channel_id=1, source_target_pairs={{1,0},{2,1},{3,2},{5,4},{6,5},{7,6},{9,8},{10,9},{11,10},{13,12},{... | collective-permute-start | bytes 30728 | tf_op jit(solution)/shard_map/ppermute | solution.py:176
  26.7 0.8 slice_reduce_fusion
  27.4 1.0 %fusion.29 = (f32[10,64,1]{2,0,1:T(8,128)}, f32[10,64,1]{2,0,1:T(8,128)S(1)}) fusion(f32[10,64,256]{2,0,1:T(8,128)S(1)} %copy_multiply_fusion), kind=kLoop, calls=%fused_computation.56 | loop fusion | bytes 10240 | tf_op jit(solution)/shard_map/slice | solution.py:166
  28.4 1.3 %copy.42 = f32[10,64,1]{1,0,2:T(8,128)S(1)} copy(f32[10,64,1]{2,0,1:T(8,128)} %get-tuple-element.21) | data formatting | bytes 5120 | tf_op jit(solution)/shard_map/slice | solution.py:166
  30.0 2.5 %copy.41 = f32[1,10,64,256]{2,1,3,0:T(8,128)} copy(f32[1,10,64,256]{3,2,1,0:T(8,128)S(1)} %copy-done.1) | data formatting | bytes 1310720 | tf_op jit(solution)/shard_map/jit(dynamic_index_in_dim)/dynamic_slice | solution.py:164
  32.5 0.7 fusion.25
  33.4 7.6 %collective-permute-start = (f32[10,64]{1,0:T(8,128)S(1)}, f32[10,64]{1,0:T(8,128)S(1)}, u32[]{:S(2)}, u32[]{:S(2)}) collective-permute-start(f32[10,64]{1,0:T(8,128)S(1)} %get-tuple-element.17), channel_id=1, source_target_pairs={{0,252},{4,0},{8,4},{12,8},{16,12},{20,16},{24,20},{28,24},{32,28}... | collective-permute-start | bytes 7688 | tf_op jit(solution)/shard_map/ppermute | solution.py:174
  41.0 1.4 %copy.77 = f32[1,10,64,256]{3,1,2,0:T(8,128)} copy(f32[1,10,64,256]{3,2,1,0:T(8,128)S(1)} %get-tuple-element.7) | data formatting | bytes 1310720 | tf_op jit(solution)/shard_map/jit(dynamic_index_in_dim)/dynamic_slice | solution.py:165
  42.4 1.3 %copy.45 = f32[1,10,64,256]{2,1,3,0:T(8,128)S(1)} copy(f32[1,10,64,256]{3,2,1,0:T(8,128)S(1)} %get-tuple-element.32) | data formatting | bytes 1310720 | tf_op jit(solution)/shard_map/jit(dynamic_index_in_dim)/dynamic_slice | solution.py:164
  44.3 8.1 %shard_map.82.adj_ref = f32[10,64,256]{2,1,0:T(8,128)} custom-call(s32[2]{0:T(128)} %si_ref.3, s32[2]{0:T(128)} %bitcast.153, s32[1]{0:T(128)} %bitcast.1.flag_ref, f32[10,10]{1,0:T(8,128)} %lm_ref.3, f32[10,64,256]{2,1,0:T(8,128)} %adj_ref.1, f32[64,256]{1,0:T(8,128)} %d_ref.3, f32[4,10,64,256]{3,2,1,0:T(8,128)} %t_ref.3, f32[4,10,64,256]{3,2,1,0:T(8,128)} %u_ref.3, ...), custom_call_target="tpu_custom_call" | custom-call | flops 9830400 | bytes 3932160 | tf_op jit(solution)/shard_map/pallas_call | solution.py:108
  52.4 0.9 %fusion.30 = (f32[10,1,256]{2,1,0:T(1,128)S(1)}, f32[10,1,256]{2,1,0:T(1,128)S(1)}) fusion(f32[10,64,256]{2,1,0:T(8,128)} %shard_map.82.adj_ref), kind=kLoop, calls=%fused_computation.57 | loop fusion | bytes 40960 | tf_op jit(solution)/shard_map/slice | solution.py:167
  53.4 1.2 %fusion.31 = (f32[10,64,1]{2,1,0:T(8,128)S(1)}, f32[10,64,1]{2,1,0:T(8,128)S(1)}) fusion(f32[10,64,256]{2,1,0:T(8,128)} %shard_map.82.adj_ref), kind=kLoop, calls=%fused_computation.58 | loop fusion | bytes 10240 | tf_op jit(solution)/shard_map/slice | solution.py:166
  54.6 0.7 fusion.11
  56.2 9.2 %collective-permute-start.9 = (f32[10,256]{1,0:T(8,128)S(1)}, f32[10,256]{1,0:T(8,128)S(1)}, u32[]{:S(2)}, u32[]{:S(2)}) collective-permute-start(f32[10,256]{1,0:T(8,128)S(1)} %get-tuple-element.18), channel_id=1, source_target_pairs={{0,1},{1,2},{2,3},{4,5},{5,6},{6,7},{8,9},{9,10},{10,11},{12,13},{... | collective-permute-start | bytes 30728 | tf_op jit(solution)/shard_map/ppermute | solution.py:177
  65.4 1.9 %collective-permute-start.7 = (f32[10,256]{1,0:T(8,128)S(1)}, f32[10,256]{1,0:T(8,128)S(1)}, u32[]{:S(2)}, u32[]{:S(2)}) collective-permute-start(f32[10,256]{1,0:T(8,128)S(1)} %get-tuple-element.20), channel_id=1, source_target_pairs={{1,0},{2,1},{3,2},{5,4},{6,5},{7,6},{9,8},{10,9},{11,10},{13,12},{... | collective-permute-start | bytes 30728 | tf_op jit(solution)/shard_map/ppermute | solution.py:176
  67.8 7.7 %collective-permute-start.5 = (f32[10,64]{1,0:T(8,128)S(1)}, f32[10,64]{1,0:T(8,128)S(1)}, u32[]{:S(2)}, u32[]{:S(2)}) collective-permute-start(f32[10,64]{1,0:T(8,128)S(1)} %get-tuple-element.14), channel_id=1, source_target_pairs={{0,252},{4,0},{8,4},{12,8},{16,12},{20,16},{24,20},{28,24},{32,28}... | collective-permute-start | bytes 7688 | tf_op jit(solution)/shard_map/ppermute | solution.py:174
  75.6 1.6 %collective-permute-done.6.hw_ref = f32[10,64]{1,0:T(8,128)S(1)} collective-permute-done((f32[10,64]{1,0:T(8,128)S(1)}, f32[10,64]{1,0:T(8,128)S(1)}, u32[]{:S(2)}, u32[]{:S(2)}) %collective-permute-start.6) | collective-permute-done | bytes 2592 | tf_op jit(solution)/shard_map/ppermute | solution.py:175
  78.4 7.9 %shard_map.83 = f32[10,64,256]{2,1,0:T(8,128)} custom-call(s32[2]{0:T(128)} %si_ref.3, s32[2]{0:T(128)} %bitcast.154, s32[1]{0:T(128)} %bitcast.1.flag_ref, f32[10,10]{1,0:T(8,128)} %lm_ref.3, f32[10,64,256]{2,1,0:T(8,128)} %shard_map.82.adj_ref, f32[64,256]{1,0:T(8,128)} %d_ref.3, f32[4,10,64,256]{3,2,1,0:T(8,128)} %t_ref.3, f32[4,10,64,256]{3,2,1,0:T(8,128)} %u_ref.3, ...), custom_call_target="tpu_custom_call" | custom-call | flops 9830400 | bytes 3932160 | tf_op jit(solution)/shard_map/pallas_call | solution.py:108
  (56 shorter events, 5.7 us)
Async XLA Ops:
  5.2 4.9 %copy-start.7 = (f32[1,256]{1,0:T(1,128)}, f32[1,256]{1,0:T(1,128)S(1)}, u32[]{:S(2)}) copy-start(f32[1,256]{1,0:T(1,128)S(1)} %get-tuple-element.27) | copy-start | bytes 3076
  5.2 4.9 %copy-start.9 = (f32[1,256]{1,0:T(1,128)}, f32[1,256]{1,0:T(1,128)S(1)}, u32[]{:S(2)}) copy-start(f32[1,256]{1,0:T(1,128)S(1)} %get-tuple-element.28) | copy-start | bytes 3076
  6.4 3.3 %copy-start = (f32[10,64,256]{2,1,0:T(8,128)S(1)}, f32[10,64,256]{2,1,0:T(8,128)}, u32[]{:S(2)}) copy-start(f32[10,64,256]{2,1,0:T(8,128)} %adj_ref.1) | copy-start | bytes 1966084
  9.3 17.4 %copy-start.2 = (f32[64,256]{1,0:T(8,128)S(1)}, f32[64,256]{1,0:T(8,128)}, u32[]{:S(2)}) copy-start(f32[64,256]{1,0:T(8,128)} %d_ref.3) | copy-start | bytes 196612
  10.1 19.9 %copy-start.1 = (f32[1,10,64,256]{3,2,1,0:T(8,128)S(1)}, f32[1,10,64,256]{3,2,1,0:T(8,128)}, u32[]{:S(2)}) copy-start(f32[1,10,64,256]{3,2,1,0:T(8,128)} %get-tuple-element.31) | copy-start | bytes 1966084
  11.5 32.2 %collective-permute-start.3 = (f32[10,256]{1,0:T(8,128)}, f32[10,256]{1,0:T(8,128)S(1)}, u32[]{:S(2)}, u32[]{:S(2)}) collective-permute-start(f32[10,256]{1,0:T(8,128)} %rev.6), channel_id=1, source_target_pairs={{3,255},{7,251},{11,247},{15,243},{19,239},{23,235},{27,231},{31,2... | collective-permute-start | bytes 30728 | tf_op jit(solution)/shard_map/ppermute | solution.py:178
  12.1 31.6 %collective-permute-start.4 = (f32[10,256]{1,0:T(8,128)}, f32[10,256]{1,0:T(8,128)}, u32[]{:S(2)}, u32[]{:S(2)}) collective-permute-start(f32[10,256]{1,0:T(8,128)} %get-tuple-element.11), channel_id=1, source_target_pairs={{0,1},{1,2},{2,3},{4,5},{5,6},{6,7},{8,9},{9,10},{10,11},{12,13},{... | collective-permute-start | bytes 30728 | tf_op jit(solution)/shard_map/ppermute | solution.py:177
  24.7 19.0 %collective-permute-start.2 = (f32[10,256]{1,0:T(8,128)}, f32[10,256]{1,0:T(8,128)}, u32[]{:S(2)}, u32[]{:S(2)}) collective-permute-start(f32[10,256]{1,0:T(8,128)} %get-tuple-element.15), channel_id=1, source_target_pairs={{1,0},{2,1},{3,2},{5,4},{6,5},{7,6},{9,8},{10,9},{11,10},{13,12},{... | collective-permute-start | bytes 30728 | tf_op jit(solution)/shard_map/ppermute | solution.py:176
  28.4 4.1 %copy-start.15 = (f32[64]{0:T(128)S(1)}, f32[64]{0:T(128)}, u32[]{:S(2)}) copy-start(f32[64]{0:T(128)} %get-tuple-element.5) | copy-start | bytes 772
  28.4 4.1 %copy-start.16 = (f32[64]{0:T(128)S(1)}, f32[64]{0:T(128)}, u32[]{:S(2)}) copy-start(f32[64]{0:T(128)} %get-tuple-element.6) | copy-start | bytes 772
  33.2 10.4 %collective-permute-start.1 = (f32[10,64]{1,0:T(8,128)S(1)}, f32[10,64]{1,0:T(8,128)S(1)}, u32[]{:S(2)}, u32[]{:S(2)}) collective-permute-start(f32[10,64]{1,0:T(8,128)S(1)} %get-tuple-element.16), channel_id=1, source_target_pairs={{0,4},{4,8},{8,12},{12,16},{16,20},{20,24},{24,28},{28,32},{32,36}... | collective-permute-start | bytes 7688 | tf_op jit(solution)/shard_map/ppermute | solution.py:175
  33.4 10.3 %collective-permute-start = (f32[10,64]{1,0:T(8,128)S(1)}, f32[10,64]{1,0:T(8,128)S(1)}, u32[]{:S(2)}, u32[]{:S(2)}) collective-permute-start(f32[10,64]{1,0:T(8,128)S(1)} %get-tuple-element.17), channel_id=1, source_target_pairs={{0,252},{4,0},{8,4},{12,8},{16,12},{20,16},{24,20},{28,24},{32,28}... | collective-permute-start | bytes 7688 | tf_op jit(solution)/shard_map/ppermute | solution.py:174
  43.7 0.6 copy-start.12
  43.7 0.6 copy-start.3
  44.3 10.3 %copy-start.8 = (f32[1,256]{1,0:T(1,128)S(1)}, f32[1,256]{1,0:T(1,128)}, u32[]{:S(2)}) copy-start(f32[1,256]{1,0:T(1,128)} %copy-done.7) | copy-start | bytes 3076
  44.3 10.3 %copy-start.10 = (f32[1,256]{1,0:T(1,128)S(1)}, f32[1,256]{1,0:T(1,128)}, u32[]{:S(2)}) copy-start(f32[1,256]{1,0:T(1,128)} %copy-done.9) | copy-start | bytes 3076
  55.5 21.7 %collective-permute-start.8 = (f32[10,256]{1,0:T(8,128)S(1)}, f32[10,256]{1,0:T(8,128)S(1)}, u32[]{:S(2)}, u32[]{:S(2)}) collective-permute-start(f32[10,256]{1,0:T(8,128)S(1)} %rev.7), channel_id=1, source_target_pairs={{3,255},{7,251},{11,247},{15,243},{19,239},{23,235},{27,231},{31,2... | collective-permute-start | bytes 30728 | tf_op jit(solution)/shard_map/ppermute | solution.py:178
  56.2 21.0 %collective-permute-start.9 = (f32[10,256]{1,0:T(8,128)S(1)}, f32[10,256]{1,0:T(8,128)S(1)}, u32[]{:S(2)}, u32[]{:S(2)}) collective-permute-start(f32[10,256]{1,0:T(8,128)S(1)} %get-tuple-element.18), channel_id=1, source_target_pairs={{0,1},{1,2},{2,3},{4,5},{5,6},{6,7},{8,9},{9,10},{10,11},{12,13},{... | collective-permute-start | bytes 30728 | tf_op jit(solution)/shard_map/ppermute | solution.py:177
  65.4 11.9 %collective-permute-start.7 = (f32[10,256]{1,0:T(8,128)S(1)}, f32[10,256]{1,0:T(8,128)S(1)}, u32[]{:S(2)}, u32[]{:S(2)}) collective-permute-start(f32[10,256]{1,0:T(8,128)S(1)} %get-tuple-element.20), channel_id=1, source_target_pairs={{1,0},{2,1},{3,2},{5,4},{6,5},{7,6},{9,8},{10,9},{11,10},{13,12},{... | collective-permute-start | bytes 30728 | tf_op jit(solution)/shard_map/ppermute | solution.py:176
  67.7 9.5 %collective-permute-start.6 = (f32[10,64]{1,0:T(8,128)S(1)}, f32[10,64]{1,0:T(8,128)S(1)}, u32[]{:S(2)}, u32[]{:S(2)}) collective-permute-start(f32[10,64]{1,0:T(8,128)S(1)} %get-tuple-element.13), channel_id=1, source_target_pairs={{0,4},{4,8},{8,12},{12,16},{16,20},{20,24},{24,28},{28,32},{32,36}... | collective-permute-start | bytes 7688 | tf_op jit(solution)/shard_map/ppermute | solution.py:175
  67.8 9.4 %collective-permute-start.5 = (f32[10,64]{1,0:T(8,128)S(1)}, f32[10,64]{1,0:T(8,128)S(1)}, u32[]{:S(2)}, u32[]{:S(2)}) collective-permute-start(f32[10,64]{1,0:T(8,128)S(1)} %get-tuple-element.14), channel_id=1, source_target_pairs={{0,252},{4,0},{8,4},{12,8},{16,12},{20,16},{24,20},{28,24},{32,28}... | collective-permute-start | bytes 7688 | tf_op jit(solution)/shard_map/ppermute | solution.py:174
  77.2 0.6 copy-start.4
  77.2 0.6 copy-start.5
  77.8 0.6 copy-start.6
  (3 other events, 1.8 us)

commit v2 on v0

v2 whole, which is shorter than its diff:
```python
import functools

import jax
import jax.numpy as jnp
from jax import lax
from jax.experimental import pallas as pl
from jax.experimental.pallas import tpu as pltpu
from jax.sharding import PartitionSpec as P

TLON = 128
STEPS = 2


advect_scale = 0.25
damping = 0.3


def shift_pairs(count, delta, periodic):
    pairs = []
    for i in range(count):
        j = i + delta
        if periodic:
            pairs.append((i, j % count))
        elif 0 <= j < count:
            pairs.append((i, j))
    return pairs


def wet_field(wt_ref, rows, width):
    lane = lax.broadcasted_iota(jnp.int32, (rows, width), 1)
    wet_i = jnp.zeros((rows, width), jnp.int32)
    for t in range(width // TLON):
        inside = (lane >= t * TLON) & (lane < (t + 1) * TLON)
        wet_i = jnp.where(inside, wt_ref[t], wet_i)
    return wet_i.astype(jnp.float32)


class Payload:
    def __init__(self, levels, rows, width):
        self.levels = levels
        self.rows = rows
        self.width = width
        self.lane = lax.broadcasted_iota(jnp.int32, (rows, TLON), 1)
        self.east = jnp.zeros((rows, TLON), jnp.float32)
        self.west = jnp.zeros((rows, TLON), jnp.float32)

    def add(self, l, a, d, u, v, pn_ref, ps_ref, pf_ref):
        rows, width = self.rows, self.width
        a_w, a_e = a[:, 0:1], a[:, width - 1:width]
        east = d[:, 0:1] * a_w + advect_scale * (u[:, 0:1] * a_w)
        west = d[:, width - 1:width] * a_e - advect_scale * (u[:, width - 1:width] * a_e)
        self.east = jnp.where(self.lane == l, jnp.broadcast_to(east, (rows, TLON)), self.east)
        self.west = jnp.where(self.lane == l, jnp.broadcast_to(west, (rows, TLON)), self.west)
        a_s, a_n = a[0:1, :], a[rows - 1:rows, :]
        pn_ref[l:l + 1, :] = d[0:1, :] * a_s + advect_scale * (v[0:1, :] * a_s)
        s_n = d[rows - 1:rows, :] * a_n
        m_n = v[rows - 1:rows, :] * a_n
        ps_ref[l:l + 1, :] = s_n - advect_scale * m_n
        pf_ref[l:l + 1, :] = s_n + advect_scale * m_n

    def finish(self, pe_ref, pw_ref):
        pe_ref[...] = self.east[:, : self.levels]
        pw_ref[...] = self.west[:, : self.levels]


def prologue_kernel(si_ref, wt_ref, af_ref, d_ref, u_ref, v_ref, pe_ref, pw_ref, pn_ref, ps_ref, pf_ref):
    del si_ref
    levels, rows, width = af_ref.shape
    wet = wet_field(wt_ref, rows, width)
    d = d_ref[...]
    out = Payload(levels, rows, width)
    for l in range(levels):
        out.add(l, af_ref[l] * wet, d, u_ref[l], v_ref[l], pn_ref, ps_ref, pf_ref)
    out.finish(pe_ref, pw_ref)


def step_kernel(first, emit, si_ref, wt_ref, flag_ref, lm_ref, adj_ref, d_ref, t_ref, u_ref, v_ref,
                he_ref, hw_ref, hn_ref, hf_ref, hs_ref, *rest):
    del si_ref
    if emit:
        u2_ref, v2_ref, out_ref, pe_ref, pw_ref, pn_ref, ps_ref, pf_ref, a_ref = rest
    else:
        out_ref, a_ref = rest
    levels, rows, width = adj_ref.shape
    lane = lax.broadcasted_iota(jnp.int32, (rows, width), 1)
    row = lax.broadcasted_iota(jnp.int32, (rows, width), 0)
    wet = wet_field(wt_ref, rows, width)
    if first:
        for m in range(levels):
            a_ref[m] = adj_ref[m] * wet
        src = a_ref
    else:
        src = adj_ref
    d = d_ref[...]
    he = he_ref[...]
    hw = hw_ref[...]
    top = flag_ref[0] == 1
    payload = Payload(levels, rows, width) if emit else None

    for l in range(levels):
        a = src[l]
        vertical = lm_ref[0, l] * src[0]
        for m in range(1, levels):
            vertical = vertical + lm_ref[m, l] * src[m]
        s = d * a
        zf = u_ref[l] * a
        mf = v_ref[l] * a
        east_src = s + advect_scale * zf
        west_src = s - advect_scale * zf
        north_src = s + advect_scale * mf
        south_src = s - advect_scale * mf

        east_col = jnp.broadcast_to(he[:, l:l + 1], (rows, width))
        west_col = jnp.broadcast_to(hw[:, l:l + 1], (rows, width))
        north_row = jnp.where(top, hf_ref[l:l + 1, :], hn_ref[l:l + 1, :])
        south_row = hs_ref[l:l + 1, :]

        east = jnp.where(lane == width - 1, east_col, pltpu.roll(east_src, width - 1, 1))
        west = jnp.where(lane == 0, west_col, pltpu.roll(west_src, 1, 1))
        north = jnp.where(row == rows - 1, north_row, pltpu.roll(north_src, rows - 1, 0))
        south = jnp.where(row == 0, south_row, pltpu.roll(south_src, 1, 0))

        t = t_ref[l]
        new = wet * (a - 4.0 * s + east + west + north + south + vertical - damping * t * t * a)
        out_ref[l] = new
        if emit:
            payload.add(l, new, d, u2_ref[l], v2_ref[l], pn_ref, ps_ref, pf_ref)
    if emit:
        payload.finish(pe_ref, pw_ref)


def payload_shapes(levels, rows, width):
    lon = jax.ShapeDtypeStruct((rows, levels), jnp.float32)
    lat = jax.ShapeDtypeStruct((levels, width), jnp.float32)
    return [lon, lon, lat, lat, lat]


def whole(shape):
    return pl.BlockSpec(shape, lambda i, *_: (0,) * len(shape))


def state_spec(k, levels, rows, width):
    return pl.BlockSpec((None, levels, rows, width), lambda i, si, *_: (si[k], 0, 0, 0))


def run_prologue(k, si, wt, af, d, zonal, merid):
    levels, rows, width = af.shape
    shapes = payload_shapes(levels, rows, width)
    n = levels * rows * width
    return pl.pallas_call(
        prologue_kernel,
        out_shape=shapes,
        grid_spec=pltpu.PrefetchScalarGridSpec(
            num_scalar_prefetch=2,
            grid=(1,),
            in_specs=[whole(af.shape), whole(d.shape), state_spec(k, levels, rows, width),
                      state_spec(k, levels, rows, width)],
            out_specs=[whole(s.shape) for s in shapes],
        ),
        cost_estimate=pl.CostEstimate(flops=2 * n, bytes_accessed=12 * n, transcendentals=0),
    )(si, wt, af, d, zonal, merid)


def run_step(k, k_next, si, wt, flags, lm, adj, d, tracer, zonal, merid, he, hw, hn, hf, hs):
    levels, rows, width = adj.shape
    first = k_next is not None
    emit = k_next is not None
    state = state_spec(k, levels, rows, width)
    in_specs = [
        pl.BlockSpec(memory_space=pltpu.SMEM),
        whole(adj.shape), whole(d.shape), state, state, state,
        whole(he.shape), whole(hw.shape), whole(hn.shape), whole(hf.shape), whole(hs.shape),
    ]
    args = [si, wt, flags, lm, adj, d, tracer, zonal, merid, he, hw, hn, hf, hs]
    out_shape = [jax.ShapeDtypeStruct(adj.shape, jnp.float32)]
    if emit:
        nxt = state_spec(k_next, levels, rows, width)
        in_specs += [nxt, nxt]
        args += [zonal, merid]
        out_shape += payload_shapes(levels, rows, width)
    n = levels * rows * width
    outs = pl.pallas_call(
        functools.partial(step_kernel, first, emit),
        out_shape=out_shape,
        grid_spec=pltpu.PrefetchScalarGridSpec(
            num_scalar_prefetch=3,
            grid=(1,),
            in_specs=in_specs,
            out_specs=[whole(s.shape) for s in out_shape],
            scratch_shapes=[pltpu.VMEM((levels, rows, width), jnp.float32)],
        ),
        cost_estimate=pl.CostEstimate(flops=60 * n, bytes_accessed=32 * n, transcendentals=0),
    )(*args)
    return outs[0], outs[1:]


def shards(
    adjoint_final,
    stored_tracer,
    stored_zonal,
    stored_meridional,
    diffusivity,
    level_mixing,
    wet_tiles,
    state_index,
):
    n_lat = lax.axis_size("lat")
    n_lon = lax.axis_size("lon")
    wt = wet_tiles.reshape(-1)
    is_top = lax.axis_index("lat") == n_lat - 1
    flags = is_top.astype(jnp.int32).reshape(1)

    to_west = shift_pairs(n_lon, -1, True)
    to_east = shift_pairs(n_lon, 1, True)
    to_south = shift_pairs(n_lat, -1, False)
    to_north = shift_pairs(n_lat, 1, False)
    top = n_lat - 1
    fold = [(j * n_lat + top, (n_lon - 1 - j) * n_lat + top) for j in range(n_lon)]

    def exchange(payloads):
        pe, pw, pn, ps, pf = payloads
        he = lax.ppermute(pe, "lon", to_west)
        hw = lax.ppermute(pw, "lon", to_east)
        hn = lax.ppermute(pn, "lat", to_south)
        hs = lax.ppermute(ps, "lat", to_north)
        hf = lax.ppermute(pf[:, ::-1], ("lon", "lat"), fold)
        return he, hw, hn, hf, hs

    payloads = run_prologue(STEPS - 1, state_index, wt, adjoint_final, diffusivity,
                            stored_zonal, stored_meridional)
    adj = adjoint_final
    for back in range(STEPS):
        k = STEPS - 1 - back
        k_next = k - 1 if k > 0 else None
        halos = exchange(payloads)
        adj, payloads = run_step(
            k, k_next, state_index, wt, flags, level_mixing, adj, diffusivity,
            stored_tracer, stored_zonal, stored_meridional, *halos,
        )
    return adj


def solution(mesh):
    return jax.shard_map(
        shards,
        mesh=mesh,
        in_specs=(
            P(None, "lat", "lon"),
            P(None, None, "lat", "lon"),
            P(None, None, "lat", "lon"),
            P(None, None, "lat", "lon"),
            P("lat", "lon"),
            P(),
            P("lat", "lon"),
            P(),
        ),
        out_specs=P(None, "lat", "lon"),
        check_vma=False,
    )
```

time: 112 us -> 61.5 us (0.55)
  the two profiles are of different devices: /device:TPU:1 before, /device:TPU:2 now
where the time goes in v2:
time: 61.5 us; the launch traced here: 61.1 us
  starting transfers between devices  27.3 us (44%)
  waiting for transfers between devices  18 us (29%)
  Pallas kernels  12.8 us (21%)
  local copies, waits for them, and re-layouts  2.88 us (5%)
    ppermute x2, waiting for transfers between devices, exchange(): hw = lax.ppermute(pw, 'lon', to_east)  14 us
    ppermute x2, starting transfers between devices, exchange(): hs = lax.ppermute(ps, 'lat', to_north)  13.9 us
    pallas_call x2, Pallas kernels, run_step(): pl.pallas_call(functools.partial(step_kernel, first, emit), out_shape=out...  9.76 us
    ppermute x2, starting transfers between devices, exchange(): he = lax.ppermute(pe, 'lon', to_west)  5.42 us
    ppermute x2, starting transfers between devices, exchange(): hn = lax.ppermute(pn, 'lat', to_south)  4.98 us
    ppermute x2, waiting for transfers between devices, exchange(): he = lax.ppermute(pe, 'lon', to_west)  4.01 us
    pallas_call x1, Pallas kernels, run_prologue(): pl.pallas_call(prologue_kernel, out_shape=shapes, grid_spec=pltpu.Prefetc...  3.09 us
    ppermute x2, starting transfers between devices, exchange(): hw = lax.ppermute(pw, 'lon', to_east)  1.71 us
  transfers between devices with their start and end apart: 10, of which 4 were waited for; matrix products, arithmetic and copies ran while one was open for 0% of the time, Pallas kernels for 0%

profile of v2, /device:TPU:2, one launch (start us, length us, event | category | flops | bytes accessed | tf_op | source)
XLA Modules:
  0.0 61.1 jit_solution(12021465847394445827)
XLA Ops:
  0.0 3.1 %shard_map.82 = (f32[64,10]{1,0:T(8,128)}, f32[64,10]{1,0:T(8,128)}, f32[10,256]{1,0:T(8,128)}, f32[10,256]{1,0:T(8,128)}, f32[10,256]{1,0:T(8,128)}) custom-call(s32[2]{0:T(128)} %si_ref.5, s32[2]{0:T(128)} %bitcast.2, f32[10,64,256]{2,1,0:T(8,128)} %adj_ref.1, f32[64,256]{1,0:T(8,128)} %d_ref.5, f32[4,10,64,256]{3,2,1,0:T(8,128)} %u_ref.5, ...), custom_call_target="tpu_custom_call" | custom-call | flops 327680 | bytes 1966080 | tf_op jit(solution)/shard_map/pallas_call | solution.py:150
  3.1 0.8 %rev.6 = f32[10,256]{1,0:T(8,128)S(1)} reverse(f32[10,256]{1,0:T(8,128)} %get-tuple-element.19), dimensions={1} | reverse | bytes 20480 | tf_op jit(solution)/shard_map/rev | solution.py:226
  3.9 0.7 %collective-permute-start.3 = (f32[10,256]{1,0:T(8,128)S(1)}, f32[10,256]{1,0:T(8,128)S(1)}, u32[]{:S(2)}, u32[]{:S(2)}) collective-permute-start(f32[10,256]{1,0:T(8,128)S(1)} %rev.6), channel_id=1, source_target_pairs={{3,255},{7,251},{11,247},{15,243},{19,239},{23,235},{27,231},{31,2... | collective-permute-start | bytes 30728 | tf_op jit(solution)/shard_map/ppermute | solution.py:226
  4.6 1.9 %collective-permute-start.2 = (f32[10,256]{1,0:T(8,128)}, f32[10,256]{1,0:T(8,128)S(1)}, u32[]{:S(2)}, u32[]{:S(2)}) collective-permute-start(f32[10,256]{1,0:T(8,128)} %get-tuple-element.18), channel_id=1, source_target_pairs={{1,0},{2,1},{3,2},{5,4},{6,5},{7,6},{9,8},{10,9},{11,10},{13,12},{... | collective-permute-start | bytes 30728 | tf_op jit(solution)/shard_map/ppermute | solution.py:224
  6.5 11.9 %collective-permute-start.4 = (f32[10,256]{1,0:T(8,128)}, f32[10,256]{1,0:T(8,128)S(1)}, u32[]{:S(2)}, u32[]{:S(2)}) collective-permute-start(f32[10,256]{1,0:T(8,128)} %get-tuple-element.20), channel_id=1, source_target_pairs={{0,1},{1,2},{2,3},{4,5},{5,6},{6,7},{8,9},{9,10},{10,11},{12,13},{... | collective-permute-start | bytes 30728 | tf_op jit(solution)/shard_map/ppermute | solution.py:225
  18.5 0.4 collective-permute-start
  18.9 1.7 %collective-permute-start.1 = (f32[64,10]{1,0:T(8,128)}, f32[64,10]{1,0:T(8,128)S(1)}, u32[]{:S(2)}, u32[]{:S(2)}) collective-permute-start(f32[64,10]{1,0:T(8,128)} %get-tuple-element.17), channel_id=1, source_target_pairs={{0,4},{4,8},{8,12},{12,16},{16,20},{20,24},{24,28},{28,32},{32,36}... | collective-permute-start | bytes 7688 | tf_op jit(solution)/shard_map/ppermute | solution.py:223
  20.6 2.1 %collective-permute-done.he_ref = f32[64,10]{1,0:T(8,128)S(1)} collective-permute-done((f32[64,10]{1,0:T(8,128)}, f32[64,10]{1,0:T(8,128)S(1)}, u32[]{:S(2)}, u32[]{:S(2)}) %collective-permute-start) | collective-permute-done | bytes 2592 | tf_op jit(solution)/shard_map/ppermute | solution.py:222
  22.7 6.0 %collective-permute-done.1.hw_ref = f32[64,10]{1,0:T(8,128)S(1)} collective-permute-done((f32[64,10]{1,0:T(8,128)}, f32[64,10]{1,0:T(8,128)S(1)}, u32[]{:S(2)}, u32[]{:S(2)}) %collective-permute-start.1) | collective-permute-done | bytes 2592 | tf_op jit(solution)/shard_map/ppermute | solution.py:223
  28.8 0.6 copy-done.1
  29.3 0.0 copy-done.4
  29.3 0.0 copy-done.6
  29.4 5.4 %shard_map.83 = (f32[10,64,256]{2,1,0:T(8,128)}, f32[64,10]{1,0:T(8,128)}, f32[64,10]{1,0:T(8,128)}, f32[10,256]{1,0:T(8,128)}, f32[10,256]{1,0:T(8,128)}, /*index=5*/f32[10,256]{1,0:T(8,128)}) custom-call(s32[2]{0:T(128)} %si_ref.5, s32[2]{0:T(128)} %bitcast.3, s32[1]{0:T(128)} %bitcast.1.flag_ref, f32[10,10]{1,0:T(8,128)} %lm_ref.3, ...), custom_call_target="tpu_custom_call" | custom-call | flops 9830400 | bytes 5242880 | tf_op jit(solution)/shard_map/pallas_call | solution.py:182
  34.7 0.8 %rev.7 = f32[10,256]{1,0:T(8,128)S(1)} reverse(f32[10,256]{1,0:T(8,128)} %get-tuple-element.25), dimensions={1} | reverse | bytes 20480 | tf_op jit(solution)/shard_map/rev | solution.py:226
  35.6 0.7 %collective-permute-start.8 = (f32[10,256]{1,0:T(8,128)S(1)}, f32[10,256]{1,0:T(8,128)S(1)}, u32[]{:S(2)}, u32[]{:S(2)}) collective-permute-start(f32[10,256]{1,0:T(8,128)S(1)} %rev.7), channel_id=1, source_target_pairs={{3,255},{7,251},{11,247},{15,243},{19,239},{23,235},{27,231},{31,2... | collective-permute-start | bytes 30728 | tf_op jit(solution)/shard_map/ppermute | solution.py:226
  36.2 3.1 %collective-permute-start.7 = (f32[10,256]{1,0:T(8,128)}, f32[10,256]{1,0:T(8,128)S(1)}, u32[]{:S(2)}, u32[]{:S(2)}) collective-permute-start(f32[10,256]{1,0:T(8,128)} %get-tuple-element.24), channel_id=1, source_target_pairs={{1,0},{2,1},{3,2},{5,4},{6,5},{7,6},{9,8},{10,9},{11,10},{13,12},{... | collective-permute-start | bytes 30728 | tf_op jit(solution)/shard_map/ppermute | solution.py:224
  39.3 1.9 %collective-permute-start.9 = (f32[10,256]{1,0:T(8,128)}, f32[10,256]{1,0:T(8,128)S(1)}, u32[]{:S(2)}, u32[]{:S(2)}) collective-permute-start(f32[10,256]{1,0:T(8,128)} %get-tuple-element.26), channel_id=1, source_target_pairs={{0,1},{1,2},{2,3},{4,5},{5,6},{6,7},{8,9},{9,10},{10,11},{12,13},{... | collective-permute-start | bytes 30728 | tf_op jit(solution)/shard_map/ppermute | solution.py:225
  41.2 5.0 %collective-permute-start.5 = (f32[64,10]{1,0:T(8,128)}, f32[64,10]{1,0:T(8,128)S(1)}, u32[]{:S(2)}, u32[]{:S(2)}) collective-permute-start(f32[64,10]{1,0:T(8,128)} %get-tuple-element.22), channel_id=1, source_target_pairs={{0,252},{4,0},{8,4},{12,8},{16,12},{20,16},{24,20},{28,24},{32,28}... | collective-permute-start | bytes 7688 | tf_op jit(solution)/shard_map/ppermute | solution.py:222
  46.2 1.9 %collective-permute-done.5.he_ref = f32[64,10]{1,0:T(8,128)S(1)} collective-permute-done((f32[64,10]{1,0:T(8,128)}, f32[64,10]{1,0:T(8,128)S(1)}, u32[]{:S(2)}, u32[]{:S(2)}) %collective-permute-start.5) | collective-permute-done | bytes 2592 | tf_op jit(solution)/shard_map/ppermute | solution.py:222
  48.1 7.9 %collective-permute-done.6.hw_ref = f32[64,10]{1,0:T(8,128)S(1)} collective-permute-done((f32[64,10]{1,0:T(8,128)}, f32[64,10]{1,0:T(8,128)S(1)}, u32[]{:S(2)}, u32[]{:S(2)}) %collective-permute-start.6) | collective-permute-done | bytes 2592 | tf_op jit(solution)/shard_map/ppermute | solution.py:223
  56.1 0.5 copy-done.3
  56.7 0.0 copy-done.7
  56.7 0.0 copy-done.9
  56.7 4.4 %shard_map.84 = f32[10,64,256]{2,1,0:T(8,128)} custom-call(s32[2]{0:T(128)} %si_ref.5, s32[2]{0:T(128)} %bitcast.4, s32[1]{0:T(128)} %bitcast.1.flag_ref, f32[10,10]{1,0:T(8,128)} %lm_ref.3, f32[10,64,256]{2,1,0:T(8,128)} %get-tuple-element.21.adj_ref, f32[64,256]{1,0:T(8,128)} %d_ref.5, f32[4,10,64,256]{3,2,1,0:T(8,128)} %t_ref.3, ...), custom_call_target="tpu_custom_call" | custom-call | flops 9830400 | bytes 5242880 | tf_op jit(solution)/shard_map/pallas_call | solution.py:182
  (21 shorter events, 0.0 us)
Async XLA Ops:
  3.9 24.8 %collective-permute-start.3 = (f32[10,256]{1,0:T(8,128)S(1)}, f32[10,256]{1,0:T(8,128)S(1)}, u32[]{:S(2)}, u32[]{:S(2)}) collective-permute-start(f32[10,256]{1,0:T(8,128)S(1)} %rev.6), channel_id=1, source_target_pairs={{3,255},{7,251},{11,247},{15,243},{19,239},{23,235},{27,231},{31,2... | collective-permute-start | bytes 30728 | tf_op jit(solution)/shard_map/ppermute | solution.py:226
  4.6 24.1 %collective-permute-start.2 = (f32[10,256]{1,0:T(8,128)}, f32[10,256]{1,0:T(8,128)S(1)}, u32[]{:S(2)}, u32[]{:S(2)}) collective-permute-start(f32[10,256]{1,0:T(8,128)} %get-tuple-element.18), channel_id=1, source_target_pairs={{1,0},{2,1},{3,2},{5,4},{6,5},{7,6},{9,8},{10,9},{11,10},{13,12},{... | collective-permute-start | bytes 30728 | tf_op jit(solution)/shard_map/ppermute | solution.py:224
  6.5 22.2 %collective-permute-start.4 = (f32[10,256]{1,0:T(8,128)}, f32[10,256]{1,0:T(8,128)S(1)}, u32[]{:S(2)}, u32[]{:S(2)}) collective-permute-start(f32[10,256]{1,0:T(8,128)} %get-tuple-element.20), channel_id=1, source_target_pairs={{0,1},{1,2},{2,3},{4,5},{5,6},{6,7},{8,9},{9,10},{10,11},{12,13},{... | collective-permute-start | bytes 30728 | tf_op jit(solution)/shard_map/ppermute | solution.py:225
  18.5 4.2 %collective-permute-start = (f32[64,10]{1,0:T(8,128)}, f32[64,10]{1,0:T(8,128)S(1)}, u32[]{:S(2)}, u32[]{:S(2)}) collective-permute-start(f32[64,10]{1,0:T(8,128)} %get-tuple-element.16), channel_id=1, source_target_pairs={{0,252},{4,0},{8,4},{12,8},{16,12},{20,16},{24,20},{28,24},{32,28}... | collective-permute-start | bytes 7688 | tf_op jit(solution)/shard_map/ppermute | solution.py:222
  18.9 9.8 %collective-permute-start.1 = (f32[64,10]{1,0:T(8,128)}, f32[64,10]{1,0:T(8,128)S(1)}, u32[]{:S(2)}, u32[]{:S(2)}) collective-permute-start(f32[64,10]{1,0:T(8,128)} %get-tuple-element.17), channel_id=1, source_target_pairs={{0,4},{4,8},{8,12},{12,16},{16,20},{20,24},{24,28},{28,32},{32,36}... | collective-permute-start | bytes 7688 | tf_op jit(solution)/shard_map/ppermute | solution.py:223
  22.7 6.1 %copy-start = (f32[64,10]{1,0:T(8,128)}, f32[64,10]{1,0:T(8,128)S(1)}, u32[]{:S(2)}) copy-start(f32[64,10]{1,0:T(8,128)S(1)} %collective-permute-done.he_ref) | copy-start | bytes 7684
  28.7 0.6 copy-start.1
  28.7 0.6 copy-start.4
  28.7 0.6 copy-start.5
  28.8 0.6 copy-start.6
  35.6 20.5 %collective-permute-start.8 = (f32[10,256]{1,0:T(8,128)S(1)}, f32[10,256]{1,0:T(8,128)S(1)}, u32[]{:S(2)}, u32[]{:S(2)}) collective-permute-start(f32[10,256]{1,0:T(8,128)S(1)} %rev.7), channel_id=1, source_target_pairs={{3,255},{7,251},{11,247},{15,243},{19,239},{23,235},{27,231},{31,2... | collective-permute-start | bytes 30728 | tf_op jit(solution)/shard_map/ppermute | solution.py:226
  36.2 19.9 %collective-permute-start.7 = (f32[10,256]{1,0:T(8,128)}, f32[10,256]{1,0:T(8,128)S(1)}, u32[]{:S(2)}, u32[]{:S(2)}) collective-permute-start(f32[10,256]{1,0:T(8,128)} %get-tuple-element.24), channel_id=1, source_target_pairs={{1,0},{2,1},{3,2},{5,4},{6,5},{7,6},{9,8},{10,9},{11,10},{13,12},{... | collective-permute-start | bytes 30728 | tf_op jit(solution)/shard_map/ppermute | solution.py:224
  39.3 16.8 %collective-permute-start.9 = (f32[10,256]{1,0:T(8,128)}, f32[10,256]{1,0:T(8,128)S(1)}, u32[]{:S(2)}, u32[]{:S(2)}) collective-permute-start(f32[10,256]{1,0:T(8,128)} %get-tuple-element.26), channel_id=1, source_target_pairs={{0,1},{1,2},{2,3},{4,5},{5,6},{6,7},{8,9},{9,10},{10,11},{12,13},{... | collective-permute-start | bytes 30728 | tf_op jit(solution)/shard_map/ppermute | solution.py:225
  41.2 6.9 %collective-permute-start.5 = (f32[64,10]{1,0:T(8,128)}, f32[64,10]{1,0:T(8,128)S(1)}, u32[]{:S(2)}, u32[]{:S(2)}) collective-permute-start(f32[64,10]{1,0:T(8,128)} %get-tuple-element.22), channel_id=1, source_target_pairs={{0,252},{4,0},{8,4},{12,8},{16,12},{20,16},{24,20},{28,24},{32,28}... | collective-permute-start | bytes 7688 | tf_op jit(solution)/shard_map/ppermute | solution.py:222
  46.2 9.8 %collective-permute-start.6 = (f32[64,10]{1,0:T(8,128)}, f32[64,10]{1,0:T(8,128)S(1)}, u32[]{:S(2)}, u32[]{:S(2)}) collective-permute-start(f32[64,10]{1,0:T(8,128)} %get-tuple-element.23), channel_id=1, source_target_pairs={{0,4},{4,8},{8,12},{12,16},{16,20},{20,24},{24,28},{28,32},{32,36}... | collective-permute-start | bytes 7688 | tf_op jit(solution)/shard_map/ppermute | solution.py:223
  48.1 8.0 %copy-start.2 = (f32[64,10]{1,0:T(8,128)}, f32[64,10]{1,0:T(8,128)S(1)}, u32[]{:S(2)}) copy-start(f32[64,10]{1,0:T(8,128)S(1)} %collective-permute-done.5.he_ref) | copy-start | bytes 7684
  56.1 0.6 copy-start.3
  56.1 0.6 %copy-start.7 = (f32[10,256]{1,0:T(8,128)}, f32[10,256]{1,0:T(8,128)S(1)}, u32[]{:S(2)}) copy-start(f32[10,256]{1,0:T(8,128)S(1)} %collective-permute-done.8.hf_ref) | copy-start | bytes 30724
  56.1 0.6 copy-start.8
  56.1 0.6 %copy-start.9 = (f32[10,256]{1,0:T(8,128)}, f32[10,256]{1,0:T(8,128)S(1)}, u32[]{:S(2)}) copy-start(f32[10,256]{1,0:T(8,128)S(1)} %collective-permute-done.9.hs_ref) | copy-start | bytes 30724

commit v3 on v2

v3 whole, which is shorter than its diff:
```python
import functools

import jax
import jax.numpy as jnp
from jax import lax
from jax.experimental import pallas as pl
from jax.experimental.pallas import tpu as pltpu
from jax.sharding import PartitionSpec as P

TLON = 128
STEPS = 2


advect_scale = 0.25
damping = 0.3


def shift_pairs(count, delta, periodic):
    pairs = []
    for i in range(count):
        j = i + delta
        if periodic:
            pairs.append((i, j % count))
        elif 0 <= j < count:
            pairs.append((i, j))
    return pairs


def wet_field(wt_ref, rows, width):
    lane = lax.broadcasted_iota(jnp.int32, (rows, width), 1)
    wet_i = jnp.zeros((rows, width), jnp.int32)
    for t in range(width // TLON):
        inside = (lane >= t * TLON) & (lane < (t + 1) * TLON)
        wet_i = jnp.where(inside, wt_ref[t], wet_i)
    return wet_i.astype(jnp.float32)


def reverse_lanes(x):
    width = x.shape[-1]
    i = lax.broadcasted_iota(jnp.int32, (width, width), 0)
    j = lax.broadcasted_iota(jnp.int32, (width, width), 1)
    flip = jnp.where(i + j == width - 1, 1.0, 0.0).astype(jnp.bfloat16)
    x1 = x.astype(jnp.bfloat16)
    r1 = x - x1.astype(jnp.float32)
    x2 = r1.astype(jnp.bfloat16)
    x3 = (r1 - x2.astype(jnp.float32)).astype(jnp.bfloat16)

    def perm(part):
        return jnp.dot(part, flip, preferred_element_type=jnp.float32)

    return (perm(x1) + perm(x2)) + perm(x3)


class Collector:
    def __init__(self, levels, rows, width, reverse_fold):
        self.levels = levels
        self.rows = rows
        self.width = width
        self.reverse_fold = reverse_fold
        self.lane = lax.broadcasted_iota(jnp.int32, (rows, TLON), 1)
        self.row = lax.broadcasted_iota(jnp.int32, (16, width), 0)
        self.cols = [jnp.zeros((rows, TLON), jnp.float32) for _ in range(2)]
        self.rows_acc = [jnp.zeros((16, width), jnp.float32) for _ in range(3)]

    def add(self, l, east, west, north, south, fold):
        for i, col in enumerate((east, west)):
            wide = jnp.broadcast_to(col, (self.rows, TLON))
            self.cols[i] = jnp.where(self.lane == l, wide, self.cols[i])
        for i, line in enumerate((north, south, fold)):
            tall = jnp.broadcast_to(line, (16, self.width))
            self.rows_acc[i] = jnp.where(self.row == l, tall, self.rows_acc[i])

    def finish(self, pe_ref, pw_ref, pn_ref, ps_ref, pf_ref):
        levels = self.levels
        pe_ref[...] = self.cols[0][:, :levels]
        pw_ref[...] = self.cols[1][:, :levels]
        pn_ref[...] = self.rows_acc[0][:levels]
        ps_ref[...] = self.rows_acc[1][:levels]
        fold = self.rows_acc[2]
        if self.reverse_fold:
            fold = reverse_lanes(fold)
        pf_ref[...] = fold[:levels]


def coefficients(l, d, u, v, rows, width):
    return (
        d[:, 0:1] + advect_scale * u[:, 0:1],
        d[:, width - 1:width] - advect_scale * u[:, width - 1:width],
        d[0:1, :] + advect_scale * v[0:1, :],
        d[rows - 1:rows, :] - advect_scale * v[rows - 1:rows, :],
        d[rows - 1:rows, :] + advect_scale * v[rows - 1:rows, :],
    )


def edge_values(ce, cw, cn, cs, cf, a, rows, width):
    return (
        ce * a[:, 0:1],
        cw * a[:, width - 1:width],
        cn * a[0:1, :],
        cs * a[rows - 1:rows, :],
        cf * a[rows - 1:rows, :],
    )


def prologue_kernel(si_ref, wt_ref, af_ref, d_ref, u_ref, v_ref, pe_ref, pw_ref, pn_ref, ps_ref, pf_ref):
    del si_ref
    levels, rows, width = af_ref.shape
    wet = wet_field(wt_ref, rows, width)
    d = d_ref[...]
    out = Collector(levels, rows, width, True)
    for l in range(levels):
        coef = coefficients(l, d, u_ref[l], v_ref[l], rows, width)
        out.add(l, *edge_values(*coef, af_ref[l] * wet, rows, width))
    out.finish(pe_ref, pw_ref, pn_ref, ps_ref, pf_ref)


def core_kernel(first, emit, si_ref, wt_ref, lm_ref, adj_ref, d_ref, t_ref, u_ref, v_ref, *rest):
    del si_ref
    if emit:
        u2_ref, v2_ref, out_ref, ce_ref, cw_ref, cn_ref, cs_ref, cf_ref, a_ref = rest
    else:
        out_ref, a_ref = rest
    levels, rows, width = adj_ref.shape
    lane = lax.broadcasted_iota(jnp.int32, (rows, width), 1)
    row = lax.broadcasted_iota(jnp.int32, (rows, width), 0)
    wet = wet_field(wt_ref, rows, width)
    if first:
        for m in range(levels):
            a_ref[m] = adj_ref[m] * wet
        src = a_ref
    else:
        src = adj_ref
    d = d_ref[...]
    coef = Collector(levels, rows, width, False) if emit else None

    for l in range(levels):
        a = src[l]
        vertical = lm_ref[0, l] * src[0]
        for m in range(1, levels):
            vertical = vertical + lm_ref[m, l] * src[m]
        s = d * a
        zf = u_ref[l] * a
        mf = v_ref[l] * a
        east = jnp.where(lane == width - 1, 0.0, pltpu.roll(s + advect_scale * zf, width - 1, 1))
        west = jnp.where(lane == 0, 0.0, pltpu.roll(s - advect_scale * zf, 1, 1))
        north = jnp.where(row == rows - 1, 0.0, pltpu.roll(s + advect_scale * mf, rows - 1, 0))
        south = jnp.where(row == 0, 0.0, pltpu.roll(s - advect_scale * mf, 1, 0))
        t = t_ref[l]
        out_ref[l] = wet * (a - 4.0 * s + east + west + north + south + vertical - damping * t * t * a)
        if emit:
            coef.add(l, *coefficients(l, d, u2_ref[l], v2_ref[l], rows, width))
    if emit:
        coef.finish(ce_ref, cw_ref, cn_ref, cs_ref, cf_ref)


def fix_kernel(emit, wt_ref, flag_ref, part_ref, he_ref, hw_ref, hn_ref, hf_ref, hs_ref, *rest):
    if emit:
        ce_ref, cw_ref, cn_ref, cs_ref, cf_ref, out_ref, pe_ref, pw_ref, pn_ref, ps_ref, pf_ref = rest
    else:
        (out_ref,) = rest
    levels, rows, width = part_ref.shape
    lane = lax.broadcasted_iota(jnp.int32, (rows, width), 1)
    row = lax.broadcasted_iota(jnp.int32, (rows, width), 0)
    wet = wet_field(wt_ref, rows, width)
    he = he_ref[...]
    hw = hw_ref[...]
    top = flag_ref[0] == 1
    if emit:
        ce = ce_ref[...]
        cw = cw_ref[...]
        out = Collector(levels, rows, width, True)
    for l in range(levels):
        north_row = jnp.where(top, hf_ref[l:l + 1, :], hn_ref[l:l + 1, :])
        corr = (
            jnp.where(lane == width - 1, jnp.broadcast_to(he[:, l:l + 1], (rows, width)), 0.0)
            + jnp.where(lane == 0, jnp.broadcast_to(hw[:, l:l + 1], (rows, width)), 0.0)
            + jnp.where(row == rows - 1, north_row, 0.0)
            + jnp.where(row == 0, hs_ref[l:l + 1, :], 0.0)
        )
        new = part_ref[l] + wet * corr
        out_ref[l] = new
        if emit:
            coef = (ce[:, l:l + 1], cw[:, l:l + 1], cn_ref[l:l + 1, :], cs_ref[l:l + 1, :], cf_ref[l:l + 1, :])
            out.add(l, *edge_values(*coef, new, rows, width))
    if emit:
        out.finish(pe_ref, pw_ref, pn_ref, ps_ref, pf_ref)


def payload_shapes(levels, rows, width):
    lon = jax.ShapeDtypeStruct((rows, levels), jnp.float32)
    lat = jax.ShapeDtypeStruct((levels, width), jnp.float32)
    return [lon, lon, lat, lat, lat]


def whole(shape):
    return pl.BlockSpec(shape, lambda i, *_: (0,) * len(shape))


def state_spec(k, levels, rows, width):
    return pl.BlockSpec((None, levels, rows, width), lambda i, si, *_: (si[k], 0, 0, 0))


def run_prologue(k, si, wt, af, d, zonal, merid):
    levels, rows, width = af.shape
    shapes = payload_shapes(levels, rows, width)
    n = levels * rows * width
    return pl.pallas_call(
        prologue_kernel,
        out_shape=shapes,
        grid_spec=pltpu.PrefetchScalarGridSpec(
            num_scalar_prefetch=2,
            grid=(1,),
            in_specs=[whole(af.shape), whole(d.shape), state_spec(k, levels, rows, width),
                      state_spec(k, levels, rows, width)],
            out_specs=[whole(s.shape) for s in shapes],
        ),
        cost_estimate=pl.CostEstimate(flops=2 * n, bytes_accessed=12 * n, transcendentals=0),
    )(si, wt, af, d, zonal, merid)


def run_core(k, k_next, si, wt, lm, adj, d, tracer, zonal, merid):
    levels, rows, width = adj.shape
    first = k_next is not None
    emit = k_next is not None
    state = state_spec(k, levels, rows, width)
    in_specs = [pl.BlockSpec(memory_space=pltpu.SMEM), whole(adj.shape), whole(d.shape), state, state, state]
    args = [si, wt, lm, adj, d, tracer, zonal, merid]
    out_shape = [jax.ShapeDtypeStruct(adj.shape, jnp.float32)]
    if emit:
        nxt = state_spec(k_next, levels, rows, width)
        in_specs += [nxt, nxt]
        args += [zonal, merid]
        out_shape += payload_shapes(levels, rows, width)
    n = levels * rows * width
    outs = pl.pallas_call(
        functools.partial(core_kernel, first, emit),
        out_shape=out_shape,
        grid_spec=pltpu.PrefetchScalarGridSpec(
            num_scalar_prefetch=2,
            grid=(1,),
            in_specs=in_specs,
            out_specs=[whole(s.shape) for s in out_shape],
            scratch_shapes=[pltpu.VMEM((levels, rows, width), jnp.float32)],
        ),
        cost_estimate=pl.CostEstimate(flops=60 * n, bytes_accessed=32 * n, transcendentals=0),
    )(*args)
    return outs[0], outs[1:]


def run_fix(wt, flags, part, halos, coefs):
    levels, rows, width = part.shape
    emit = bool(coefs)
    args = [wt, flags, part, *halos, *coefs]
    in_specs = [whole(x.shape) for x in args[2:]]
    out_shape = [jax.ShapeDtypeStruct(part.shape, jnp.float32)]
    if emit:
        out_shape += payload_shapes(levels, rows, width)
    n = levels * rows * width
    outs = pl.pallas_call(
        functools.partial(fix_kernel, emit),
        out_shape=out_shape,
        grid_spec=pltpu.PrefetchScalarGridSpec(
            num_scalar_prefetch=2,
            grid=(1,),
            in_specs=in_specs,
            out_specs=[whole(s.shape) for s in out_shape],
        ),
        cost_estimate=pl.CostEstimate(flops=10 * n, bytes_accessed=8 * n, transcendentals=0),
    )(*args)
    return outs[0], outs[1:]


def shards(
    adjoint_final,
    stored_tracer,
    stored_zonal,
    stored_meridional,
    diffusivity,
    level_mixing,
    wet_tiles,
    state_index,
):
    n_lat = lax.axis_size("lat")
    n_lon = lax.axis_size("lon")
    wt = wet_tiles.reshape(-1)
    is_top = lax.axis_index("lat") == n_lat - 1
    flags = is_top.astype(jnp.int32).reshape(1)

    to_west = shift_pairs(n_lon, -1, True)
    to_east = shift_pairs(n_lon, 1, True)
    to_south = shift_pairs(n_lat, -1, False)
    to_north = shift_pairs(n_lat, 1, False)
    top = n_lat - 1
    fold = [(j * n_lat + top, (n_lon - 1 - j) * n_lat + top) for j in range(n_lon)]

    def exchange(payloads):
        pe, pw, pn, ps, pf = payloads
        he = lax.ppermute(pe, "lon", to_west)
        hw = lax.ppermute(pw, "lon", to_east)
        hn = lax.ppermute(pn, "lat", to_south)
        hs = lax.ppermute(ps, "lat", to_north)
        hf = lax.ppermute(pf, ("lon", "lat"), fold)
        return he, hw, hn, hf, hs

    payloads = run_prologue(STEPS - 1, state_index, wt, adjoint_final, diffusivity,
                            stored_zonal, stored_meridional)
    adj = adjoint_final
    for back in range(STEPS):
        k = STEPS - 1 - back
        k_next = k - 1 if k > 0 else None
        halos = exchange(payloads)
        part, coefs = run_core(k, k_next, state_index, wt, level_mixing, adj, diffusivity,
                               stored_tracer, stored_zonal, stored_meridional)
        adj, payloads = run_fix(wt, flags, part, halos, coefs)
    return adj


def solution(mesh):
    return jax.shard_map(
        shards,
        mesh=mesh,
        in_specs=(
            P(None, "lat", "lon"),
            P(None, None, "lat", "lon"),
            P(None, None, "lat", "lon"),
            P(None, None, "lat", "lon"),
            P("lat", "lon"),
            P(),
            P("lat", "lon"),
            P(),
        ),
        out_specs=P(None, "lat", "lon"),
        check_vma=False,
    )
```

time: 61.5 us -> 62.1 us (level)
  waiting for transfers between devices: 18 us -> 8.74 us
  Pallas kernels: 12.8 us -> 19.4 us
  starting transfers between devices: 27.3 us -> 31.7 us
  local copies, waits for them, and re-layouts: 2.88 us -> 1.78 us
    pallas_call x2 -> x4, Pallas kernels: 9.76 us -> 16.3 us  [the longest x2 9.21 us: run_core(): pl.pallas_call(functools.partial(core_kernel, first, emit), out_shape=out...]
    ppermute x2, starting transfers between devices: 13.9 us -> 19.4 us  [exchange(): hs = lax.ppermute(ps, 'lat', to_north)]
    ppermute x2, waiting for transfers between devices: 14 us -> 8.72 us  [exchange(): hw = lax.ppermute(pw, 'lon', to_east)]
    ppermute x2, waiting for transfers between devices: 4.01 us -> 0.01 us  [exchange(): he = lax.ppermute(pe, 'lon', to_west)]
    rev x2 -> x0, local copies, waits for them, and re-layouts: 1.68 us -> none  [exchange(): hf = lax.ppermute(pf[:, ::-1], ('lon', 'lat'), fold)]
    ppermute x2, starting transfers between devices: 4.98 us -> 3.82 us  [exchange(): hn = lax.ppermute(pn, 'lat', to_south)]
  transfers between devices with their start and end apart: 10 -> 10, of which waited for: 4 -> 2; matrix products, arithmetic and copies ran while one was open for 0% -> 0% of each run, Pallas kernels for 0% -> 15%
where the time goes in v3:
time: 62.1 us; the launch traced here: 61.7 us
  starting transfers between devices  31.7 us (51%)
  Pallas kernels  19.4 us (31%)
  waiting for transfers between devices  8.74 us (14%)
  local copies, waits for them, and re-layouts  1.78 us (3%)
    ppermute x2, starting transfers between devices, exchange(): hs = lax.ppermute(ps, 'lat', to_north)  19.4 us
    pallas_call x2, Pallas kernels, run_core(): pl.pallas_call(functools.partial(core_kernel, first, emit), out_shape=out...  9.21 us
    ppermute x2, waiting for transfers between devices, exchange(): hw = lax.ppermute(pw, 'lon', to_east)  8.72 us
    pallas_call x2, Pallas kernels, run_fix(): pl.pallas_call(functools.partial(fix_kernel, emit), out_shape=out_shape,...  7.05 us
    ppermute x2, starting transfers between devices, exchange(): he = lax.ppermute(pe, 'lon', to_west)  5.37 us
    ppermute x2, starting transfers between devices, exchange(): hn = lax.ppermute(pn, 'lat', to_south)  3.82 us
    pallas_call x1, Pallas kernels, run_prologue(): pl.pallas_call(prologue_kernel, out_shape=shapes, grid_spec=pltpu.Prefetc...  3.09 us
    unnamed x20, local copies, waits for them, and re-layouts  1.78 us
  transfers between devices with their start and end apart: 10, of which 2 were waited for; matrix products, arithmetic and copies ran while one was open for 0% of the time, Pallas kernels for 15%

profile of v3, /device:TPU:2, one launch (start us, length us, event | category | flops | bytes accessed | tf_op | source)
XLA Modules:
  0.0 61.7 jit_solution(1031489132063976811)
XLA Ops:
  0.0 3.1 %shard_map.83 = (f32[64,10]{1,0:T(8,128)}, f32[64,10]{1,0:T(8,128)}, f32[10,256]{1,0:T(8,128)}, f32[10,256]{1,0:T(8,128)}, f32[10,256]{1,0:T(8,128)}) custom-call(s32[2]{0:T(128)} %si_ref.5, s32[2]{0:T(128)} %bitcast.2, f32[10,64,256]{2,1,0:T(8,128)} %af_ref.1, f32[64,256]{1,0:T(8,128)} %d_ref.5, f32[4,10,64,256]{3,2,1,0:T(8,128)} %u_ref.5, ...), custom_call_target="tpu_custom_call" | custom-call | flops 327680 | bytes 1966080 | tf_op jit(solution)/shard_map/pallas_call | solution.py:207
  3.1 1.9 %collective-permute-start.2 = (f32[10,256]{1,0:T(8,128)}, f32[10,256]{1,0:T(8,128)S(1)}, u32[]{:S(2)}, u32[]{:S(2)}) collective-permute-start(f32[10,256]{1,0:T(8,128)} %get-tuple-element.25), channel_id=1, source_target_pairs={{1,0},{2,1},{3,2},{5,4},{6,5},{7,6},{9,8},{10,9},{11,10},{13,12},{... | collective-permute-start | bytes 30728 | tf_op jit(solution)/shard_map/ppermute | solution.py:300
  5.0 0.7 %collective-permute-start.3 = (f32[10,256]{1,0:T(8,128)}, f32[10,256]{1,0:T(8,128)S(1)}, u32[]{:S(2)}, u32[]{:S(2)}) collective-permute-start(f32[10,256]{1,0:T(8,128)} %get-tuple-element.26), channel_id=1, source_target_pairs={{3,255},{7,251},{11,247},{15,243},{19,239},{23,235},{27,231},{31,2... | collective-permute-start | bytes 30728 | tf_op jit(solution)/shard_map/ppermute | solution.py:302
  5.7 13.2 %collective-permute-start.4 = (f32[10,256]{1,0:T(8,128)}, f32[10,256]{1,0:T(8,128)S(1)}, u32[]{:S(2)}, u32[]{:S(2)}) collective-permute-start(f32[10,256]{1,0:T(8,128)} %get-tuple-element.27), channel_id=1, source_target_pairs={{0,1},{1,2},{2,3},{4,5},{5,6},{6,7},{8,9},{9,10},{10,11},{12,13},{... | collective-permute-start | bytes 30728 | tf_op jit(solution)/shard_map/ppermute | solution.py:301
  18.9 0.4 collective-permute-start
  19.3 1.7 %collective-permute-start.1 = (f32[64,10]{1,0:T(8,128)}, f32[64,10]{1,0:T(8,128)S(1)}, u32[]{:S(2)}, u32[]{:S(2)}) collective-permute-start(f32[64,10]{1,0:T(8,128)} %get-tuple-element.24), channel_id=1, source_target_pairs={{0,4},{4,8},{8,12},{12,16},{16,20},{20,24},{24,28},{28,32},{32,36}... | collective-permute-start | bytes 7688 | tf_op jit(solution)/shard_map/ppermute | solution.py:299
  21.0 4.9 %shard_map.82 = (f32[10,64,256]{2,1,0:T(8,128)}, f32[64,10]{1,0:T(8,128)}, f32[64,10]{1,0:T(8,128)}, f32[10,256]{1,0:T(8,128)}, f32[10,256]{1,0:T(8,128)}, /*index=5*/f32[10,256]{1,0:T(8,128)}) custom-call(s32[2]{0:T(128)} %si_ref.5, s32[2]{0:T(128)} %bitcast.3, f32[10,10]{1,0:T(8,128)} %lm_ref.3, f32[10,64,256]{2,1,0:T(8,128)} %af_ref.1, f32[64,256]{1,0:T(8,128)} %d_ref.5, ...), custom_call_target="tpu_custom_call" | custom-call | flops 9830400 | bytes 5242880 | tf_op jit(solution)/shard_map/pallas_call | solution.py:235
  25.9 3.2 %collective-permute-done.1.hw_ref = f32[64,10]{1,0:T(8,128)S(1)} collective-permute-done((f32[64,10]{1,0:T(8,128)}, f32[64,10]{1,0:T(8,128)S(1)}, u32[]{:S(2)}, u32[]{:S(2)}) %collective-permute-start.1) | collective-permute-done | bytes 2592 | tf_op jit(solution)/shard_map/ppermute | solution.py:299
  29.1 0.0 collective-permute-done.2.hn_ref
  29.2 0.6 copy-done.1
  29.7 0.0 copy-done.7
  29.8 0.0 copy-done.8
  29.8 0.0 copy-done.9
  29.8 4.2 %shard_map.84 = (f32[10,64,256]{2,1,0:T(8,128)}, f32[64,10]{1,0:T(8,128)}, f32[64,10]{1,0:T(8,128)}, f32[10,256]{1,0:T(8,128)}, f32[10,256]{1,0:T(8,128)}, /*index=5*/f32[10,256]{1,0:T(8,128)}) custom-call(s32[2]{0:T(128)} %bitcast.4, s32[1]{0:T(128)} %bitcast.1.flag_ref, f32[10,64,256]{2,1,0:T(8,128)} %get-tuple-element.22.part_ref, f32[64,10]{1,0:T(8,128)} %copy-done, ...), custom_call_target="tpu_custom_call" | custom-call | flops 1638400 | bytes 1310720 | tf_op jit(solution)/shard_map/pallas_call | solution.py:259
  33.9 1.9 %collective-permute-start.7 = (f32[10,256]{1,0:T(8,128)}, f32[10,256]{1,0:T(8,128)S(1)}, u32[]{:S(2)}, u32[]{:S(2)}) collective-permute-start(f32[10,256]{1,0:T(8,128)} %get-tuple-element.36), channel_id=1, source_target_pairs={{1,0},{2,1},{3,2},{5,4},{6,5},{7,6},{9,8},{10,9},{11,10},{13,12},{... | collective-permute-start | bytes 30728 | tf_op jit(solution)/shard_map/ppermute | solution.py:300
  35.9 0.7 %collective-permute-start.8 = (f32[10,256]{1,0:T(8,128)}, f32[10,256]{1,0:T(8,128)S(1)}, u32[]{:S(2)}, u32[]{:S(2)}) collective-permute-start(f32[10,256]{1,0:T(8,128)} %get-tuple-element.37), channel_id=1, source_target_pairs={{3,255},{7,251},{11,247},{15,243},{19,239},{23,235},{27,231},{31,2... | collective-permute-start | bytes 30728 | tf_op jit(solution)/shard_map/ppermute | solution.py:302
  36.5 6.2 %collective-permute-start.9 = (f32[10,256]{1,0:T(8,128)}, f32[10,256]{1,0:T(8,128)S(1)}, u32[]{:S(2)}, u32[]{:S(2)}) collective-permute-start(f32[10,256]{1,0:T(8,128)} %get-tuple-element.38), channel_id=1, source_target_pairs={{0,1},{1,2},{2,3},{4,5},{5,6},{6,7},{8,9},{9,10},{10,11},{12,13},{... | collective-permute-start | bytes 30728 | tf_op jit(solution)/shard_map/ppermute | solution.py:301
  42.7 5.0 %collective-permute-start.5 = (f32[64,10]{1,0:T(8,128)}, f32[64,10]{1,0:T(8,128)S(1)}, u32[]{:S(2)}, u32[]{:S(2)}) collective-permute-start(f32[64,10]{1,0:T(8,128)} %get-tuple-element.34), channel_id=1, source_target_pairs={{0,252},{4,0},{8,4},{12,8},{16,12},{20,16},{24,20},{28,24},{32,28}... | collective-permute-start | bytes 7688 | tf_op jit(solution)/shard_map/ppermute | solution.py:298
  47.7 4.3 %shard_map.85.part_ref = f32[10,64,256]{2,1,0:T(8,128)} custom-call(s32[2]{0:T(128)} %si_ref.5, s32[2]{0:T(128)} %bitcast.5, f32[10,10]{1,0:T(8,128)} %lm_ref.3, f32[10,64,256]{2,1,0:T(8,128)} %get-tuple-element.33.adj_ref, f32[64,256]{1,0:T(8,128)} %d_ref.5, f32[4,10,64,256]{3,2,1,0:T(8,128)} %t_ref.3, f32[4,10,64,256]{3,2,1,0:T(8,128)} %u_ref.5, ...), custom_call_target="tpu_custom_call" | custom-call | flops 9830400 | bytes 5242880 | tf_op jit(solution)/shard_map/pallas_call | solution.py:235
  52.1 5.5 %collective-permute-done.6.hw_ref = f32[64,10]{1,0:T(8,128)S(1)} collective-permute-done((f32[64,10]{1,0:T(8,128)}, f32[64,10]{1,0:T(8,128)S(1)}, u32[]{:S(2)}, u32[]{:S(2)}) %collective-permute-start.6) | collective-permute-done | bytes 2592 | tf_op jit(solution)/shard_map/ppermute | solution.py:299
  57.6 0.6 copy-done.3
  58.2 0.0 copy-done.5
  58.2 0.6 copy-done.6
  58.8 2.9 %shard_map.86 = f32[10,64,256]{2,1,0:T(8,128)} custom-call(s32[2]{0:T(128)} %bitcast.6, s32[1]{0:T(128)} %bitcast.1.flag_ref, f32[10,64,256]{2,1,0:T(8,128)} %shard_map.85.part_ref, f32[64,10]{1,0:T(8,128)} %copy-done.2, f32[64,10]{1,0:T(8,128)} %copy-done.3, f32[10,256]{1,0:T(8,128)} %copy-done.4, f32[10,256]{1,0:T(8,128)} %copy-done.5, f32[10,256]{1,0:T(8,128)} %copy-done.6), custom_call_target="tpu_custom_call" | custom-call | flops 1638400 | bytes 1310720 | tf_op jit(solution)/shard_map/pallas_call | solution.py:259
  (21 shorter events, 0.0 us)
Async XLA Ops:
  3.1 26.1 %collective-permute-start.2 = (f32[10,256]{1,0:T(8,128)}, f32[10,256]{1,0:T(8,128)S(1)}, u32[]{:S(2)}, u32[]{:S(2)}) collective-permute-start(f32[10,256]{1,0:T(8,128)} %get-tuple-element.25), channel_id=1, source_target_pairs={{1,0},{2,1},{3,2},{5,4},{6,5},{7,6},{9,8},{10,9},{11,10},{13,12},{... | collective-permute-start | bytes 30728 | tf_op jit(solution)/shard_map/ppermute | solution.py:300
  5.0 24.1 %collective-permute-start.3 = (f32[10,256]{1,0:T(8,128)}, f32[10,256]{1,0:T(8,128)S(1)}, u32[]{:S(2)}, u32[]{:S(2)}) collective-permute-start(f32[10,256]{1,0:T(8,128)} %get-tuple-element.26), channel_id=1, source_target_pairs={{3,255},{7,251},{11,247},{15,243},{19,239},{23,235},{27,231},{31,2... | collective-permute-start | bytes 30728 | tf_op jit(solution)/shard_map/ppermute | solution.py:302
  5.7 23.5 %collective-permute-start.4 = (f32[10,256]{1,0:T(8,128)}, f32[10,256]{1,0:T(8,128)S(1)}, u32[]{:S(2)}, u32[]{:S(2)}) collective-permute-start(f32[10,256]{1,0:T(8,128)} %get-tuple-element.27), channel_id=1, source_target_pairs={{0,1},{1,2},{2,3},{4,5},{5,6},{6,7},{8,9},{9,10},{10,11},{12,13},{... | collective-permute-start | bytes 30728 | tf_op jit(solution)/shard_map/ppermute | solution.py:301
  18.9 7.0 %collective-permute-start = (f32[64,10]{1,0:T(8,128)}, f32[64,10]{1,0:T(8,128)S(1)}, u32[]{:S(2)}, u32[]{:S(2)}) collective-permute-start(f32[64,10]{1,0:T(8,128)} %get-tuple-element.23), channel_id=1, source_target_pairs={{0,252},{4,0},{8,4},{12,8},{16,12},{20,16},{24,20},{28,24},{32,28}... | collective-permute-start | bytes 7688 | tf_op jit(solution)/shard_map/ppermute | solution.py:298
  19.3 9.8 %collective-permute-start.1 = (f32[64,10]{1,0:T(8,128)}, f32[64,10]{1,0:T(8,128)S(1)}, u32[]{:S(2)}, u32[]{:S(2)}) collective-permute-start(f32[64,10]{1,0:T(8,128)} %get-tuple-element.24), channel_id=1, source_target_pairs={{0,4},{4,8},{8,12},{12,16},{16,20},{20,24},{24,28},{28,32},{32,36}... | collective-permute-start | bytes 7688 | tf_op jit(solution)/shard_map/ppermute | solution.py:299
  25.9 3.3 %copy-start = (f32[64,10]{1,0:T(8,128)}, f32[64,10]{1,0:T(8,128)S(1)}, u32[]{:S(2)}) copy-start(f32[64,10]{1,0:T(8,128)S(1)} %collective-permute-done.he_ref) | copy-start | bytes 7684
  29.1 0.6 copy-start.1
  29.1 0.6 copy-start.7
  29.2 0.6 copy-start.8
  29.2 0.6 copy-start.9
  33.9 23.6 %collective-permute-start.7 = (f32[10,256]{1,0:T(8,128)}, f32[10,256]{1,0:T(8,128)S(1)}, u32[]{:S(2)}, u32[]{:S(2)}) collective-permute-start(f32[10,256]{1,0:T(8,128)} %get-tuple-element.36), channel_id=1, source_target_pairs={{1,0},{2,1},{3,2},{5,4},{6,5},{7,6},{9,8},{10,9},{11,10},{13,12},{... | collective-permute-start | bytes 30728 | tf_op jit(solution)/shard_map/ppermute | solution.py:300
  35.9 21.7 %collective-permute-start.8 = (f32[10,256]{1,0:T(8,128)}, f32[10,256]{1,0:T(8,128)S(1)}, u32[]{:S(2)}, u32[]{:S(2)}) collective-permute-start(f32[10,256]{1,0:T(8,128)} %get-tuple-element.37), channel_id=1, source_target_pairs={{3,255},{7,251},{11,247},{15,243},{19,239},{23,235},{27,231},{31,2... | collective-permute-start | bytes 30728 | tf_op jit(solution)/shard_map/ppermute | solution.py:302
  36.5 21.1 %collective-permute-start.9 = (f32[10,256]{1,0:T(8,128)}, f32[10,256]{1,0:T(8,128)S(1)}, u32[]{:S(2)}, u32[]{:S(2)}) collective-permute-start(f32[10,256]{1,0:T(8,128)} %get-tuple-element.38), channel_id=1, source_target_pairs={{0,1},{1,2},{2,3},{4,5},{5,6},{6,7},{8,9},{9,10},{10,11},{12,13},{... | collective-permute-start | bytes 30728 | tf_op jit(solution)/shard_map/ppermute | solution.py:301
  42.7 9.4 %collective-permute-start.5 = (f32[64,10]{1,0:T(8,128)}, f32[64,10]{1,0:T(8,128)S(1)}, u32[]{:S(2)}, u32[]{:S(2)}) collective-permute-start(f32[64,10]{1,0:T(8,128)} %get-tuple-element.34), channel_id=1, source_target_pairs={{0,252},{4,0},{8,4},{12,8},{16,12},{20,16},{24,20},{28,24},{32,28}... | collective-permute-start | bytes 7688 | tf_op jit(solution)/shard_map/ppermute | solution.py:298
  47.7 9.8 %collective-permute-start.6 = (f32[64,10]{1,0:T(8,128)}, f32[64,10]{1,0:T(8,128)S(1)}, u32[]{:S(2)}, u32[]{:S(2)}) collective-permute-start(f32[64,10]{1,0:T(8,128)} %get-tuple-element.35), channel_id=1, source_target_pairs={{0,4},{4,8},{8,12},{12,16},{16,20},{20,24},{24,28},{28,32},{32,36}... | collective-permute-start | bytes 7688 | tf_op jit(solution)/shard_map/ppermute | solution.py:299
  52.1 5.5 %copy-start.2 = (f32[64,10]{1,0:T(8,128)}, f32[64,10]{1,0:T(8,128)S(1)}, u32[]{:S(2)}) copy-start(f32[64,10]{1,0:T(8,128)S(1)} %collective-permute-done.5.he_ref) | copy-start | bytes 7684
  57.6 0.6 %copy-start.3 = (f32[64,10]{1,0:T(8,128)}, f32[64,10]{1,0:T(8,128)S(1)}, u32[]{:S(2)}) copy-start(f32[64,10]{1,0:T(8,128)S(1)} %collective-permute-done.6.hw_ref) | copy-start | bytes 7684
  57.6 0.6 %copy-start.4 = (f32[10,256]{1,0:T(8,128)}, f32[10,256]{1,0:T(8,128)S(1)}, u32[]{:S(2)}) copy-start(f32[10,256]{1,0:T(8,128)S(1)} %collective-permute-done.7.hn_ref) | copy-start | bytes 30724
  57.6 0.6 %copy-start.5 = (f32[10,256]{1,0:T(8,128)}, f32[10,256]{1,0:T(8,128)S(1)}, u32[]{:S(2)}) copy-start(f32[10,256]{1,0:T(8,128)S(1)} %collective-permute-done.8.hf_ref) | copy-start | bytes 30724
  58.2 0.6 copy-start.6

commit v4 on v3

--- a/solution.py
+++ b/solution.py
@@ -81,6 +81,18 @@
             fold = reverse_lanes(fold)
         pf_ref[...] = fold[:levels]
 
+    def finish_pairs(self, flag_ref, pe_ref, pw_ref, pa_ref, pb_ref):
+        levels = self.levels
+        pe_ref[...] = self.cols[0][:, :levels]
+        pw_ref[...] = self.cols[1][:, :levels]
+        north_going = self.rows_acc[0][:levels]
+        south_going = self.rows_acc[1][:levels]
+        fold = reverse_lanes(self.rows_acc[2])[:levels]
+        even = flag_ref[0] == 0
+        top = flag_ref[1] == 1
+        pa_ref[...] = jnp.where(even, south_going, north_going)
+        pb_ref[...] = jnp.where(top, fold, jnp.where(even, north_going, south_going))
+
 
 def coefficients(l, d, u, v, rows, width):
     return (
@@ -102,7 +114,7 @@
     )
 
 
-def prologue_kernel(si_ref, wt_ref, af_ref, d_ref, u_ref, v_ref, pe_ref, pw_ref, pn_ref, ps_ref, pf_ref):
+def prologue_kernel(si_ref, wt_ref, flag_ref, af_ref, d_ref, u_ref, v_ref, pe_ref, pw_ref, pa_ref, pb_ref):
     del si_ref
     levels, rows, width = af_ref.shape
     wet = wet_field(wt_ref, rows, width)
@@ -111,7 +123,7 @@
     for l in range(levels):
         coef = coefficients(l, d, u_ref[l], v_ref[l], rows, width)
         out.add(l, *edge_values(*coef, af_ref[l] * wet, rows, width))
-    out.finish(pe_ref, pw_ref, pn_ref, ps_ref, pf_ref)
+    out.finish_pairs(flag_ref, pe_ref, pw_ref, pa_ref, pb_ref)
 
 
 def core_kernel(first, emit, si_ref, wt_ref, lm_ref, adj_ref, d_ref, t_ref, u_ref, v_ref, *rest):
@@ -153,37 +165,42 @@
         coef.finish(ce_ref, cw_ref, cn_ref, cs_ref, cf_ref)
 
 
-def fix_kernel(emit, wt_ref, flag_ref, part_ref, he_ref, hw_ref, hn_ref, hf_ref, hs_ref, *rest):
-    if emit:
-        ce_ref, cw_ref, cn_ref, cs_ref, cf_ref, out_ref, pe_ref, pw_ref, pn_ref, ps_ref, pf_ref = rest
+def fix_kernel(emit, wt_ref, flag_ref, part_ref, he_ref, hw_ref, ha_ref, hb_ref, *rest):
+    if emit:
+        ce_ref, cw_ref, cn_ref, cs_ref, cf_ref, out_ref, pe_ref, pw_ref, pa_ref, pb_ref = rest
     else:
         (out_ref,) = rest
     levels, rows, width = part_ref.shape
-    lane = lax.broadcasted_iota(jnp.int32, (rows, width), 1)
-    row = lax.broadcasted_iota(jnp.int32, (rows, width), 0)
     wet = wet_field(wt_ref, rows, width)
+    wet_left, wet_right = wet[:, :TLON], wet[:, width - TLON:]
+    wet_bottom, wet_top = wet[0:1, :], wet[rows - 1:rows, :]
+    lane = lax.broadcasted_iota(jnp.int32, (rows, TLON), 1)
     he = he_ref[...]
     hw = hw_ref[...]
-    top = flag_ref[0] == 1
+    even = flag_ref[0] == 0
     if emit:
         ce = ce_ref[...]
         cw = cw_ref[...]
         out = Collector(levels, rows, width, True)
     for l in range(levels):
-        north_row = jnp.where(top, hf_ref[l:l + 1, :], hn_ref[l:l + 1, :])
-        corr = (
-            jnp.where(lane == width - 1, jnp.broadcast_to(he[:, l:l + 1], (rows, width)), 0.0)
-            + jnp.where(lane == 0, jnp.broadcast_to(hw[:, l:l + 1], (rows, width)), 0.0)
-            + jnp.where(row == rows - 1, north_row, 0.0)
-            + jnp.where(row == 0, hs_ref[l:l + 1, :], 0.0)
-        )
-        new = part_ref[l] + wet * corr
-        out_ref[l] = new
+        x = part_ref[l]
+        east = jnp.where(lane == TLON - 1, jnp.broadcast_to(he[:, l:l + 1], (rows, TLON)), 0.0)
+        west = jnp.where(lane == 0, jnp.broadcast_to(hw[:, l:l + 1], (rows, TLON)), 0.0)
+        out_ref[l] = x
+        out_ref[l, :, width - TLON:] = x[:, width - TLON:] + wet_right * east
+        out_ref[l, :, :TLON] = out_ref[l, :, :TLON] + wet_left * west
+        a_row = ha_ref[l:l + 1, :]
+        b_row = hb_ref[l:l + 1, :]
+        north_row = jnp.where(even, a_row, b_row)
+        south_row = jnp.where(even, b_row, a_row)
+        out_ref[l, rows - 1:rows, :] = out_ref[l, rows - 1:rows, :] + wet_top * north_row
+        out_ref[l, 0:1, :] = out_ref[l, 0:1, :] + wet_bottom * south_row
         if emit:
+            new = out_ref[l]
             coef = (ce[:, l:l + 1], cw[:, l:l + 1], cn_ref[l:l + 1, :], cs_ref[l:l + 1, :], cf_ref[l:l + 1, :])
             out.add(l, *edge_values(*coef, new, rows, width))
     if emit:
-        out.finish(pe_ref, pw_ref, pn_ref, ps_ref, pf_ref)
+        out.finish_pairs(flag_ref, pe_ref, pw_ref, pa_ref, pb_ref)
 
 
 def payload_shapes(levels, rows, width):
@@ -192,6 +209,10 @@
     return [lon, lon, lat, lat, lat]
 
 
+def pair_shapes(levels, rows, width):
+    return payload_shapes(levels, rows, width)[:4]
+
+
 def whole(shape):
     return pl.BlockSpec(shape, lambda i, *_: (0,) * len(shape))
 
@@ -200,22 +221,22 @@
     return pl.BlockSpec((None, levels, rows, width), lambda i, si, *_: (si[k], 0, 0, 0))
 
 
-def run_prologue(k, si, wt, af, d, zonal, merid):
+def run_prologue(k, si, wt, flags, af, d, zonal, merid):
     levels, rows, width = af.shape
-    shapes = payload_shapes(levels, rows, width)
+    shapes = pair_shapes(levels, rows, width)
     n = levels * rows * width
     return pl.pallas_call(
         prologue_kernel,
         out_shape=shapes,
         grid_spec=pltpu.PrefetchScalarGridSpec(
-            num_scalar_prefetch=2,
+            num_scalar_prefetch=3,
             grid=(1,),
             in_specs=[whole(af.shape), whole(d.shape), state_spec(k, levels, rows, width),
                       state_spec(k, levels, rows, width)],
             out_specs=[whole(s.shape) for s in shapes],
         ),
         cost_estimate=pl.CostEstimate(flops=2 * n, bytes_accessed=12 * n, transcendentals=0),
-    )(si, wt, af, d, zonal, merid)
+    )(si, wt, flags, af, d, zonal, merid)
 
 
 def run_core(k, k_next, si, wt, lm, adj, d, tracer, zonal, merid):
@@ -254,7 +275,7 @@
     in_specs = [whole(x.shape) for x in args[2:]]
     out_shape = [jax.ShapeDtypeStruct(part.shape, jnp.float32)]
     if emit:
-        out_shape += payload_shapes(levels, rows, width)
+        out_shape += pair_shapes(levels, rows, width)
     n = levels * rows * width
     outs = pl.pallas_call(
         functools.partial(fix_kernel, emit),
@@ -283,26 +304,28 @@
     n_lat = lax.axis_size("lat")
     n_lon = lax.axis_size("lon")
     wt = wet_tiles.reshape(-1)
-    is_top = lax.axis_index("lat") == n_lat - 1
-    flags = is_top.astype(jnp.int32).reshape(1)
+    lat_index = lax.axis_index("lat")
+    flags = jnp.stack([lat_index % 2, (lat_index == n_lat - 1).astype(jnp.int32)]).astype(jnp.int32)
 
     to_west = shift_pairs(n_lon, -1, True)
     to_east = shift_pairs(n_lon, 1, True)
-    to_south = shift_pairs(n_lat, -1, False)
-    to_north = shift_pairs(n_lat, 1, False)
+    pairs_a = [(i, i ^ 1) for i in range(n_lat)]
     top = n_lat - 1
-    fold = [(j * n_lat + top, (n_lon - 1 - j) * n_lat + top) for j in range(n_lon)]
+    pairs_b = []
+    for j in range(n_lon):
+        for i in range(1, n_lat - 1, 2):
+            pairs_b += [(j * n_lat + i, j * n_lat + i + 1), (j * n_lat + i + 1, j * n_lat + i)]
+        pairs_b.append((j * n_lat + top, (n_lon - 1 - j) * n_lat + top))
 
     def exchange(payloads):
-        pe, pw, pn, ps, pf = payloads
+        pe, pw, pa, pb = payloads
         he = lax.ppermute(pe, "lon", to_west)
         hw = lax.ppermute(pw, "lon", to_east)
-        hn = lax.ppermute(pn, "lat", to_south)
-        hs = lax.ppermute(ps, "lat", to_north)
-        hf = lax.ppermute(pf, ("lon", "lat"), fold)
-        return he, hw, hn, hf, hs
-
-    payloads = run_prologue(STEPS - 1, state_index, wt, adjoint_final, diffusivity,
+        ha = lax.ppermute(pa, "lat", pairs_a)
+        hb = lax.ppermute(pb, ("lon", "lat"), pairs_b)
+        return he, hw, ha, hb
+
+    payloads = run_prologue(STEPS - 1, state_index, wt, flags, adjoint_final, diffusivity,
                             stored_zonal, stored_meridional)
     adj = adjoint_final
     for back in range(STEPS):

time: 62.1 us -> 54 us (0.87)
  the two profiles are of different devices: /device:TPU:2 before, /device:TPU:3 now
where the time goes in v4:
time: 54 us; the launch traced here: 53.8 us
  starting transfers between devices  25.1 us (46%)
  Pallas kernels  19.3 us (36%)
  waiting for transfers between devices  6.79 us (13%)
  local copies, waits for them, and re-layouts  1.79 us (3%)
  other arithmetic  0.65 us (1%)
    ppermute x2, starting transfers between devices, exchange(): hb = lax.ppermute(pb, ('lon', 'lat'), pairs_b)  15.9 us
    pallas_call x2, Pallas kernels, run_core(): pl.pallas_call(functools.partial(core_kernel, first, emit), out_shape=out...  9.22 us
    pallas_call x2, Pallas kernels, run_fix(): pl.pallas_call(functools.partial(fix_kernel, emit), out_shape=out_shape,...  6.98 us
    ppermute x2, waiting for transfers between devices, exchange(): hw = lax.ppermute(pw, 'lon', to_east)  6.77 us
    ppermute x2, starting transfers between devices, exchange(): he = lax.ppermute(pe, 'lon', to_west)  4.82 us
    pallas_call x1, Pallas kernels, run_prologue(): pl.pallas_call(prologue_kernel, out_shape=shapes, grid_spec=pltpu.Prefetc...  3.1 us
    ppermute x2, starting transfers between devices, exchange(): ha = lax.ppermute(pa, 'lat', pairs_a)  2.96 us
    unnamed x16, local copies, waits for them, and re-layouts  1.79 us
  transfers between devices with their start and end apart: 8, of which 2 were waited for; matrix products, arithmetic and copies ran while one was open for 0% of the time, Pallas kernels for 17%

profile of v4, /device:TPU:3, one launch (start us, length us, event | category | flops | bytes accessed | tf_op | source)
XLA Modules:
  0.0 53.8 jit_solution(15903495996300523828)
XLA Ops:
  0.0 0.7 %pad_add_fusion.flag_ref = s32[2]{0:T(128)} fusion(s32[1]{0:T(128)} %bitcast.2, s32[1]{0:T(128)} %bitcast.1), kind=kLoop, calls=%fused_computation | loop fusion | flops 2 | bytes 16 | tf_op jit(solution)/shard_map/stack | solution.py:308
  0.7 3.1 %shard_map.83 = (f32[64,10]{1,0:T(8,128)}, f32[64,10]{1,0:T(8,128)}, f32[10,256]{1,0:T(8,128)}, f32[10,256]{1,0:T(8,128)}) custom-call(s32[2]{0:T(128)} %si_ref.5, s32[2]{0:T(128)} %bitcast.3, s32[2]{0:T(128)} %pad_add_fusion.flag_ref, f32[10,64,256]{2,1,0:T(8,128)} %af_ref.1, f32[64,256]{1,0:T(8,128)} %d_ref.5, f32[4,10,64,256]{3,2,1,0:T(8,128)} %u_ref.5, ...), custom_call_target="tpu_custom_call" | custom-call | flops 327680 | bytes 1966080 | tf_op jit(solution)/shard_map/pallas_call | solution.py:228
  3.8 0.7 %collective-permute-start.2 = (f32[10,256]{1,0:T(8,128)}, f32[10,256]{1,0:T(8,128)S(1)}, u32[]{:S(2)}, u32[]{:S(2)}) collective-permute-start(f32[10,256]{1,0:T(8,128)} %get-tuple-element.23), channel_id=1, source_target_pairs={{0,1},{1,0},{2,3},{3,2},{4,5},{5,4},{6,7},{7,6},{8,9},{9,8},{10,11... | collective-permute-start | bytes 30728 | tf_op jit(solution)/shard_map/ppermute | solution.py:324
  4.4 11.5 %collective-permute-start.3 = (f32[10,256]{1,0:T(8,128)}, f32[10,256]{1,0:T(8,128)S(1)}, u32[]{:S(2)}, u32[]{:S(2)}) collective-permute-start(f32[10,256]{1,0:T(8,128)} %get-tuple-element.24), channel_id=1, source_target_pairs={{1,2},{2,1},{3,255},{5,6},{6,5},{7,251},{9,10},{10,9},{11,247},{13... | collective-permute-start | bytes 30728 | tf_op jit(solution)/shard_map/ppermute | solution.py:325
  15.9 0.1 collective-permute-start
  16.0 1.5 %collective-permute-start.1 = (f32[64,10]{1,0:T(8,128)}, f32[64,10]{1,0:T(8,128)S(1)}, u32[]{:S(2)}, u32[]{:S(2)}) collective-permute-start(f32[64,10]{1,0:T(8,128)} %get-tuple-element.22), channel_id=1, source_target_pairs={{0,4},{4,8},{8,12},{12,16},{16,20},{20,24},{24,28},{28,32},{32,36}... | collective-permute-start | bytes 7688 | tf_op jit(solution)/shard_map/ppermute | solution.py:323
  17.5 4.9 %shard_map.82 = (f32[10,64,256]{2,1,0:T(8,128)}, f32[64,10]{1,0:T(8,128)}, f32[64,10]{1,0:T(8,128)}, f32[10,256]{1,0:T(8,128)}, f32[10,256]{1,0:T(8,128)}, /*index=5*/f32[10,256]{1,0:T(8,128)}) custom-call(s32[2]{0:T(128)} %si_ref.5, s32[2]{0:T(128)} %bitcast.4, f32[10,10]{1,0:T(8,128)} %lm_ref.3, f32[10,64,256]{2,1,0:T(8,128)} %af_ref.1, f32[64,256]{1,0:T(8,128)} %d_ref.5, ...), custom_call_target="tpu_custom_call" | custom-call | flops 9830400 | bytes 5242880 | tf_op jit(solution)/shard_map/pallas_call | solution.py:256
  22.3 0.0 collective-permute-done.he_ref
  22.3 2.4 %collective-permute-done.1.hw_ref = f32[64,10]{1,0:T(8,128)S(1)} collective-permute-done((f32[64,10]{1,0:T(8,128)}, f32[64,10]{1,0:T(8,128)S(1)}, u32[]{:S(2)}, u32[]{:S(2)}) %collective-permute-start.1) | collective-permute-done | bytes 2592 | tf_op jit(solution)/shard_map/ppermute | solution.py:323
  24.8 0.0 collective-permute-done.2.ha_ref
  24.8 0.0 collective-permute-done.3.hb_ref
  24.8 0.6 %copy-done.3 = f32[64,10]{1,0:T(8,128)} copy-done((f32[64,10]{1,0:T(8,128)}, f32[64,10]{1,0:T(8,128)S(1)}, u32[]{:S(2)}) %copy-start.3) | copy-done | bytes 2584
  25.4 4.1 %shard_map.84 = (f32[10,64,256]{2,1,0:T(8,128)}, f32[64,10]{1,0:T(8,128)}, f32[64,10]{1,0:T(8,128)}, f32[10,256]{1,0:T(8,128)}, f32[10,256]{1,0:T(8,128)}) custom-call(s32[2]{0:T(128)} %bitcast.5, s32[2]{0:T(128)} %pad_add_fusion.flag_ref, f32[10,64,256]{2,1,0:T(8,128)} %get-tuple-element.20.part_ref, f32[64,10]{1,0:T(8,128)} %copy-done.2, ...), custom_call_target="tpu_custom_call" | custom-call | flops 1638400 | bytes 1310720 | tf_op jit(solution)/shard_map/pallas_call | solution.py:280
  29.5 2.3 %collective-permute-start.6 = (f32[10,256]{1,0:T(8,128)}, f32[10,256]{1,0:T(8,128)S(1)}, u32[]{:S(2)}, u32[]{:S(2)}) collective-permute-start(f32[10,256]{1,0:T(8,128)} %get-tuple-element.33), channel_id=1, source_target_pairs={{0,1},{1,0},{2,3},{3,2},{4,5},{5,4},{6,7},{7,6},{8,9},{9,8},{10,11... | collective-permute-start | bytes 30728 | tf_op jit(solution)/shard_map/ppermute | solution.py:324
  31.8 4.4 %collective-permute-start.7 = (f32[10,256]{1,0:T(8,128)}, f32[10,256]{1,0:T(8,128)S(1)}, u32[]{:S(2)}, u32[]{:S(2)}) collective-permute-start(f32[10,256]{1,0:T(8,128)} %get-tuple-element.34), channel_id=1, source_target_pairs={{1,2},{2,1},{3,255},{5,6},{6,5},{7,251},{9,10},{10,9},{11,247},{13... | collective-permute-start | bytes 30728 | tf_op jit(solution)/shard_map/ppermute | solution.py:325
  36.2 4.7 %collective-permute-start.4 = (f32[64,10]{1,0:T(8,128)}, f32[64,10]{1,0:T(8,128)S(1)}, u32[]{:S(2)}, u32[]{:S(2)}) collective-permute-start(f32[64,10]{1,0:T(8,128)} %get-tuple-element.31), channel_id=1, source_target_pairs={{0,252},{4,0},{8,4},{12,8},{16,12},{20,16},{24,20},{28,24},{32,28}... | collective-permute-start | bytes 7688 | tf_op jit(solution)/shard_map/ppermute | solution.py:322
  40.9 0.0 collective-permute-start.5
  40.9 4.4 %shard_map.85.part_ref = f32[10,64,256]{2,1,0:T(8,128)} custom-call(s32[2]{0:T(128)} %si_ref.5, s32[2]{0:T(128)} %bitcast.6, f32[10,10]{1,0:T(8,128)} %lm_ref.3, f32[10,64,256]{2,1,0:T(8,128)} %get-tuple-element.30.adj_ref, f32[64,256]{1,0:T(8,128)} %d_ref.5, f32[4,10,64,256]{3,2,1,0:T(8,128)} %t_ref.3, f32[4,10,64,256]{3,2,1,0:T(8,128)} %u_ref.5, ...), custom_call_target="tpu_custom_call" | custom-call | flops 9830400 | bytes 5242880 | tf_op jit(solution)/shard_map/pallas_call | solution.py:256
  45.3 4.3 %collective-permute-done.5.hw_ref = f32[64,10]{1,0:T(8,128)S(1)} collective-permute-done((f32[64,10]{1,0:T(8,128)}, f32[64,10]{1,0:T(8,128)S(1)}, u32[]{:S(2)}, u32[]{:S(2)}) %collective-permute-start.5) | collective-permute-done | bytes 2592 | tf_op jit(solution)/shard_map/ppermute | solution.py:323
  49.6 0.0 collective-permute-done.6.ha_ref
  49.7 0.6 %copy-done.1 = f32[64,10]{1,0:T(8,128)} copy-done((f32[64,10]{1,0:T(8,128)}, f32[64,10]{1,0:T(8,128)S(1)}, u32[]{:S(2)}) %copy-start.1) | copy-done | bytes 2584
  50.2 0.0 copy-done.4
  50.2 0.6 %copy-done.5 = f32[10,256]{1,0:T(8,128)} copy-done((f32[10,256]{1,0:T(8,128)}, f32[10,256]{1,0:T(8,128)S(1)}, u32[]{:S(2)}) %copy-start.5) | copy-done | bytes 10264
  50.8 2.9 %shard_map.86 = f32[10,64,256]{2,1,0:T(8,128)} custom-call(s32[2]{0:T(128)} %bitcast.7, s32[2]{0:T(128)} %pad_add_fusion.flag_ref, f32[10,64,256]{2,1,0:T(8,128)} %shard_map.85.part_ref, f32[64,10]{1,0:T(8,128)} %copy-done, f32[64,10]{1,0:T(8,128)} %copy-done.1, f32[10,256]{1,0:T(8,128)} %copy-done.4, f32[10,256]{1,0:T(8,128)} %copy-done.5), custom_call_target="tpu_custom_call" | custom-call | flops 1638400 | bytes 1310720 | tf_op jit(solution)/shard_map/pallas_call | solution.py:280
  (14 shorter events, 0.0 us)
Async XLA Ops:
  3.8 21.0 %collective-permute-start.2 = (f32[10,256]{1,0:T(8,128)}, f32[10,256]{1,0:T(8,128)S(1)}, u32[]{:S(2)}, u32[]{:S(2)}) collective-permute-start(f32[10,256]{1,0:T(8,128)} %get-tuple-element.23), channel_id=1, source_target_pairs={{0,1},{1,0},{2,3},{3,2},{4,5},{5,4},{6,7},{7,6},{8,9},{9,8},{10,11... | collective-permute-start | bytes 30728 | tf_op jit(solution)/shard_map/ppermute | solution.py:324
  4.4 20.4 %collective-permute-start.3 = (f32[10,256]{1,0:T(8,128)}, f32[10,256]{1,0:T(8,128)S(1)}, u32[]{:S(2)}, u32[]{:S(2)}) collective-permute-start(f32[10,256]{1,0:T(8,128)} %get-tuple-element.24), channel_id=1, source_target_pairs={{1,2},{2,1},{3,255},{5,6},{6,5},{7,251},{9,10},{10,9},{11,247},{13... | collective-permute-start | bytes 30728 | tf_op jit(solution)/shard_map/ppermute | solution.py:325
  15.9 6.4 %collective-permute-start = (f32[64,10]{1,0:T(8,128)}, f32[64,10]{1,0:T(8,128)S(1)}, u32[]{:S(2)}, u32[]{:S(2)}) collective-permute-start(f32[64,10]{1,0:T(8,128)} %get-tuple-element.21), channel_id=1, source_target_pairs={{0,252},{4,0},{8,4},{12,8},{16,12},{20,16},{24,20},{28,24},{32,28}... | collective-permute-start | bytes 7688 | tf_op jit(solution)/shard_map/ppermute | solution.py:322
  16.0 8.8 %collective-permute-start.1 = (f32[64,10]{1,0:T(8,128)}, f32[64,10]{1,0:T(8,128)S(1)}, u32[]{:S(2)}, u32[]{:S(2)}) collective-permute-start(f32[64,10]{1,0:T(8,128)} %get-tuple-element.22), channel_id=1, source_target_pairs={{0,4},{4,8},{8,12},{12,16},{16,20},{20,24},{24,28},{28,32},{32,36}... | collective-permute-start | bytes 7688 | tf_op jit(solution)/shard_map/ppermute | solution.py:323
  22.3 2.5 %copy-start.2 = (f32[64,10]{1,0:T(8,128)}, f32[64,10]{1,0:T(8,128)S(1)}, u32[]{:S(2)}) copy-start(f32[64,10]{1,0:T(8,128)S(1)} %collective-permute-done.he_ref) | copy-start | bytes 7684
  24.8 0.6 %copy-start.3 = (f32[64,10]{1,0:T(8,128)}, f32[64,10]{1,0:T(8,128)S(1)}, u32[]{:S(2)}) copy-start(f32[64,10]{1,0:T(8,128)S(1)} %collective-permute-done.1.hw_ref) | copy-start | bytes 7684
  24.8 0.6 %copy-start.6 = (f32[10,256]{1,0:T(8,128)}, f32[10,256]{1,0:T(8,128)S(1)}, u32[]{:S(2)}) copy-start(f32[10,256]{1,0:T(8,128)S(1)} %collective-permute-done.2.ha_ref) | copy-start | bytes 30724
  24.8 0.6 %copy-start.7 = (f32[10,256]{1,0:T(8,128)}, f32[10,256]{1,0:T(8,128)S(1)}, u32[]{:S(2)}) copy-start(f32[10,256]{1,0:T(8,128)S(1)} %collective-permute-done.3.hb_ref) | copy-start | bytes 30724
  29.5 20.2 %collective-permute-start.6 = (f32[10,256]{1,0:T(8,128)}, f32[10,256]{1,0:T(8,128)S(1)}, u32[]{:S(2)}, u32[]{:S(2)}) collective-permute-start(f32[10,256]{1,0:T(8,128)} %get-tuple-element.33), channel_id=1, source_target_pairs={{0,1},{1,0},{2,3},{3,2},{4,5},{5,4},{6,7},{7,6},{8,9},{9,8},{10,11... | collective-permute-start | bytes 30728 | tf_op jit(solution)/shard_map/ppermute | solution.py:324
  31.8 17.9 %collective-permute-start.7 = (f32[10,256]{1,0:T(8,128)}, f32[10,256]{1,0:T(8,128)S(1)}, u32[]{:S(2)}, u32[]{:S(2)}) collective-permute-start(f32[10,256]{1,0:T(8,128)} %get-tuple-element.34), channel_id=1, source_target_pairs={{1,2},{2,1},{3,255},{5,6},{6,5},{7,251},{9,10},{10,9},{11,247},{13... | collective-permute-start | bytes 30728 | tf_op jit(solution)/shard_map/ppermute | solution.py:325
  36.2 9.1 %collective-permute-start.4 = (f32[64,10]{1,0:T(8,128)}, f32[64,10]{1,0:T(8,128)S(1)}, u32[]{:S(2)}, u32[]{:S(2)}) collective-permute-start(f32[64,10]{1,0:T(8,128)} %get-tuple-element.31), channel_id=1, source_target_pairs={{0,252},{4,0},{8,4},{12,8},{16,12},{20,16},{24,20},{28,24},{32,28}... | collective-permute-start | bytes 7688 | tf_op jit(solution)/shard_map/ppermute | solution.py:322
  40.9 8.7 %collective-permute-start.5 = (f32[64,10]{1,0:T(8,128)}, f32[64,10]{1,0:T(8,128)S(1)}, u32[]{:S(2)}, u32[]{:S(2)}) collective-permute-start(f32[64,10]{1,0:T(8,128)} %get-tuple-element.32), channel_id=1, source_target_pairs={{0,4},{4,8},{8,12},{12,16},{16,20},{20,24},{24,28},{28,32},{32,36}... | collective-permute-start | bytes 7688 | tf_op jit(solution)/shard_map/ppermute | solution.py:323
  45.3 4.4 %copy-start = (f32[64,10]{1,0:T(8,128)}, f32[64,10]{1,0:T(8,128)S(1)}, u32[]{:S(2)}) copy-start(f32[64,10]{1,0:T(8,128)S(1)} %collective-permute-done.4.he_ref) | copy-start | bytes 7684
  49.6 0.6 %copy-start.1 = (f32[64,10]{1,0:T(8,128)}, f32[64,10]{1,0:T(8,128)S(1)}, u32[]{:S(2)}) copy-start(f32[64,10]{1,0:T(8,128)S(1)} %collective-permute-done.5.hw_ref) | copy-start | bytes 7684
  49.6 0.6 %copy-start.4 = (f32[10,256]{1,0:T(8,128)}, f32[10,256]{1,0:T(8,128)S(1)}, u32[]{:S(2)}) copy-start(f32[10,256]{1,0:T(8,128)S(1)} %collective-permute-done.6.ha_ref) | copy-start | bytes 30724
  50.2 0.6 %copy-start.5 = (f32[10,256]{1,0:T(8,128)}, f32[10,256]{1,0:T(8,128)S(1)}, u32[]{:S(2)}) copy-start(f32[10,256]{1,0:T(8,128)S(1)} %collective-permute-done.7.hb_ref) | copy-start | bytes 30724

commit v5 on v4

--- a/solution.py
+++ b/solution.py
@@ -114,15 +114,25 @@
     )
 
 
-def prologue_kernel(si_ref, wt_ref, flag_ref, af_ref, d_ref, u_ref, v_ref, pe_ref, pw_ref, pa_ref, pb_ref):
-    del si_ref
-    levels, rows, width = af_ref.shape
+def prologue_kernel(k, si_ref, wt_ref, flag_ref, af_hbm, d_ref, u_hbm, v_hbm, pe_ref, pw_ref, pa_ref, pb_ref,
+                    af_buf, u_buf, v_buf, sem):
+    levels, rows, width = af_buf.shape
+    chosen = si_ref[k]
+    copies = []
+    for l in range(levels):
+        for i, (src, dst) in enumerate(((af_hbm.at[l], af_buf.at[l]), (u_hbm.at[chosen, l], u_buf.at[l]),
+                                        (v_hbm.at[chosen, l], v_buf.at[l]))):
+            copy = pltpu.make_async_copy(src, dst, sem.at[i, l])
+            copy.start()
+            copies.append(copy)
     wet = wet_field(wt_ref, rows, width)
     d = d_ref[...]
     out = Collector(levels, rows, width, True)
     for l in range(levels):
-        coef = coefficients(l, d, u_ref[l], v_ref[l], rows, width)
-        out.add(l, *edge_values(*coef, af_ref[l] * wet, rows, width))
+        for copy in copies[3 * l:3 * l + 3]:
+            copy.wait()
+        coef = coefficients(l, d, u_buf[l], v_buf[l], rows, width)
+        out.add(l, *edge_values(*coef, af_buf[l] * wet, rows, width))
     out.finish_pairs(flag_ref, pe_ref, pw_ref, pa_ref, pb_ref)
 
 
@@ -165,42 +175,62 @@
         coef.finish(ce_ref, cw_ref, cn_ref, cs_ref, cf_ref)
 
 
-def fix_kernel(emit, wt_ref, flag_ref, part_ref, he_ref, hw_ref, ha_ref, hb_ref, *rest):
-    if emit:
-        ce_ref, cw_ref, cn_ref, cs_ref, cf_ref, out_ref, pe_ref, pw_ref, pa_ref, pb_ref = rest
+def fix_kernel(emit, n_small, wt_ref, flag_ref, part_hbm, *rest):
+    small_hbm = rest[:n_small]
+    rest = rest[n_small:]
+    if emit:
+        out_hbm, pe_ref, pw_ref, pa_ref, pb_ref = rest[:5]
+        rest = rest[5:]
     else:
-        (out_ref,) = rest
-    levels, rows, width = part_ref.shape
+        out_hbm = rest[0]
+        rest = rest[1:]
+    part_buf, out_buf, in_sem, out_sem = rest
+    small = small_hbm
+    levels, rows, width = part_buf.shape
+
+    in_copies = [pltpu.make_async_copy(part_hbm.at[l], part_buf.at[l], in_sem.at[l]) for l in range(levels)]
+    for c in in_copies:
+        c.start()
+
     wet = wet_field(wt_ref, rows, width)
     wet_left, wet_right = wet[:, :TLON], wet[:, width - TLON:]
     wet_bottom, wet_top = wet[0:1, :], wet[rows - 1:rows, :]
     lane = lax.broadcasted_iota(jnp.int32, (rows, TLON), 1)
+    even = flag_ref[0] == 0
+    he_ref, hw_ref, ha_ref, hb_ref = small[:4]
     he = he_ref[...]
     hw = hw_ref[...]
-    even = flag_ref[0] == 0
-    if emit:
+    if emit:
+        ce_ref, cw_ref, cn_ref, cs_ref, cf_ref = small[4:]
         ce = ce_ref[...]
         cw = cw_ref[...]
         out = Collector(levels, rows, width, True)
+    out_copies = []
     for l in range(levels):
-        x = part_ref[l]
+        in_copies[l].wait()
+        x = part_buf[l]
         east = jnp.where(lane == TLON - 1, jnp.broadcast_to(he[:, l:l + 1], (rows, TLON)), 0.0)
         west = jnp.where(lane == 0, jnp.broadcast_to(hw[:, l:l + 1], (rows, TLON)), 0.0)
-        out_ref[l] = x
-        out_ref[l, :, width - TLON:] = x[:, width - TLON:] + wet_right * east
-        out_ref[l, :, :TLON] = out_ref[l, :, :TLON] + wet_left * west
+        out_buf[l] = x
+        out_buf[l, :, width - TLON:] = x[:, width - TLON:] + wet_right * east
+        out_buf[l, :, :TLON] = out_buf[l, :, :TLON] + wet_left * west
         a_row = ha_ref[l:l + 1, :]
         b_row = hb_ref[l:l + 1, :]
         north_row = jnp.where(even, a_row, b_row)
         south_row = jnp.where(even, b_row, a_row)
-        out_ref[l, rows - 1:rows, :] = out_ref[l, rows - 1:rows, :] + wet_top * north_row
-        out_ref[l, 0:1, :] = out_ref[l, 0:1, :] + wet_bottom * south_row
+        out_buf[l, rows - 1:rows, :] = out_buf[l, rows - 1:rows, :] + wet_top * north_row
+        out_buf[l, 0:1, :] = out_buf[l, 0:1, :] + wet_bottom * south_row
+        copy = pltpu.make_async_copy(out_buf.at[l], out_hbm.at[l], out_sem.at[l])
+        copy.start()
+        out_copies.append(copy)
         if emit:
-            new = out_ref[l]
+            new = out_buf[l]
             coef = (ce[:, l:l + 1], cw[:, l:l + 1], cn_ref[l:l + 1, :], cs_ref[l:l + 1, :], cf_ref[l:l + 1, :])
             out.add(l, *edge_values(*coef, new, rows, width))
     if emit:
         out.finish_pairs(flag_ref, pe_ref, pw_ref, pa_ref, pb_ref)
+    for c in out_copies:
+        c.wait()
 
 
 def payload_shapes(levels, rows, width):
@@ -224,16 +254,18 @@
 def run_prologue(k, si, wt, flags, af, d, zonal, merid):
     levels, rows, width = af.shape
     shapes = pair_shapes(levels, rows, width)
+    anywhere = pl.BlockSpec(memory_space=pl.ANY)
     n = levels * rows * width
     return pl.pallas_call(
-        prologue_kernel,
+        functools.partial(prologue_kernel, k),
         out_shape=shapes,
         grid_spec=pltpu.PrefetchScalarGridSpec(
             num_scalar_prefetch=3,
             grid=(1,),
-            in_specs=[whole(af.shape), whole(d.shape), state_spec(k, levels, rows, width),
-                      state_spec(k, levels, rows, width)],
+            in_specs=[anywhere, whole(d.shape), anywhere, anywhere],
             out_specs=[whole(s.shape) for s in shapes],
+            scratch_shapes=[pltpu.VMEM(af.shape, jnp.float32) for _ in range(3)]
+            + [pltpu.SemaphoreType.DMA((3, levels))],
         ),
         cost_estimate=pl.CostEstimate(flops=2 * n, bytes_accessed=12 * n, transcendentals=0),
     )(si, wt, flags, af, d, zonal, merid)
@@ -271,20 +303,32 @@
 def run_fix(wt, flags, part, halos, coefs):
     levels, rows, width = part.shape
     emit = bool(coefs)
-    args = [wt, flags, part, *halos, *coefs]
-    in_specs = [whole(x.shape) for x in args[2:]]
+    small = [*halos, *coefs]
+    args = [wt, flags, part, *small]
+    anywhere = pl.BlockSpec(memory_space=pl.ANY)
+    in_specs = [anywhere] + [pl.BlockSpec(memory_space=pltpu.VMEM)] * len(small)
     out_shape = [jax.ShapeDtypeStruct(part.shape, jnp.float32)]
-    if emit:
-        out_shape += pair_shapes(levels, rows, width)
+    out_specs = [anywhere]
+    if emit:
+        shapes = pair_shapes(levels, rows, width)
+        out_shape += shapes
+        out_specs += [whole(x.shape) for x in shapes]
+    scratch = [
+        pltpu.VMEM(part.shape, jnp.float32),
+        pltpu.VMEM(part.shape, jnp.float32),
+        pltpu.SemaphoreType.DMA((levels,)),
+        pltpu.SemaphoreType.DMA((levels,)),
+    ]
     n = levels * rows * width
     outs = pl.pallas_call(
-        functools.partial(fix_kernel, emit),
+        functools.partial(fix_kernel, emit, len(small)),
         out_shape=out_shape,
         grid_spec=pltpu.PrefetchScalarGridSpec(
             num_scalar_prefetch=2,
             grid=(1,),
             in_specs=in_specs,
-            out_specs=[whole(s.shape) for s in out_shape],
+            out_specs=out_specs,
+            scratch_shapes=scratch,
         ),
         cost_estimate=pl.CostEstimate(flops=10 * n, bytes_accessed=8 * n, transcendentals=0),
     )(*args)

time: 54 us -> 58.7 us (1.087)
  Pallas kernels: 19.3 us -> 23.5 us
    pallas_call x3, Pallas kernels: 10.1 us -> 14.3 us  [the longest x2 10 us: run_fix(): pl.pallas_call(functools.partial(fix_kernel, emit, len(small)), out_shape...]
  transfers between devices with their start and end apart: 8 -> 8, of which waited for: 2 -> 2; matrix products, arithmetic and copies ran while one was open for 0% -> 0% of each run, Pallas kernels for 17% -> 16%
where the time goes in v5:
time: 58.7 us; the launch traced here: 58.2 us
  starting transfers between devices  25.3 us (43%)
  Pallas kernels  23.5 us (40%)
  waiting for transfers between devices  6.79 us (12%)
  local copies, waits for them, and re-layouts  1.79 us (3%)
  other arithmetic  0.65 us (1%)
    ppermute x2, starting transfers between devices, exchange(): hb = lax.ppermute(pb, ('lon', 'lat'), pairs_b)  15.9 us
    pallas_call x2, Pallas kernels, run_fix(): pl.pallas_call(functools.partial(fix_kernel, emit, len(small)), out_shape...  10 us
    pallas_call x2, Pallas kernels, run_core(): pl.pallas_call(functools.partial(core_kernel, first, emit), out_shape=out...  9.22 us
    ppermute x2, waiting for transfers between devices, exchange(): hw = lax.ppermute(pw, 'lon', to_east)  6.77 us
    ppermute x2, starting transfers between devices, exchange(): he = lax.ppermute(pe, 'lon', to_west)  4.82 us
    pallas_call x1, Pallas kernels, run_prologue(): pl.pallas_call(functools.partial(prologue_kernel, k), out_shape=shapes, g...  4.31 us
    ppermute x2, starting transfers between devices, exchange(): ha = lax.ppermute(pa, 'lat', pairs_a)  3.13 us
    unnamed x16, local copies, waits for them, and re-layouts  1.79 us
  transfers between devices with their start and end apart: 8, of which 2 were waited for; matrix products, arithmetic and copies ran while one was open for 0% of the time, Pallas kernels for 16%

profile of v5, /device:TPU:3, one launch (start us, length us, event | category | flops | bytes accessed | tf_op | source)
XLA Modules:
  0.0 58.2 jit_solution(639220891545580225)
XLA Ops:
  0.0 0.7 %pad_add_fusion.flag_ref = s32[2]{0:T(128)} fusion(s32[1]{0:T(128)} %bitcast.2, s32[1]{0:T(128)} %bitcast.1), kind=kLoop, calls=%fused_computation | loop fusion | flops 2 | bytes 16 | tf_op jit(solution)/shard_map/stack | solution.py:352
  0.7 4.3 %shard_map.83 = (f32[64,10]{1,0:T(8,128)}, f32[64,10]{1,0:T(8,128)}, f32[10,256]{1,0:T(8,128)}, f32[10,256]{1,0:T(8,128)}) custom-call(s32[2]{0:T(128)} %si_ref.5, s32[2]{0:T(128)} %bitcast.3, s32[2]{0:T(128)} %pad_add_fusion.flag_ref, f32[10,64,256]{2,1,0:T(8,128)} %af_hbm.1, f32[64,256]{1,0:T(8,128)} %d_ref.5, f32[4,10,64,256]{3,2,1,0:T(8,128)} %u_ref.3, ...), custom_call_target="tpu_custom_call" | custom-call | flops 327680 | bytes 1966080 | tf_op jit(solution)/shard_map/pallas_call | solution.py:259
  5.0 0.8 %collective-permute-start.2 = (f32[10,256]{1,0:T(8,128)}, f32[10,256]{1,0:T(8,128)S(1)}, u32[]{:S(2)}, u32[]{:S(2)}) collective-permute-start(f32[10,256]{1,0:T(8,128)} %get-tuple-element.23), channel_id=1, source_target_pairs={{0,1},{1,0},{2,3},{3,2},{4,5},{5,4},{6,7},{7,6},{8,9},{9,8},{10,11... | collective-permute-start | bytes 30728 | tf_op jit(solution)/shard_map/ppermute | solution.py:368
  5.7 11.5 %collective-permute-start.3 = (f32[10,256]{1,0:T(8,128)}, f32[10,256]{1,0:T(8,128)S(1)}, u32[]{:S(2)}, u32[]{:S(2)}) collective-permute-start(f32[10,256]{1,0:T(8,128)} %get-tuple-element.24), channel_id=1, source_target_pairs={{1,2},{2,1},{3,255},{5,6},{6,5},{7,251},{9,10},{10,9},{11,247},{13... | collective-permute-start | bytes 30728 | tf_op jit(solution)/shard_map/ppermute | solution.py:369
  17.2 0.1 collective-permute-start
  17.3 1.5 %collective-permute-start.1 = (f32[64,10]{1,0:T(8,128)}, f32[64,10]{1,0:T(8,128)S(1)}, u32[]{:S(2)}, u32[]{:S(2)}) collective-permute-start(f32[64,10]{1,0:T(8,128)} %get-tuple-element.22), channel_id=1, source_target_pairs={{0,4},{4,8},{8,12},{12,16},{16,20},{20,24},{24,28},{28,32},{32,36}... | collective-permute-start | bytes 7688 | tf_op jit(solution)/shard_map/ppermute | solution.py:367
  18.8 4.9 %shard_map.82 = (f32[10,64,256]{2,1,0:T(8,128)}, f32[64,10]{1,0:T(8,128)}, f32[64,10]{1,0:T(8,128)}, f32[10,256]{1,0:T(8,128)}, f32[10,256]{1,0:T(8,128)}, /*index=5*/f32[10,256]{1,0:T(8,128)}) custom-call(s32[2]{0:T(128)} %si_ref.5, s32[2]{0:T(128)} %bitcast.4, f32[10,10]{1,0:T(8,128)} %lm_ref.3, f32[10,64,256]{2,1,0:T(8,128)} %af_hbm.1, f32[64,256]{1,0:T(8,128)} %d_ref.5, ...), custom_call_target="tpu_custom_call" | custom-call | flops 9830400 | bytes 5242880 | tf_op jit(solution)/shard_map/pallas_call | solution.py:288
  23.6 0.0 collective-permute-done.rest_0_
  23.7 2.4 %collective-permute-done.1.rest_1_ = f32[64,10]{1,0:T(8,128)S(1)} collective-permute-done((f32[64,10]{1,0:T(8,128)}, f32[64,10]{1,0:T(8,128)S(1)}, u32[]{:S(2)}, u32[]{:S(2)}) %collective-permute-start.1) | collective-permute-done | bytes 2592 | tf_op jit(solution)/shard_map/ppermute | solution.py:367
  26.1 0.0 collective-permute-done.3.rest_3_
  26.1 0.6 copy-done.3
  26.7 6.0 %shard_map.84 = (f32[10,64,256]{2,1,0:T(8,128)}, f32[64,10]{1,0:T(8,128)}, f32[64,10]{1,0:T(8,128)}, f32[10,256]{1,0:T(8,128)}, f32[10,256]{1,0:T(8,128)}) custom-call(s32[2]{0:T(128)} %bitcast.5, s32[2]{0:T(128)} %pad_add_fusion.flag_ref, f32[10,64,256]{2,1,0:T(8,128)} %get-tuple-element.20.part_hbm, f32[64,10]{1,0:T(8,128)} %copy-done.2, ...), custom_call_target="tpu_custom_call" | custom-call | flops 1638400 | bytes 1310720 | tf_op jit(solution)/shard_map/pallas_call | solution.py:323
  32.7 2.4 %collective-permute-start.6 = (f32[10,256]{1,0:T(8,128)}, f32[10,256]{1,0:T(8,128)S(1)}, u32[]{:S(2)}, u32[]{:S(2)}) collective-permute-start(f32[10,256]{1,0:T(8,128)} %get-tuple-element.33), channel_id=1, source_target_pairs={{0,1},{1,0},{2,3},{3,2},{4,5},{5,4},{6,7},{7,6},{8,9},{9,8},{10,11... | collective-permute-start | bytes 30728 | tf_op jit(solution)/shard_map/ppermute | solution.py:368
  35.1 4.4 %collective-permute-start.7 = (f32[10,256]{1,0:T(8,128)}, f32[10,256]{1,0:T(8,128)S(1)}, u32[]{:S(2)}, u32[]{:S(2)}) collective-permute-start(f32[10,256]{1,0:T(8,128)} %get-tuple-element.34), channel_id=1, source_target_pairs={{1,2},{2,1},{3,255},{5,6},{6,5},{7,251},{9,10},{10,9},{11,247},{13... | collective-permute-start | bytes 30728 | tf_op jit(solution)/shard_map/ppermute | solution.py:369
  39.5 4.7 %collective-permute-start.4 = (f32[64,10]{1,0:T(8,128)}, f32[64,10]{1,0:T(8,128)S(1)}, u32[]{:S(2)}, u32[]{:S(2)}) collective-permute-start(f32[64,10]{1,0:T(8,128)} %get-tuple-element.31), channel_id=1, source_target_pairs={{0,252},{4,0},{8,4},{12,8},{16,12},{20,16},{24,20},{28,24},{32,28}... | collective-permute-start | bytes 7688 | tf_op jit(solution)/shard_map/ppermute | solution.py:366
  44.3 0.0 collective-permute-start.5
  44.3 4.4 %shard_map.85.part_hbm = f32[10,64,256]{2,1,0:T(8,128)} custom-call(s32[2]{0:T(128)} %si_ref.5, s32[2]{0:T(128)} %bitcast.6, f32[10,10]{1,0:T(8,128)} %lm_ref.3, f32[10,64,256]{2,1,0:T(8,128)} %get-tuple-element.30.adj_ref, f32[64,256]{1,0:T(8,128)} %d_ref.5, f32[4,10,64,256]{3,2,1,0:T(8,128)} %t_ref.3, f32[4,10,64,256]{3,2,1,0:T(8,128)} %u_ref.3, ...), custom_call_target="tpu_custom_call" | custom-call | flops 9830400 | bytes 5242880 | tf_op jit(solution)/shard_map/pallas_call | solution.py:288
  48.6 4.3 %collective-permute-done.5.rest_1_ = f32[64,10]{1,0:T(8,128)S(1)} collective-permute-done((f32[64,10]{1,0:T(8,128)}, f32[64,10]{1,0:T(8,128)S(1)}, u32[]{:S(2)}, u32[]{:S(2)}) %collective-permute-start.5) | collective-permute-done | bytes 2592 | tf_op jit(solution)/shard_map/ppermute | solution.py:367
  53.0 0.0 collective-permute-done.6.rest_2_
  53.0 0.0 collective-permute-done.7.rest_3_
  53.0 0.6 %copy-done.1 = f32[64,10]{1,0:T(8,128)} copy-done((f32[64,10]{1,0:T(8,128)}, f32[64,10]{1,0:T(8,128)S(1)}, u32[]{:S(2)}) %copy-start.1) | copy-done | bytes 2584
  53.6 0.0 copy-done.4
  53.6 0.6 %copy-done.5 = f32[10,256]{1,0:T(8,128)} copy-done((f32[10,256]{1,0:T(8,128)}, f32[10,256]{1,0:T(8,128)S(1)}, u32[]{:S(2)}) %copy-start.5) | copy-done | bytes 10264
  54.2 4.0 %shard_map.86 = f32[10,64,256]{2,1,0:T(8,128)} custom-call(s32[2]{0:T(128)} %bitcast.7, s32[2]{0:T(128)} %pad_add_fusion.flag_ref, f32[10,64,256]{2,1,0:T(8,128)} %shard_map.85.part_hbm, f32[64,10]{1,0:T(8,128)} %copy-done, f32[64,10]{1,0:T(8,128)} %copy-done.1, f32[10,256]{1,0:T(8,128)} %copy-done.4, f32[10,256]{1,0:T(8,128)} %copy-done.5), custom_call_target="tpu_custom_call" | custom-call | flops 1638400 | bytes 1310720 | tf_op jit(solution)/shard_map/pallas_call | solution.py:323
  (14 shorter events, 0.0 us)
Async XLA Ops:
  5.0 21.1 %collective-permute-start.2 = (f32[10,256]{1,0:T(8,128)}, f32[10,256]{1,0:T(8,128)S(1)}, u32[]{:S(2)}, u32[]{:S(2)}) collective-permute-start(f32[10,256]{1,0:T(8,128)} %get-tuple-element.23), channel_id=1, source_target_pairs={{0,1},{1,0},{2,3},{3,2},{4,5},{5,4},{6,7},{7,6},{8,9},{9,8},{10,11... | collective-permute-start | bytes 30728 | tf_op jit(solution)/shard_map/ppermute | solution.py:368
  5.7 20.4 %collective-permute-start.3 = (f32[10,256]{1,0:T(8,128)}, f32[10,256]{1,0:T(8,128)S(1)}, u32[]{:S(2)}, u32[]{:S(2)}) collective-permute-start(f32[10,256]{1,0:T(8,128)} %get-tuple-element.24), channel_id=1, source_target_pairs={{1,2},{2,1},{3,255},{5,6},{6,5},{7,251},{9,10},{10,9},{11,247},{13... | collective-permute-start | bytes 30728 | tf_op jit(solution)/shard_map/ppermute | solution.py:369
  17.2 6.4 %collective-permute-start = (f32[64,10]{1,0:T(8,128)}, f32[64,10]{1,0:T(8,128)S(1)}, u32[]{:S(2)}, u32[]{:S(2)}) collective-permute-start(f32[64,10]{1,0:T(8,128)} %get-tuple-element.21), channel_id=1, source_target_pairs={{0,252},{4,0},{8,4},{12,8},{16,12},{20,16},{24,20},{28,24},{32,28}... | collective-permute-start | bytes 7688 | tf_op jit(solution)/shard_map/ppermute | solution.py:366
  17.3 8.8 %collective-permute-start.1 = (f32[64,10]{1,0:T(8,128)}, f32[64,10]{1,0:T(8,128)S(1)}, u32[]{:S(2)}, u32[]{:S(2)}) collective-permute-start(f32[64,10]{1,0:T(8,128)} %get-tuple-element.22), channel_id=1, source_target_pairs={{0,4},{4,8},{8,12},{12,16},{16,20},{20,24},{24,28},{28,32},{32,36}... | collective-permute-start | bytes 7688 | tf_op jit(solution)/shard_map/ppermute | solution.py:367
  23.6 2.5 %copy-start.2 = (f32[64,10]{1,0:T(8,128)}, f32[64,10]{1,0:T(8,128)S(1)}, u32[]{:S(2)}) copy-start(f32[64,10]{1,0:T(8,128)S(1)} %collective-permute-done.rest_0_) | copy-start | bytes 7684
  26.1 0.6 %copy-start.3 = (f32[64,10]{1,0:T(8,128)}, f32[64,10]{1,0:T(8,128)S(1)}, u32[]{:S(2)}) copy-start(f32[64,10]{1,0:T(8,128)S(1)} %collective-permute-done.1.rest_1_) | copy-start | bytes 7684
  26.1 0.6 %copy-start.6 = (f32[10,256]{1,0:T(8,128)}, f32[10,256]{1,0:T(8,128)S(1)}, u32[]{:S(2)}) copy-start(f32[10,256]{1,0:T(8,128)S(1)} %collective-permute-done.2.rest_2_) | copy-start | bytes 30724
  26.1 0.6 %copy-start.7 = (f32[10,256]{1,0:T(8,128)}, f32[10,256]{1,0:T(8,128)S(1)}, u32[]{:S(2)}) copy-start(f32[10,256]{1,0:T(8,128)S(1)} %collective-permute-done.3.rest_3_) | copy-start | bytes 30724
  32.7 20.2 %collective-permute-start.6 = (f32[10,256]{1,0:T(8,128)}, f32[10,256]{1,0:T(8,128)S(1)}, u32[]{:S(2)}, u32[]{:S(2)}) collective-permute-start(f32[10,256]{1,0:T(8,128)} %get-tuple-element.33), channel_id=1, source_target_pairs={{0,1},{1,0},{2,3},{3,2},{4,5},{5,4},{6,7},{7,6},{8,9},{9,8},{10,11... | collective-permute-start | bytes 30728 | tf_op jit(solution)/shard_map/ppermute | solution.py:368
  35.1 17.9 %collective-permute-start.7 = (f32[10,256]{1,0:T(8,128)}, f32[10,256]{1,0:T(8,128)S(1)}, u32[]{:S(2)}, u32[]{:S(2)}) collective-permute-start(f32[10,256]{1,0:T(8,128)} %get-tuple-element.34), channel_id=1, source_target_pairs={{1,2},{2,1},{3,255},{5,6},{6,5},{7,251},{9,10},{10,9},{11,247},{13... | collective-permute-start | bytes 30728 | tf_op jit(solution)/shard_map/ppermute | solution.py:369
  39.5 9.1 %collective-permute-start.4 = (f32[64,10]{1,0:T(8,128)}, f32[64,10]{1,0:T(8,128)S(1)}, u32[]{:S(2)}, u32[]{:S(2)}) collective-permute-start(f32[64,10]{1,0:T(8,128)} %get-tuple-element.31), channel_id=1, source_target_pairs={{0,252},{4,0},{8,4},{12,8},{16,12},{20,16},{24,20},{28,24},{32,28}... | collective-permute-start | bytes 7688 | tf_op jit(solution)/shard_map/ppermute | solution.py:366
  44.3 8.7 %collective-permute-start.5 = (f32[64,10]{1,0:T(8,128)}, f32[64,10]{1,0:T(8,128)S(1)}, u32[]{:S(2)}, u32[]{:S(2)}) collective-permute-start(f32[64,10]{1,0:T(8,128)} %get-tuple-element.32), channel_id=1, source_target_pairs={{0,4},{4,8},{8,12},{12,16},{16,20},{20,24},{24,28},{28,32},{32,36}... | collective-permute-start | bytes 7688 | tf_op jit(solution)/shard_map/ppermute | solution.py:367
  48.6 4.4 %copy-start = (f32[64,10]{1,0:T(8,128)}, f32[64,10]{1,0:T(8,128)S(1)}, u32[]{:S(2)}) copy-start(f32[64,10]{1,0:T(8,128)S(1)} %collective-permute-done.4.rest_0_) | copy-start | bytes 7684
  53.0 0.6 %copy-start.1 = (f32[64,10]{1,0:T(8,128)}, f32[64,10]{1,0:T(8,128)S(1)}, u32[]{:S(2)}) copy-start(f32[64,10]{1,0:T(8,128)S(1)} %collective-permute-done.5.rest_1_) | copy-start | bytes 7684
  53.0 0.6 %copy-start.4 = (f32[10,256]{1,0:T(8,128)}, f32[10,256]{1,0:T(8,128)S(1)}, u32[]{:S(2)}) copy-start(f32[10,256]{1,0:T(8,128)S(1)} %collective-permute-done.6.rest_2_) | copy-start | bytes 30724
  53.6 0.6 %copy-start.5 = (f32[10,256]{1,0:T(8,128)}, f32[10,256]{1,0:T(8,128)S(1)}, u32[]{:S(2)}) copy-start(f32[10,256]{1,0:T(8,128)S(1)} %collective-permute-done.7.rest_3_) | copy-start | bytes 30724

commit v6 on v4

--- a/solution.py
+++ b/solution.py
@@ -291,6 +291,24 @@
     return outs[0], outs[1:]
 
 
+def fix_in_xla(wet_tiles, lat_index, part, halos):
+    levels, rows, width = part.shape
+    he, hw, ha, hb = halos
+    even = lat_index % 2 == 0
+    north = jnp.where(even, ha, hb)
+    south = jnp.where(even, hb, ha)
+    wet = jnp.repeat(wet_tiles.reshape(-1), TLON).astype(jnp.float32)
+    g = lax.broadcasted_iota(jnp.int32, part.shape, 2)
+    r = lax.broadcasted_iota(jnp.int32, part.shape, 1)
+    corr = (
+        jnp.where(g == width - 1, he.T[:, :, None], 0.0)
+        + jnp.where(g == 0, hw.T[:, :, None], 0.0)
+        + jnp.where(r == rows - 1, north[:, None, :], 0.0)
+        + jnp.where(r == 0, south[:, None, :], 0.0)
+    )
+    return part + wet * corr
+
+
 def shards(
     adjoint_final,
     stored_tracer,
@@ -334,7 +352,10 @@
         halos = exchange(payloads)
         part, coefs = run_core(k, k_next, state_index, wt, level_mixing, adj, diffusivity,
                                stored_tracer, stored_zonal, stored_meridional)
-        adj, payloads = run_fix(wt, flags, part, halos, coefs)
+        if coefs:
+            adj, payloads = run_fix(wt, flags, part, halos, coefs)
+        else:
+            adj = fix_in_xla(wet_tiles, lat_index, part, halos)
     return adj
 
 

time: 54 us -> 53.3 us (0.987)
  starting transfers between devices: 25.1 us -> 32.5 us
  waiting for transfers between devices: 6.79 us -> 0.02 us
  Pallas kernels: 19.3 us -> 16.5 us
  other arithmetic: 0.65 us -> 2.9 us
  local copies, waits for them, and re-layouts: 1.79 us -> 0.82 us
    ppermute x2, starting transfers between devices: 4.82 us -> 16.8 us  [exchange(): he = lax.ppermute(pe, 'lon', to_west)]
    ppermute x2, waiting for transfers between devices: 6.77 us -> 0.01 us  [exchange(): hw = lax.ppermute(pw, 'lon', to_east)]
    pallas_call x2 -> x1, Pallas kernels: 6.98 us -> 4.09 us  [run_fix(): pl.pallas_call(functools.partial(fix_kernel, emit), out_shape=out_shape,...]
    add x0 -> x1, other arithmetic: none -> 2.21 us  [fix_in_xla(): return part + wet * corr]
    ppermute x2, starting transfers between devices: 2.96 us -> 0.96 us  [exchange(): ha = lax.ppermute(pa, 'lat', pairs_a)]
    ppermute x2, starting transfers between devices: 1.46 us -> 0.09 us  [exchange(): hw = lax.ppermute(pw, 'lon', to_east)]
    unnamed x16 -> x10, local copies, waits for them, and re-layouts: 1.79 us -> 0.6 us
    ppermute x2, starting transfers between devices: 15.9 us -> 14.7 us  [exchange(): hb = lax.ppermute(pb, ('lon', 'lat'), pairs_b)]
  transfers between devices with their start and end apart: 8 -> 8, of which waited for: 2 -> 0; matrix products, arithmetic and copies ran while one was open for 0% -> 0% of each run, Pallas kernels for 17% -> 17%
where the time goes in v6:
time: 53.3 us; the launch traced here: 53 us
  starting transfers between devices  32.5 us (61%)
  Pallas kernels  16.5 us (31%)
  other arithmetic  2.9 us (5%)
  local copies, waits for them, and re-layouts  0.82 us (2%)
    ppermute x2, starting transfers between devices, exchange(): he = lax.ppermute(pe, 'lon', to_west)  16.8 us
    ppermute x2, starting transfers between devices, exchange(): hb = lax.ppermute(pb, ('lon', 'lat'), pairs_b)  14.7 us
    pallas_call x2, Pallas kernels, run_core(): pl.pallas_call(functools.partial(core_kernel, first, emit), out_shape=out...  9.2 us
    pallas_call x1, Pallas kernels, run_fix(): pl.pallas_call(functools.partial(fix_kernel, emit), out_shape=out_shape,...  4.09 us
    pallas_call x1, Pallas kernels, run_prologue(): pl.pallas_call(prologue_kernel, out_shape=shapes, grid_spec=pltpu.Prefetc...  3.25 us
    add x1, other arithmetic, fix_in_xla(): return part + wet * corr  2.21 us
  transfers between devices with their start and end apart: 8, of which 0 were waited for; matrix products, arithmetic and copies ran while one was open for 0% of the time, Pallas kernels for 17%

profile of v6, /device:TPU:3, one launch (start us, length us, event | category | flops | bytes accessed | tf_op | source)
XLA Modules:
  0.0 53.0 jit_solution(10312058135411222103)
XLA Ops:
  0.0 0.7 %pad_add_fusion.flag_ref = s32[2]{0:T(128)} fusion(s32[1]{0:T(128)} %bitcast.2, s32[1]{0:T(128)} %bitcast.1), kind=kLoop, calls=%fused_computation.5 | loop fusion | flops 2 | bytes 16 | tf_op jit(solution)/shard_map/stack | solution.py:326
  0.7 3.2 %shard_map.83 = (f32[64,10]{1,0:T(8,128)}, f32[64,10]{1,0:T(8,128)}, f32[10,256]{1,0:T(8,128)}, f32[10,256]{1,0:T(8,128)}) custom-call(s32[2]{0:T(128)} %si_ref.5, s32[2]{0:T(128)} %bitcast.10, s32[2]{0:T(128)} %pad_add_fusion.flag_ref, f32[10,64,256]{2,1,0:T(8,128)} %af_ref.1, f32[64,256]{1,0:T(8,128)} %d_ref.5, f32[4,10,64,256]{3,2,1,0:T(8,128)} %u_ref.5, ...), custom_call_target="tpu_custom_call" | custom-call | flops 327680 | bytes 1966080 | tf_op jit(solution)/shard_map/pallas_call | solution.py:228
  3.9 9.6 %collective-permute-start = (f32[64,10]{1,0:T(8,128)}, f32[64,10]{1,0:T(8,128)S(1)}, u32[]{:S(2)}, u32[]{:S(2)}) collective-permute-start(f32[64,10]{1,0:T(8,128)} %get-tuple-element.21), channel_id=1, source_target_pairs={{0,252},{4,0},{8,4},{12,8},{16,12},{20,16},{24,20},{28,24},{32,28}... | collective-permute-start | bytes 7688 | tf_op jit(solution)/shard_map/ppermute | solution.py:340
  13.5 1.0 %collective-permute-start.2 = (f32[10,256]{1,0:T(8,128)}, f32[10,256]{1,0:T(8,128)S(1)}, u32[]{:S(2)}, u32[]{:S(2)}) collective-permute-start(f32[10,256]{1,0:T(8,128)} %get-tuple-element.23), channel_id=1, source_target_pairs={{0,1},{1,0},{2,3},{3,2},{4,5},{5,4},{6,7},{7,6},{8,9},{9,8},{10,11... | collective-permute-start | bytes 30728 | tf_op jit(solution)/shard_map/ppermute | solution.py:342
  14.5 9.4 %collective-permute-start.3 = (f32[10,256]{1,0:T(8,128)}, f32[10,256]{1,0:T(8,128)S(1)}, u32[]{:S(2)}, u32[]{:S(2)}) collective-permute-start(f32[10,256]{1,0:T(8,128)} %get-tuple-element.24), channel_id=1, source_target_pairs={{1,2},{2,1},{3,255},{5,6},{6,5},{7,251},{9,10},{10,9},{11,247},{13... | collective-permute-start | bytes 30728 | tf_op jit(solution)/shard_map/ppermute | solution.py:343
  23.9 0.1 broadcast_bitcast_fusion
  23.9 4.9 %shard_map.82 = (f32[10,64,256]{2,1,0:T(8,128)}, f32[64,10]{1,0:T(8,128)}, f32[64,10]{1,0:T(8,128)}, f32[10,256]{1,0:T(8,128)}, f32[10,256]{1,0:T(8,128)}, /*index=5*/f32[10,256]{1,0:T(8,128)}) custom-call(s32[2]{0:T(128)} %si_ref.5, s32[2]{0:T(128)} %bitcast.11, f32[10,10]{1,0:T(8,128)} %lm_ref.3, f32[10,64,256]{2,1,0:T(8,128)} %af_ref.1, f32[64,256]{1,0:T(8,128)} %d_ref.5, ...), custom_call_target="tpu_custom_call" | custom-call | flops 9830400 | bytes 5242880 | tf_op jit(solution)/shard_map/pallas_call | solution.py:256
  28.8 0.0 collective-permute-done.he_ref
  28.8 0.0 collective-permute-done.1.hw_ref
  28.8 0.0 collective-permute-done.2.ha_ref
  28.9 0.5 %copy-done = f32[64,10]{1,0:T(8,128)} copy-done((f32[64,10]{1,0:T(8,128)}, f32[64,10]{1,0:T(8,128)S(1)}, u32[]{:S(2)}) %copy-start) | copy-done | bytes 2584
  29.4 0.0 copy-done.1
  29.4 0.0 copy-done.2
  29.4 0.0 copy-done.3
  29.5 4.1 %shard_map.84 = (f32[10,64,256]{2,1,0:T(8,128)}, f32[64,10]{1,0:T(8,128)}, f32[64,10]{1,0:T(8,128)}, f32[10,256]{1,0:T(8,128)}, f32[10,256]{1,0:T(8,128)}) custom-call(s32[2]{0:T(128)} %bitcast.12, s32[2]{0:T(128)} %pad_add_fusion.flag_ref, f32[10,64,256]{2,1,0:T(8,128)} %get-tuple-element.20.part_ref, f32[64,10]{1,0:T(8,128)} %copy-done, ...), custom_call_target="tpu_custom_call" | custom-call | flops 1638400 | bytes 1310720 | tf_op jit(solution)/shard_map/pallas_call | solution.py:280
  33.6 0.0 collective-permute-start.6
  33.6 5.4 %collective-permute-start.7 = (f32[10,256]{1,0:T(8,128)}, f32[10,256]{1,0:T(8,128)S(1)}, u32[]{:S(2)}, u32[]{:S(2)}) collective-permute-start(f32[10,256]{1,0:T(8,128)} %get-tuple-element.34), channel_id=1, source_target_pairs={{1,2},{2,1},{3,255},{5,6},{6,5},{7,251},{9,10},{10,9},{11,247},{13... | collective-permute-start | bytes 30728 | tf_op jit(solution)/shard_map/ppermute | solution.py:343
  38.9 0.1 collective-permute-start.5
  39.0 7.2 %collective-permute-start.4 = (f32[64,10]{1,0:T(8,128)}, f32[64,10]{1,0:T(8,128)S(1)}, u32[]{:S(2)}, u32[]{:S(2)}) collective-permute-start(f32[64,10]{1,0:T(8,128)} %get-tuple-element.31), channel_id=1, source_target_pairs={{0,252},{4,0},{8,4},{12,8},{16,12},{20,16},{24,20},{28,24},{32,28}... | collective-permute-start | bytes 7688 | tf_op jit(solution)/shard_map/ppermute | solution.py:340
  46.2 4.3 %shard_map.85 = f32[10,64,256]{2,1,0:T(8,128)} custom-call(s32[2]{0:T(128)} %si_ref.5, s32[2]{0:T(128)} %bitcast.13, f32[10,10]{1,0:T(8,128)} %lm_ref.3, f32[10,64,256]{2,1,0:T(8,128)} %get-tuple-element.30.adj_ref, f32[64,256]{1,0:T(8,128)} %d_ref.5, f32[4,10,64,256]{3,2,1,0:T(8,128)} %t_ref.3, f32[4,10,64,256]{3,2,1,0:T(8,128)} %u_ref.5, ...), custom_call_target="tpu_custom_call" | custom-call | flops 9830400 | bytes 5242880 | tf_op jit(solution)/shard_map/pallas_call | solution.py:256
  50.6 0.1 copy.10
  50.6 0.1 copy.9
  50.7 0.0 collective-permute-done.7
  50.7 2.2 %multiply_add_fusion = f32[10,64,256]{2,1,0:T(8,128)} fusion(f32[10,64,256]{2,1,0:T(8,128)} %shard_map.85, f32[10,256]{1,0:T(8,128)S(1)} %get-tuple-element.36, f32[10,256]{1,0:T(8,128)S(1)} %get-tuple-element.35, f32[10,64]{1,0:T(8,128)S(1)} %copy.10, f32[10,64]{1,0:T(8,128)S(1)} %copy.9, f32[256]{0:T(256)S(1)} %broadcast_bitcast_fusion, ...), kind=kLoop, calls=%fused_computation | loop fusion | flops 1474560 | bytes 1337984 | tf_op jit(solution)/shard_map/add | solution.py:309
  (15 shorter events, 0.0 us)
Async XLA Ops:
  0.7 23.2 %copy-start.4 = (s32[1,2]{1,0:T(1,128)S(1)}, s32[1,2]{1,0:T(1,128)}, u32[]{:S(2)}) copy-start(s32[1,2]{1,0:T(1,128)} %param.14) | copy-start | bytes 28
  3.9 24.9 %collective-permute-start = (f32[64,10]{1,0:T(8,128)}, f32[64,10]{1,0:T(8,128)S(1)}, u32[]{:S(2)}, u32[]{:S(2)}) collective-permute-start(f32[64,10]{1,0:T(8,128)} %get-tuple-element.21), channel_id=1, source_target_pairs={{0,252},{4,0},{8,4},{12,8},{16,12},{20,16},{24,20},{28,24},{32,28}... | collective-permute-start | bytes 7688 | tf_op jit(solution)/shard_map/ppermute | solution.py:340
  13.5 15.3 %collective-permute-start.1 = (f32[64,10]{1,0:T(8,128)}, f32[64,10]{1,0:T(8,128)S(1)}, u32[]{:S(2)}, u32[]{:S(2)}) collective-permute-start(f32[64,10]{1,0:T(8,128)} %get-tuple-element.22), channel_id=1, source_target_pairs={{0,4},{4,8},{8,12},{12,16},{16,20},{20,24},{24,28},{28,32},{32,36}... | collective-permute-start | bytes 7688 | tf_op jit(solution)/shard_map/ppermute | solution.py:341
  13.5 15.3 %collective-permute-start.2 = (f32[10,256]{1,0:T(8,128)}, f32[10,256]{1,0:T(8,128)S(1)}, u32[]{:S(2)}, u32[]{:S(2)}) collective-permute-start(f32[10,256]{1,0:T(8,128)} %get-tuple-element.23), channel_id=1, source_target_pairs={{0,1},{1,0},{2,3},{3,2},{4,5},{5,4},{6,7},{7,6},{8,9},{9,8},{10,11... | collective-permute-start | bytes 30728 | tf_op jit(solution)/shard_map/ppermute | solution.py:342
  14.5 14.4 %collective-permute-start.3 = (f32[10,256]{1,0:T(8,128)}, f32[10,256]{1,0:T(8,128)S(1)}, u32[]{:S(2)}, u32[]{:S(2)}) collective-permute-start(f32[10,256]{1,0:T(8,128)} %get-tuple-element.24), channel_id=1, source_target_pairs={{1,2},{2,1},{3,255},{5,6},{6,5},{7,251},{9,10},{10,9},{11,247},{13... | collective-permute-start | bytes 30728 | tf_op jit(solution)/shard_map/ppermute | solution.py:343
  28.8 0.6 %copy-start = (f32[64,10]{1,0:T(8,128)}, f32[64,10]{1,0:T(8,128)S(1)}, u32[]{:S(2)}) copy-start(f32[64,10]{1,0:T(8,128)S(1)} %collective-permute-done.he_ref) | copy-start | bytes 7684
  28.8 0.6 %copy-start.1 = (f32[64,10]{1,0:T(8,128)}, f32[64,10]{1,0:T(8,128)S(1)}, u32[]{:S(2)}) copy-start(f32[64,10]{1,0:T(8,128)S(1)} %collective-permute-done.1.hw_ref) | copy-start | bytes 7684
  28.9 0.6 %copy-start.2 = (f32[10,256]{1,0:T(8,128)}, f32[10,256]{1,0:T(8,128)S(1)}, u32[]{:S(2)}) copy-start(f32[10,256]{1,0:T(8,128)S(1)} %collective-permute-done.2.ha_ref) | copy-start | bytes 30724
  28.9 0.6 %copy-start.3 = (f32[10,256]{1,0:T(8,128)}, f32[10,256]{1,0:T(8,128)S(1)}, u32[]{:S(2)}) copy-start(f32[10,256]{1,0:T(8,128)S(1)} %collective-permute-done.3.hb_ref) | copy-start | bytes 30724
  33.6 17.2 %collective-permute-start.6 = (f32[10,256]{1,0:T(8,128)}, f32[10,256]{1,0:T(8,128)S(1)}, u32[]{:S(2)}, u32[]{:S(2)}) collective-permute-start(f32[10,256]{1,0:T(8,128)} %get-tuple-element.33), channel_id=1, source_target_pairs={{0,1},{1,0},{2,3},{3,2},{4,5},{5,4},{6,7},{7,6},{8,9},{9,8},{10,11... | collective-permute-start | bytes 30728 | tf_op jit(solution)/shard_map/ppermute | solution.py:342
  33.6 17.2 %collective-permute-start.7 = (f32[10,256]{1,0:T(8,128)}, f32[10,256]{1,0:T(8,128)S(1)}, u32[]{:S(2)}, u32[]{:S(2)}) collective-permute-start(f32[10,256]{1,0:T(8,128)} %get-tuple-element.34), channel_id=1, source_target_pairs={{1,2},{2,1},{3,255},{5,6},{6,5},{7,251},{9,10},{10,9},{11,247},{13... | collective-permute-start | bytes 30728 | tf_op jit(solution)/shard_map/ppermute | solution.py:343
  38.9 11.6 %collective-permute-start.5 = (f32[64,10]{1,0:T(8,128)}, f32[64,10]{1,0:T(8,128)S(1)}, u32[]{:S(2)}, u32[]{:S(2)}) collective-permute-start(f32[64,10]{1,0:T(8,128)} %get-tuple-element.32), channel_id=1, source_target_pairs={{0,4},{4,8},{8,12},{12,16},{16,20},{20,24},{24,28},{28,32},{32,36}... | collective-permute-start | bytes 7688 | tf_op jit(solution)/shard_map/ppermute | solution.py:341
  39.0 11.6 %collective-permute-start.4 = (f32[64,10]{1,0:T(8,128)}, f32[64,10]{1,0:T(8,128)S(1)}, u32[]{:S(2)}, u32[]{:S(2)}) collective-permute-start(f32[64,10]{1,0:T(8,128)} %get-tuple-element.31), channel_id=1, source_target_pairs={{0,252},{4,0},{8,4},{12,8},{16,12},{20,16},{24,20},{28,24},{32,28}... | collective-permute-start | bytes 7688 | tf_op jit(solution)/shard_map/ppermute | solution.py:340

commit v7 on v6

--- a/solution.py
+++ b/solution.py
@@ -80,6 +80,13 @@
         if self.reverse_fold:
             fold = reverse_lanes(fold)
         pf_ref[...] = fold[:levels]
+
+    def finish4(self, ec_ref, wc_ref, sr_ref, nr_ref):
+        levels = self.levels
+        ec_ref[...] = self.cols[0][:, :levels]
+        wc_ref[...] = self.cols[1][:, :levels]
+        sr_ref[...] = self.rows_acc[0][:levels]
+        nr_ref[...] = self.rows_acc[1][:levels]
 
     def finish_pairs(self, flag_ref, pe_ref, pw_ref, pa_ref, pb_ref):
         levels = self.levels
@@ -126,10 +133,14 @@
     out.finish_pairs(flag_ref, pe_ref, pw_ref, pa_ref, pb_ref)
 
 
-def core_kernel(first, emit, si_ref, wt_ref, lm_ref, adj_ref, d_ref, t_ref, u_ref, v_ref, *rest):
+def core_kernel(first, emit, fixin, si_ref, wt_ref, flag_ref, lm_ref, adj_ref, d_ref, t_ref, u_ref, v_ref, *rest):
     del si_ref
-    if emit:
-        u2_ref, v2_ref, out_ref, ce_ref, cw_ref, cn_ref, cs_ref, cf_ref, a_ref = rest
+    rest = list(rest)
+    if fixin:
+        he_ref, hw_ref, ha_ref, hb_ref = rest[:4]
+        rest = rest[4:]
+    if emit:
+        u2_ref, v2_ref, out_ref, ce_ref, cw_ref, cn_ref, cs_ref, cf_ref, ec_ref, wc_ref, sr_ref, nr_ref, a_ref = rest
     else:
         out_ref, a_ref = rest
     levels, rows, width = adj_ref.shape
@@ -140,10 +151,27 @@
         for m in range(levels):
             a_ref[m] = adj_ref[m] * wet
         src = a_ref
+    elif fixin:
+        he = he_ref[...]
+        hw = hw_ref[...]
+        even = flag_ref[0] == 0
+        for m in range(levels):
+            a_row = ha_ref[m:m + 1, :]
+            b_row = hb_ref[m:m + 1, :]
+            corr = (
+                jnp.where(lane == width - 1, jnp.broadcast_to(he[:, m:m + 1], (rows, width)), 0.0)
+                + jnp.where(lane == 0, jnp.broadcast_to(hw[:, m:m + 1], (rows, width)), 0.0)
+                + jnp.where(row == rows - 1, jnp.where(even, a_row, b_row), 0.0)
+                + jnp.where(row == 0, jnp.where(even, b_row, a_row), 0.0)
+            )
+            a_ref[m] = adj_ref[m] + wet * corr
+        src = a_ref
     else:
         src = adj_ref
     d = d_ref[...]
-    coef = Collector(levels, rows, width, False) if emit else None
+    if emit:
+        coef = Collector(levels, rows, width, False)
+        edges = Collector(levels, rows, width, False)
 
     for l in range(levels):
         a = src[l]
@@ -158,11 +186,61 @@
         north = jnp.where(row == rows - 1, 0.0, pltpu.roll(s + advect_scale * mf, rows - 1, 0))
         south = jnp.where(row == 0, 0.0, pltpu.roll(s - advect_scale * mf, 1, 0))
         t = t_ref[l]
-        out_ref[l] = wet * (a - 4.0 * s + east + west + north + south + vertical - damping * t * t * a)
+        new = wet * (a - 4.0 * s + east + west + north + south + vertical - damping * t * t * a)
+        out_ref[l] = new
         if emit:
             coef.add(l, *coefficients(l, d, u2_ref[l], v2_ref[l], rows, width))
+            bottom, top_row = new[0:1, :], new[rows - 1:rows, :]
+            edges.add(l, new[:, 0:1], new[:, width - 1:width], bottom, top_row, top_row)
     if emit:
         coef.finish(ce_ref, cw_ref, cn_ref, cs_ref, cf_ref)
+        edges.finish4(ec_ref, wc_ref, sr_ref, nr_ref)
+
+
+def payload_kernel(wt_ref, flag_ref, ec_ref, wc_ref, sr_ref, nr_ref, he_ref, hw_ref, ha_ref, hb_ref,
+                   ce_ref, cw_ref, cn_ref, cs_ref, cf_ref, pe_ref, pw_ref, pa_ref, pb_ref):
+    rows, levels = ec_ref.shape
+    width = sr_ref.shape[1]
+    wet_row = wet_field(wt_ref, 1, width)
+    wet_first = wet_row[:, 0:1]
+    wet_last = wet_row[:, width - 1:width]
+    r = lax.broadcasted_iota(jnp.int32, (rows, 1), 0)
+    g = lax.broadcasted_iota(jnp.int32, (1, width), 1)
+    even = flag_ref[0] == 0
+    ec, wc, he, hw, ce, cw = (x[...] for x in (ec_ref, wc_ref, he_ref, hw_ref, ce_ref, cw_ref))
+    out = Collector(levels, rows, width, True)
+    for l in range(levels):
+        a_row = ha_ref[l:l + 1, :]
+        b_row = hb_ref[l:l + 1, :]
+        north_row = jnp.where(even, a_row, b_row)
+        south_row = jnp.where(even, b_row, a_row)
+        he_c = he[:, l:l + 1]
+        hw_c = hw[:, l:l + 1]
+        col_first = ec[:, l:l + 1] + wet_first * (
+            hw_c + jnp.where(r == 0, south_row[:, 0:1], 0.0) + jnp.where(r == rows - 1, north_row[:, 0:1], 0.0)
+        )
+        col_last = wc[:, l:l + 1] + wet_last * (
+            he_c
+            + jnp.where(r == 0, south_row[:, width - 1:width], 0.0)
+            + jnp.where(r == rows - 1, north_row[:, width - 1:width], 0.0)
+        )
+        row_first = sr_ref[l:l + 1, :] + wet_row * (
+            south_row + jnp.where(g == 0, hw_c[0:1, :], 0.0) + jnp.where(g == width - 1, he_c[0:1, :], 0.0)
+        )
+        row_last = nr_ref[l:l + 1, :] + wet_row * (
+            north_row
+            + jnp.where(g == 0, hw_c[rows - 1:rows, :], 0.0)
+            + jnp.where(g == width - 1, he_c[rows - 1:rows, :], 0.0)
+        )
+        out.add(
+            l,
+            ce[:, l:l + 1] * col_first,
+            cw[:, l:l + 1] * col_last,
+            cn_ref[l:l + 1, :] * row_first,
+            cs_ref[l:l + 1, :] * row_last,
+            cf_ref[l:l + 1, :] * row_last,
+        )
+    out.finish_pairs(flag_ref, pe_ref, pw_ref, pa_ref, pb_ref)
 
 
 def fix_kernel(emit, wt_ref, flag_ref, part_ref, he_ref, hw_ref, ha_ref, hb_ref, *rest):
@@ -239,25 +317,29 @@
     )(si, wt, flags, af, d, zonal, merid)
 
 
-def run_core(k, k_next, si, wt, lm, adj, d, tracer, zonal, merid):
+def run_core(k, k_next, si, wt, flags, lm, adj, d, tracer, zonal, merid, halos=()):
     levels, rows, width = adj.shape
     first = k_next is not None
     emit = k_next is not None
+    fixin = bool(halos)
     state = state_spec(k, levels, rows, width)
     in_specs = [pl.BlockSpec(memory_space=pltpu.SMEM), whole(adj.shape), whole(d.shape), state, state, state]
-    args = [si, wt, lm, adj, d, tracer, zonal, merid]
+    args = [si, wt, flags, lm, adj, d, tracer, zonal, merid]
+    if fixin:
+        in_specs += [whole(h.shape) for h in halos]
+        args += list(halos)
     out_shape = [jax.ShapeDtypeStruct(adj.shape, jnp.float32)]
     if emit:
         nxt = state_spec(k_next, levels, rows, width)
         in_specs += [nxt, nxt]
         args += [zonal, merid]
-        out_shape += payload_shapes(levels, rows, width)
+        out_shape += payload_shapes(levels, rows, width) + pair_shapes(levels, rows, width)
     n = levels * rows * width
     outs = pl.pallas_call(
-        functools.partial(core_kernel, first, emit),
+        functools.partial(core_kernel, first, emit, fixin),
         out_shape=out_shape,
         grid_spec=pltpu.PrefetchScalarGridSpec(
-            num_scalar_prefetch=2,
+            num_scalar_prefetch=3,
             grid=(1,),
             in_specs=in_specs,
             out_specs=[whole(s.shape) for s in out_shape],
@@ -265,7 +347,26 @@
         ),
         cost_estimate=pl.CostEstimate(flops=60 * n, bytes_accessed=32 * n, transcendentals=0),
     )(*args)
-    return outs[0], outs[1:]
+    return outs[0], outs[1:6], outs[6:]
+
+
+def run_payload(wt, flags, edges, halos, coefs):
+    small = [*edges, *halos, *coefs]
+    rows, levels = edges[0].shape
+    width = edges[2].shape[1]
+    shapes = pair_shapes(levels, rows, width)
+    return pl.pallas_call(
+        payload_kernel,
+        out_shape=shapes,
+        grid_spec=pltpu.PrefetchScalarGridSpec(
+            num_scalar_prefetch=2,
+            grid=(1,),
+            in_specs=[whole(x.shape) for x in small],
+            out_specs=[whole(x.shape) for x in shapes],
+        ),
+        cost_estimate=pl.CostEstimate(flops=40 * levels * width, bytes_accessed=64 * levels * width,
+                                      transcendentals=0),
+    )(wt, flags, *small)
 
 
 def run_fix(wt, flags, part, halos, coefs):
@@ -346,14 +447,17 @@
     payloads = run_prologue(STEPS - 1, state_index, wt, flags, adjoint_final, diffusivity,
                             stored_zonal, stored_meridional)
     adj = adjoint_final
+    previous = ()
     for back in range(STEPS):
         k = STEPS - 1 - back
         k_next = k - 1 if k > 0 else None
         halos = exchange(payloads)
-        part, coefs = run_core(k, k_next, state_index, wt, level_mixing, adj, diffusivity,
-                               stored_tracer, stored_zonal, stored_meridional)
+        part, coefs, edges = run_core(k, k_next, state_index, wt, flags, level_mixing, adj, diffusivity,
+                                      stored_tracer, stored_zonal, stored_meridional, previous)
         if coefs:
-            adj, payloads = run_fix(wt, flags, part, halos, coefs)
+            payloads = run_payload(wt, flags, edges, halos, coefs)
+            adj = part
+            previous = halos
         else:
             adj = fix_in_xla(wet_tiles, lat_index, part, halos)
     return adj

time: 53.3 us -> 54.4 us (1.021)
  Pallas kernels: 16.5 us -> 17.9 us
    pallas_call x3, Pallas kernels: 13.3 us -> 14.7 us  [the longest x2 9.57 us: run_core(): pl.pallas_call(functools.partial(core_kernel, first, emit, fixin), out_sh...]
  transfers between devices with their start and end apart: 8 -> 8, of which waited for: 0 -> 0; matrix products, arithmetic and copies ran while one was open for 0% -> 0% of each run, Pallas kernels for 17% -> 18%
where the time goes in v7:
time: 54.4 us; the launch traced here: 54.1 us
  starting transfers between devices  32.4 us (60%)
  Pallas kernels  17.9 us (33%)
  other arithmetic  2.84 us (5%)
  local copies, waits for them, and re-layouts  0.83 us (2%)
    ppermute x2, starting transfers between devices, exchange(): he = lax.ppermute(pe, 'lon', to_west)  16.8 us
    ppermute x2, starting transfers between devices, exchange(): hb = lax.ppermute(pb, ('lon', 'lat'), pairs_b)  14.6 us
    pallas_call x2, Pallas kernels, run_core(): pl.pallas_call(functools.partial(core_kernel, first, emit, fixin), out_sh...  9.57 us
    pallas_call x1, Pallas kernels, run_payload(): pl.pallas_call(payload_kernel, out_shape=shapes, grid_spec=pltpu.Prefetch...  5.08 us
    pallas_call x1, Pallas kernels, run_prologue(): pl.pallas_call(prologue_kernel, out_shape=shapes, grid_spec=pltpu.Prefetc...  3.23 us
    add x1, other arithmetic, fix_in_xla(): return part + wet * corr  2.21 us
  transfers between devices with their start and end apart: 8, of which 0 were waited for; matrix products, arithmetic and copies ran while one was open for 0% of the time, Pallas kernels for 18%

profile of v7, /device:TPU:3, one launch (start us, length us, event | category | flops | bytes accessed | tf_op | source)
XLA Modules:
  0.0 54.1 jit_solution(18366153402404537087)
XLA Ops:
  0.0 0.6 %pad_add_fusion.flag_ref = s32[2]{0:T(128)} fusion(s32[1]{0:T(128)} %bitcast.2, s32[1]{0:T(128)} %bitcast.1), kind=kLoop, calls=%fused_computation.5 | loop fusion | flops 2 | bytes 16 | tf_op jit(solution)/shard_map/stack | solution.py:427
  0.6 3.2 %shard_map.83 = (f32[64,10]{1,0:T(8,128)}, f32[64,10]{1,0:T(8,128)}, f32[10,256]{1,0:T(8,128)}, f32[10,256]{1,0:T(8,128)}) custom-call(s32[2]{0:T(128)} %si_ref.5, s32[2]{0:T(128)} %bitcast.10, s32[2]{0:T(128)} %pad_add_fusion.flag_ref, f32[10,64,256]{2,1,0:T(8,128)} %af_ref.1, f32[64,256]{1,0:T(8,128)} %d_ref.5, f32[4,10,64,256]{3,2,1,0:T(8,128)} %u_ref.5, ...), custom_call_target="tpu_custom_call" | custom-call | flops 327680 | bytes 1966080 | tf_op jit(solution)/shard_map/pallas_call | solution.py:306
  3.8 9.6 %collective-permute-start = (f32[64,10]{1,0:T(8,128)}, f32[64,10]{1,0:T(8,128)S(1)}, u32[]{:S(2)}, u32[]{:S(2)}) collective-permute-start(f32[64,10]{1,0:T(8,128)} %get-tuple-element.24), channel_id=1, source_target_pairs={{0,252},{4,0},{8,4},{12,8},{16,12},{20,16},{24,20},{28,24},{32,28}... | collective-permute-start | bytes 7688 | tf_op jit(solution)/shard_map/ppermute | solution.py:441
  13.4 0.0 collective-permute-start.1
  13.4 1.0 %collective-permute-start.2 = (f32[10,256]{1,0:T(8,128)}, f32[10,256]{1,0:T(8,128)S(1)}, u32[]{:S(2)}, u32[]{:S(2)}) collective-permute-start(f32[10,256]{1,0:T(8,128)} %get-tuple-element.26), channel_id=1, source_target_pairs={{0,1},{1,0},{2,3},{3,2},{4,5},{5,4},{6,7},{7,6},{8,9},{9,8},{10,11... | collective-permute-start | bytes 30728 | tf_op jit(solution)/shard_map/ppermute | solution.py:443
  14.4 9.4 %collective-permute-start.3 = (f32[10,256]{1,0:T(8,128)}, f32[10,256]{1,0:T(8,128)S(1)}, u32[]{:S(2)}, u32[]{:S(2)}) collective-permute-start(f32[10,256]{1,0:T(8,128)} %get-tuple-element.27), channel_id=1, source_target_pairs={{1,2},{2,1},{3,255},{5,6},{6,5},{7,251},{9,10},{10,9},{11,247},{13... | collective-permute-start | bytes 30728 | tf_op jit(solution)/shard_map/ppermute | solution.py:444
  23.8 0.1 broadcast_bitcast_fusion
  23.9 5.0 %shard_map.82 = (f32[10,64,256]{2,1,0:T(8,128)}, f32[64,10]{1,0:T(8,128)}, f32[64,10]{1,0:T(8,128)}, f32[10,256]{1,0:T(8,128)}, f32[10,256]{1,0:T(8,128)}, /*ind...) custom-call(s32[2]{0:T(128)} %si_ref.5, s32[2]{0:T(128)} %bitcast.11, ...), custom_call_target="tpu_custom_call" | custom-call | flops 9830400 | bytes 5242880 | tf_op jit(solution)/shard_map/pallas_call | solution.py:338
  28.9 0.0 collective-permute-done.rest_0_.he_ref
  28.9 0.0 collective-permute-done.1.rest_1_.hw_ref
  29.0 0.5 copy-done
  29.5 0.0 copy-done.1
  29.5 0.0 copy-done.2
  29.6 0.0 copy-done.3
  29.6 5.1 %shard_map.85 = (f32[64,10]{1,0:T(8,128)}, f32[64,10]{1,0:T(8,128)}, f32[10,256]{1,0:T(8,128)}, f32[10,256]{1,0:T(8,128)}) custom-call(s32[2]{0:T(128)} %bitcast.12, s32[2]{0:T(128)} %pad_add_fusion.flag_ref, f32[64,10]{1,0:T(8,128)} %get-tuple-element.28.ec_ref, f32[64,10]{1,0:T(8,128)} %get-tuple-element.29.wc_ref, f32[10,256]{1,0:T(8,128)} %get-tuple-element.30.sr_ref, ...), custom_call_target="tpu_custom_call" | custom-call | flops 102400 | bytes 163840 | tf_op jit(solution)/shard_map/pallas_call | solution.py:358
  34.7 0.0 collective-permute-start.6
  34.7 5.2 %collective-permute-start.7 = (f32[10,256]{1,0:T(8,128)}, f32[10,256]{1,0:T(8,128)S(1)}, u32[]{:S(2)}, u32[]{:S(2)}) collective-permute-start(f32[10,256]{1,0:T(8,128)} %get-tuple-element.40), channel_id=1, source_target_pairs={{1,2},{2,1},{3,255},{5,6},{6,5},{7,251},{9,10},{10,9},{11,247},{13... | collective-permute-start | bytes 30728 | tf_op jit(solution)/shard_map/ppermute | solution.py:444
  39.9 0.1 collective-permute-start.5
  40.0 7.2 %collective-permute-start.4 = (f32[64,10]{1,0:T(8,128)}, f32[64,10]{1,0:T(8,128)S(1)}, u32[]{:S(2)}, u32[]{:S(2)}) collective-permute-start(f32[64,10]{1,0:T(8,128)} %get-tuple-element.37), channel_id=1, source_target_pairs={{0,252},{4,0},{8,4},{12,8},{16,12},{20,16},{24,20},{28,24},{32,28}... | collective-permute-start | bytes 7688 | tf_op jit(solution)/shard_map/ppermute | solution.py:441
  47.1 4.5 %shard_map.84 = f32[10,64,256]{2,1,0:T(8,128)} custom-call(s32[2]{0:T(128)} %si_ref.5, s32[2]{0:T(128)} %bitcast.13, s32[2]{0:T(128)} %pad_add_fusion.flag_ref, f32[10,10]{1,0:T(8,128)} %lm_ref.3, f32[10,64,256]{2,1,0:T(8,128)} %get-tuple-element.23.adj_ref, f32[64,256]{1,0:T(8,128)} %d_ref.5, f32[4,10,64,256]{3,2,1,0:T(8,128)} %t_ref.3, ...), custom_call_target="tpu_custom_call" | custom-call | flops 9830400 | bytes 5242880 | tf_op jit(solution)/shard_map/pallas_call | solution.py:338
  51.7 0.1 copy.10
  51.7 0.1 copy.9
  51.8 0.0 collective-permute-done.7
  51.9 2.2 %multiply_add_fusion = f32[10,64,256]{2,1,0:T(8,128)} fusion(f32[10,64,256]{2,1,0:T(8,128)} %shard_map.84, f32[10,256]{1,0:T(8,128)S(1)} %get-tuple-element.42, f32[10,256]{1,0:T(8,128)S(1)} %get-tuple-element.41, f32[10,64]{1,0:T(8,128)S(1)} %copy.10, f32[10,64]{1,0:T(8,128)S(1)} %copy.9, f32[256]{0:T(256)S(1)} %broadcast_bitcast_fusion, ...), kind=kLoop, calls=%fused_computation | loop fusion | flops 1474560 | bytes 1337984 | tf_op jit(solution)/shard_map/add | solution.py:410
  (15 shorter events, 0.0 us)
Async XLA Ops:
  0.6 23.2 %copy-start.4 = (s32[1,2]{1,0:T(1,128)S(1)}, s32[1,2]{1,0:T(1,128)}, u32[]{:S(2)}) copy-start(s32[1,2]{1,0:T(1,128)} %param.14) | copy-start | bytes 28
  3.8 25.1 %collective-permute-start = (f32[64,10]{1,0:T(8,128)}, f32[64,10]{1,0:T(8,128)S(1)}, u32[]{:S(2)}, u32[]{:S(2)}) collective-permute-start(f32[64,10]{1,0:T(8,128)} %get-tuple-element.24), channel_id=1, source_target_pairs={{0,252},{4,0},{8,4},{12,8},{16,12},{20,16},{24,20},{28,24},{32,28}... | collective-permute-start | bytes 7688 | tf_op jit(solution)/shard_map/ppermute | solution.py:441
  13.4 15.5 %collective-permute-start.1 = (f32[64,10]{1,0:T(8,128)}, f32[64,10]{1,0:T(8,128)S(1)}, u32[]{:S(2)}, u32[]{:S(2)}) collective-permute-start(f32[64,10]{1,0:T(8,128)} %get-tuple-element.25), channel_id=1, source_target_pairs={{0,4},{4,8},{8,12},{12,16},{16,20},{20,24},{24,28},{28,32},{32,36}... | collective-permute-start | bytes 7688 | tf_op jit(solution)/shard_map/ppermute | solution.py:442
  13.4 15.5 %collective-permute-start.2 = (f32[10,256]{1,0:T(8,128)}, f32[10,256]{1,0:T(8,128)S(1)}, u32[]{:S(2)}, u32[]{:S(2)}) collective-permute-start(f32[10,256]{1,0:T(8,128)} %get-tuple-element.26), channel_id=1, source_target_pairs={{0,1},{1,0},{2,3},{3,2},{4,5},{5,4},{6,7},{7,6},{8,9},{9,8},{10,11... | collective-permute-start | bytes 30728 | tf_op jit(solution)/shard_map/ppermute | solution.py:443
  14.4 14.6 %collective-permute-start.3 = (f32[10,256]{1,0:T(8,128)}, f32[10,256]{1,0:T(8,128)S(1)}, u32[]{:S(2)}, u32[]{:S(2)}) collective-permute-start(f32[10,256]{1,0:T(8,128)} %get-tuple-element.27), channel_id=1, source_target_pairs={{1,2},{2,1},{3,255},{5,6},{6,5},{7,251},{9,10},{10,9},{11,247},{13... | collective-permute-start | bytes 30728 | tf_op jit(solution)/shard_map/ppermute | solution.py:444
  28.9 0.6 %copy-start = (f32[64,10]{1,0:T(8,128)}, f32[64,10]{1,0:T(8,128)S(1)}, u32[]{:S(2)}) copy-start(f32[64,10]{1,0:T(8,128)S(1)} %collective-permute-done.rest_0_.he_ref) | copy-start | bytes 7684
  28.9 0.6 %copy-start.1 = (f32[64,10]{1,0:T(8,128)}, f32[64,10]{1,0:T(8,128)S(1)}, u32[]{:S(2)}) copy-start(f32[64,10]{1,0:T(8,128)S(1)} %collective-permute-done.1.rest_1_.hw_ref) | copy-start | bytes 7684
  28.9 0.6 %copy-start.2 = (f32[10,256]{1,0:T(8,128)}, f32[10,256]{1,0:T(8,128)S(1)}, u32[]{:S(2)}) copy-start(f32[10,256]{1,0:T(8,128)S(1)} %collective-permute-done.2.rest_2_.ha_ref) | copy-start | bytes 30724
  29.0 0.6 %copy-start.3 = (f32[10,256]{1,0:T(8,128)}, f32[10,256]{1,0:T(8,128)S(1)}, u32[]{:S(2)}) copy-start(f32[10,256]{1,0:T(8,128)S(1)} %collective-permute-done.3.rest_3_.hb_ref) | copy-start | bytes 30724
  34.7 17.2 %collective-permute-start.6 = (f32[10,256]{1,0:T(8,128)}, f32[10,256]{1,0:T(8,128)S(1)}, u32[]{:S(2)}, u32[]{:S(2)}) collective-permute-start(f32[10,256]{1,0:T(8,128)} %get-tuple-element.39), channel_id=1, source_target_pairs={{0,1},{1,0},{2,3},{3,2},{4,5},{5,4},{6,7},{7,6},{8,9},{9,8},{10,11... | collective-permute-start | bytes 30728 | tf_op jit(solution)/shard_map/ppermute | solution.py:443
  34.7 17.2 %collective-permute-start.7 = (f32[10,256]{1,0:T(8,128)}, f32[10,256]{1,0:T(8,128)S(1)}, u32[]{:S(2)}, u32[]{:S(2)}) collective-permute-start(f32[10,256]{1,0:T(8,128)} %get-tuple-element.40), channel_id=1, source_target_pairs={{1,2},{2,1},{3,255},{5,6},{6,5},{7,251},{9,10},{10,9},{11,247},{13... | collective-permute-start | bytes 30728 | tf_op jit(solution)/shard_map/ppermute | solution.py:444
  39.9 11.8 %collective-permute-start.5 = (f32[64,10]{1,0:T(8,128)}, f32[64,10]{1,0:T(8,128)S(1)}, u32[]{:S(2)}, u32[]{:S(2)}) collective-permute-start(f32[64,10]{1,0:T(8,128)} %get-tuple-element.38), channel_id=1, source_target_pairs={{0,4},{4,8},{8,12},{12,16},{16,20},{20,24},{24,28},{28,32},{32,36}... | collective-permute-start | bytes 7688 | tf_op jit(solution)/shard_map/ppermute | solution.py:442
  40.0 11.8 %collective-permute-start.4 = (f32[64,10]{1,0:T(8,128)}, f32[64,10]{1,0:T(8,128)S(1)}, u32[]{:S(2)}, u32[]{:S(2)}) collective-permute-start(f32[64,10]{1,0:T(8,128)} %get-tuple-element.37), channel_id=1, source_target_pairs={{0,252},{4,0},{8,4},{12,8},{16,12},{20,16},{24,20},{28,24},{32,28}... | collective-permute-start | bytes 7688 | tf_op jit(solution)/shard_map/ppermute | solution.py:441

commit v8 on v7

--- a/solution.py
+++ b/solution.py
@@ -140,7 +140,7 @@
         he_ref, hw_ref, ha_ref, hb_ref = rest[:4]
         rest = rest[4:]
     if emit:
-        u2_ref, v2_ref, out_ref, ce_ref, cw_ref, cn_ref, cs_ref, cf_ref, ec_ref, wc_ref, sr_ref, nr_ref, a_ref = rest
+        u2_ref, v2_ref, out_ref, lon_ref, lat_ref, a_ref = rest
     else:
         out_ref, a_ref = rest
     levels, rows, width = adj_ref.shape
@@ -170,8 +170,11 @@
         src = adj_ref
     d = d_ref[...]
     if emit:
-        coef = Collector(levels, rows, width, False)
-        edges = Collector(levels, rows, width, False)
+        lon_lane = lax.broadcasted_iota(jnp.int32, (rows, TLON), 1)
+        lat_rows = -(-5 * levels // 8) * 8
+        lat_row = lax.broadcasted_iota(jnp.int32, (lat_rows, width), 0)
+        lon_acc = jnp.zeros((rows, TLON), jnp.float32)
+        lat_acc = jnp.zeros((lat_rows, width), jnp.float32)
 
     for l in range(levels):
         a = src[l]
@@ -189,25 +192,31 @@
         new = wet * (a - 4.0 * s + east + west + north + south + vertical - damping * t * t * a)
         out_ref[l] = new
         if emit:
-            coef.add(l, *coefficients(l, d, u2_ref[l], v2_ref[l], rows, width))
-            bottom, top_row = new[0:1, :], new[rows - 1:rows, :]
-            edges.add(l, new[:, 0:1], new[:, width - 1:width], bottom, top_row, top_row)
-    if emit:
-        coef.finish(ce_ref, cw_ref, cn_ref, cs_ref, cf_ref)
-        edges.finish4(ec_ref, wc_ref, sr_ref, nr_ref)
-
-
-def payload_kernel(wt_ref, flag_ref, ec_ref, wc_ref, sr_ref, nr_ref, he_ref, hw_ref, ha_ref, hb_ref,
-                   ce_ref, cw_ref, cn_ref, cs_ref, cf_ref, pe_ref, pw_ref, pa_ref, pb_ref):
-    rows, levels = ec_ref.shape
-    width = sr_ref.shape[1]
+            ce, cw, cn, cs, cf = coefficients(l, d, u2_ref[l], v2_ref[l], rows, width)
+            for j, col in enumerate((ce, cw, new[:, 0:1], new[:, width - 1:width])):
+                lon_acc = jnp.where(lon_lane == j * levels + l, jnp.broadcast_to(col, (rows, TLON)), lon_acc)
+            for j, line in enumerate((cn, cs, cf, new[0:1, :], new[rows - 1:rows, :])):
+                lat_acc = jnp.where(lat_row == j * levels + l, jnp.broadcast_to(line, lat_acc.shape), lat_acc)
+    if emit:
+        lon_ref[...] = lon_acc[:, : 4 * levels]
+        lat_ref[...] = lat_acc[: 5 * levels]
+
+
+def payload_kernel(wt_ref, flag_ref, lon_ref, lat_ref, he_ref, hw_ref, ha_ref, hb_ref, pe_ref, pw_ref, pa_ref, pb_ref):
+    rows, levels = he_ref.shape
+    width = ha_ref.shape[1]
     wet_row = wet_field(wt_ref, 1, width)
     wet_first = wet_row[:, 0:1]
     wet_last = wet_row[:, width - 1:width]
     r = lax.broadcasted_iota(jnp.int32, (rows, 1), 0)
     g = lax.broadcasted_iota(jnp.int32, (1, width), 1)
     even = flag_ref[0] == 0
-    ec, wc, he, hw, ce, cw = (x[...] for x in (ec_ref, wc_ref, he_ref, hw_ref, ce_ref, cw_ref))
+    lon, he, hw = lon_ref[...], he_ref[...], hw_ref[...]
+    ce, cw, ec, wc = (lon[:, j * levels:(j + 1) * levels] for j in range(4))
+
+    def lat(j, l):
+        return lat_ref[j * levels + l:j * levels + l + 1, :]
+
     out = Collector(levels, rows, width, True)
     for l in range(levels):
         a_row = ha_ref[l:l + 1, :]
@@ -224,10 +233,10 @@
             + jnp.where(r == 0, south_row[:, width - 1:width], 0.0)
             + jnp.where(r == rows - 1, north_row[:, width - 1:width], 0.0)
         )
-        row_first = sr_ref[l:l + 1, :] + wet_row * (
+        row_first = lat(3, l) + wet_row * (
             south_row + jnp.where(g == 0, hw_c[0:1, :], 0.0) + jnp.where(g == width - 1, he_c[0:1, :], 0.0)
         )
-        row_last = nr_ref[l:l + 1, :] + wet_row * (
+        row_last = lat(4, l) + wet_row * (
             north_row
             + jnp.where(g == 0, hw_c[rows - 1:rows, :], 0.0)
             + jnp.where(g == width - 1, he_c[rows - 1:rows, :], 0.0)
@@ -236,9 +245,9 @@
             l,
             ce[:, l:l + 1] * col_first,
             cw[:, l:l + 1] * col_last,
-            cn_ref[l:l + 1, :] * row_first,
-            cs_ref[l:l + 1, :] * row_last,
-            cf_ref[l:l + 1, :] * row_last,
+            lat(0, l) * row_first,
+            lat(1, l) * row_last,
+            lat(2, l) * row_last,
         )
     out.finish_pairs(flag_ref, pe_ref, pw_ref, pa_ref, pb_ref)
 
@@ -333,7 +342,8 @@
         nxt = state_spec(k_next, levels, rows, width)
         in_specs += [nxt, nxt]
         args += [zonal, merid]
-        out_shape += payload_shapes(levels, rows, width) + pair_shapes(levels, rows, width)
+        out_shape += [jax.ShapeDtypeStruct((rows, 4 * levels), jnp.float32),
+                      jax.ShapeDtypeStruct((5 * levels, width), jnp.float32)]
     n = levels * rows * width
     outs = pl.pallas_call(
         functools.partial(core_kernel, first, emit, fixin),
@@ -347,13 +357,13 @@
         ),
         cost_estimate=pl.CostEstimate(flops=60 * n, bytes_accessed=32 * n, transcendentals=0),
     )(*args)
-    return outs[0], outs[1:6], outs[6:]
-
-
-def run_payload(wt, flags, edges, halos, coefs):
-    small = [*edges, *halos, *coefs]
-    rows, levels = edges[0].shape
-    width = edges[2].shape[1]
+    return outs[0], outs[1:]
+
+
+def run_payload(wt, flags, packed, halos):
+    small = [*packed, *halos]
+    rows, levels = halos[0].shape
+    width = halos[2].shape[1]
     shapes = pair_shapes(levels, rows, width)
     return pl.pallas_call(
         payload_kernel,
@@ -367,29 +377,6 @@
         cost_estimate=pl.CostEstimate(flops=40 * levels * width, bytes_accessed=64 * levels * width,
                                       transcendentals=0),
     )(wt, flags, *small)
-
-
-def run_fix(wt, flags, part, halos, coefs):
-    levels, rows, width = part.shape
-    emit = bool(coefs)
-    args = [wt, flags, part, *halos, *coefs]
-    in_specs = [whole(x.shape) for x in args[2:]]
-    out_shape = [jax.ShapeDtypeStruct(part.shape, jnp.float32)]
-    if emit:
-        out_shape += pair_shapes(levels, rows, width)
-    n = levels * rows * width
-    outs = pl.pallas_call(
-        functools.partial(fix_kernel, emit),
-        out_shape=out_shape,
-        grid_spec=pltpu.PrefetchScalarGridSpec(
-            num_scalar_prefetch=2,
-            grid=(1,),
-            in_specs=in_specs,
-            out_specs=[whole(s.shape) for s in out_shape],
-        ),
-        cost_estimate=pl.CostEstimate(flops=10 * n, bytes_accessed=8 * n, transcendentals=0),
-    )(*args)
-    return outs[0], outs[1:]
 
 
 def fix_in_xla(wet_tiles, lat_index, part, halos):
@@ -452,10 +439,10 @@
         k = STEPS - 1 - back
         k_next = k - 1 if k > 0 else None
         halos = exchange(payloads)
-        part, coefs, edges = run_core(k, k_next, state_index, wt, flags, level_mixing, adj, diffusivity,
-                                      stored_tracer, stored_zonal, stored_meridional, previous)
-        if coefs:
-            payloads = run_payload(wt, flags, edges, halos, coefs)
+        part, packed = run_core(k, k_next, state_index, wt, flags, level_mixing, adj, diffusivity,
+                                stored_tracer, stored_zonal, stored_meridional, previous)
+        if packed:
+            payloads = run_payload(wt, flags, packed, halos)
             adj = part
             previous = halos
         else:

time: 54.4 us -> 54.9 us (level)
  no operation moved by 1% of the time
where the time goes in v8:
time: 54.9 us; the launch traced here: 54.5 us
  starting transfers between devices  32.4 us (59%)
  Pallas kernels  18.3 us (33%)
  other arithmetic  2.84 us (5%)
  local copies, waits for them, and re-layouts  0.83 us (2%)
    ppermute x2, starting transfers between devices, exchange(): he = lax.ppermute(pe, 'lon', to_west)  16.8 us
    ppermute x2, starting transfers between devices, exchange(): hb = lax.ppermute(pb, ('lon', 'lat'), pairs_b)  14.6 us
    pallas_call x2, Pallas kernels, run_core(): pl.pallas_call(functools.partial(core_kernel, first, emit, fixin), out_sh...  9.56 us
    pallas_call x1, Pallas kernels, run_payload(): pl.pallas_call(payload_kernel, out_shape=shapes, grid_spec=pltpu.Prefetch...  5.55 us
    pallas_call x1, Pallas kernels, run_prologue(): pl.pallas_call(prologue_kernel, out_shape=shapes, grid_spec=pltpu.Prefetc...  3.22 us
    add x1, other arithmetic, fix_in_xla(): return part + wet * corr  2.21 us
  transfers between devices with their start and end apart: 8, of which 0 were waited for; matrix products, arithmetic and copies ran while one was open for 0% of the time, Pallas kernels for 18%

profile of v8, /device:TPU:3, one launch (start us, length us, event | category | flops | bytes accessed | tf_op | source)
XLA Modules:
  0.0 54.5 jit_solution(8275243366729154963)
XLA Ops:
  0.0 0.6 %pad_add_fusion.flag_ref = s32[2]{0:T(128)} fusion(s32[1]{0:T(128)} %bitcast.2, s32[1]{0:T(128)} %bitcast.1), kind=kLoop, calls=%fused_computation.5 | loop fusion | flops 2 | bytes 16 | tf_op jit(solution)/shard_map/stack | solution.py:414
  0.6 3.2 %shard_map.83 = (f32[64,10]{1,0:T(8,128)}, f32[64,10]{1,0:T(8,128)}, f32[10,256]{1,0:T(8,128)}, f32[10,256]{1,0:T(8,128)}) custom-call(s32[2]{0:T(128)} %si_ref.5, s32[2]{0:T(128)} %bitcast.10, s32[2]{0:T(128)} %pad_add_fusion.flag_ref, f32[10,64,256]{2,1,0:T(8,128)} %af_ref.1, f32[64,256]{1,0:T(8,128)} %d_ref.5, f32[4,10,64,256]{3,2,1,0:T(8,128)} %u_ref.5, ...), custom_call_target="tpu_custom_call" | custom-call | flops 327680 | bytes 1966080 | tf_op jit(solution)/shard_map/pallas_call | solution.py:315
  3.8 9.6 %collective-permute-start = (f32[64,10]{1,0:T(8,128)}, f32[64,10]{1,0:T(8,128)S(1)}, u32[]{:S(2)}, u32[]{:S(2)}) collective-permute-start(f32[64,10]{1,0:T(8,128)} %get-tuple-element.17), channel_id=1, source_target_pairs={{0,252},{4,0},{8,4},{12,8},{16,12},{20,16},{24,20},{28,24},{32,28}... | collective-permute-start | bytes 7688 | tf_op jit(solution)/shard_map/ppermute | solution.py:428
  13.4 0.0 collective-permute-start.1
  13.4 1.0 %collective-permute-start.2 = (f32[10,256]{1,0:T(8,128)}, f32[10,256]{1,0:T(8,128)S(1)}, u32[]{:S(2)}, u32[]{:S(2)}) collective-permute-start(f32[10,256]{1,0:T(8,128)} %get-tuple-element.19), channel_id=1, source_target_pairs={{0,1},{1,0},{2,3},{3,2},{4,5},{5,4},{6,7},{7,6},{8,9},{9,8},{10,11... | collective-permute-start | bytes 30728 | tf_op jit(solution)/shard_map/ppermute | solution.py:430
  14.4 9.4 %collective-permute-start.3 = (f32[10,256]{1,0:T(8,128)}, f32[10,256]{1,0:T(8,128)S(1)}, u32[]{:S(2)}, u32[]{:S(2)}) collective-permute-start(f32[10,256]{1,0:T(8,128)} %get-tuple-element.20), channel_id=1, source_target_pairs={{1,2},{2,1},{3,255},{5,6},{6,5},{7,251},{9,10},{10,9},{11,247},{13... | collective-permute-start | bytes 30728 | tf_op jit(solution)/shard_map/ppermute | solution.py:431
  23.8 0.1 broadcast_bitcast_fusion
  23.8 5.0 %shard_map.82 = (f32[10,64,256]{2,1,0:T(8,128)}, f32[64,40]{1,0:T(8,128)}, f32[50,256]{1,0:T(8,128)}) custom-call(s32[2]{0:T(128)} %si_ref.5, s32[2]{0:T(128)} %bitcast.11, s32[2]{0:T(128)} %pad_add_fusion.flag_ref, f32[10,10]{1,0:T(8,128)} %lm_ref.3, f32[10,64,256]{2,1,0:T(8,128)} %af_ref.1, f32[64,256]{1,0:T(8,128)} %d_ref.5, f32[4,10,64,256]{3,2,1,0:T(8,128)} %t_ref.3, ...), custom_call_target="tpu_custom_call" | custom-call | flops 9830400 | bytes 5242880 | tf_op jit(solution)/shard_map/pallas_call | solution.py:348
  28.9 0.0 collective-permute-done.1.rest_1_.hw_ref
  28.9 0.5 copy-done
  29.5 0.0 copy-done.1
  29.5 0.0 copy-done.2
  29.5 0.0 copy-done.3
  29.5 5.5 %shard_map.85 = (f32[64,10]{1,0:T(8,128)}, f32[64,10]{1,0:T(8,128)}, f32[10,256]{1,0:T(8,128)}, f32[10,256]{1,0:T(8,128)}) custom-call(s32[2]{0:T(128)} %bitcast.12, s32[2]{0:T(128)} %pad_add_fusion.flag_ref, f32[64,40]{1,0:T(8,128)} %get-tuple-element.21.lon_ref, f32[50,256]{1,0:T(8,128)} %get-tuple-element.22.lat_ref, f32[64,10]{1,0:T(8,128)} %copy-done, ...), custom_call_target="tpu_custom_call" | custom-call | flops 102400 | bytes 163840 | tf_op jit(solution)/shard_map/pallas_call | solution.py:368
  35.1 0.0 collective-permute-start.6
  35.1 5.2 %collective-permute-start.7 = (f32[10,256]{1,0:T(8,128)}, f32[10,256]{1,0:T(8,128)S(1)}, u32[]{:S(2)}, u32[]{:S(2)}) collective-permute-start(f32[10,256]{1,0:T(8,128)} %get-tuple-element.26), channel_id=1, source_target_pairs={{1,2},{2,1},{3,255},{5,6},{6,5},{7,251},{9,10},{10,9},{11,247},{13... | collective-permute-start | bytes 30728 | tf_op jit(solution)/shard_map/ppermute | solution.py:431
  40.3 0.1 collective-permute-start.5
  40.4 7.2 %collective-permute-start.4 = (f32[64,10]{1,0:T(8,128)}, f32[64,10]{1,0:T(8,128)S(1)}, u32[]{:S(2)}, u32[]{:S(2)}) collective-permute-start(f32[64,10]{1,0:T(8,128)} %get-tuple-element.23), channel_id=1, source_target_pairs={{0,252},{4,0},{8,4},{12,8},{16,12},{20,16},{24,20},{28,24},{32,28}... | collective-permute-start | bytes 7688 | tf_op jit(solution)/shard_map/ppermute | solution.py:428
  47.6 4.5 %shard_map.84 = f32[10,64,256]{2,1,0:T(8,128)} custom-call(s32[2]{0:T(128)} %si_ref.5, s32[2]{0:T(128)} %bitcast.13, s32[2]{0:T(128)} %pad_add_fusion.flag_ref, f32[10,10]{1,0:T(8,128)} %lm_ref.3, f32[10,64,256]{2,1,0:T(8,128)} %get-tuple-element.16.adj_ref, f32[64,256]{1,0:T(8,128)} %d_ref.5, f32[4,10,64,256]{3,2,1,0:T(8,128)} %t_ref.3, ...), custom_call_target="tpu_custom_call" | custom-call | flops 9830400 | bytes 5242880 | tf_op jit(solution)/shard_map/pallas_call | solution.py:348
  52.1 0.0 collective-permute-done.5
  52.1 0.1 copy.10
  52.2 0.1 copy.9
  52.3 0.0 collective-permute-done.7
  52.3 2.2 %multiply_add_fusion = f32[10,64,256]{2,1,0:T(8,128)} fusion(f32[10,64,256]{2,1,0:T(8,128)} %shard_map.84, f32[10,256]{1,0:T(8,128)S(1)} %get-tuple-element.28, f32[10,256]{1,0:T(8,128)S(1)} %get-tuple-element.27, f32[10,64]{1,0:T(8,128)S(1)} %copy.10, f32[10,64]{1,0:T(8,128)S(1)} %copy.9, f32[256]{0:T(256)S(1)} %broadcast_bitcast_fusion, ...), kind=kLoop, calls=%fused_computation | loop fusion | flops 1474560 | bytes 1337984 | tf_op jit(solution)/shard_map/add | solution.py:397
  (15 shorter events, 0.0 us)
Async XLA Ops:
  0.6 23.1 %copy-start.4 = (s32[1,2]{1,0:T(1,128)S(1)}, s32[1,2]{1,0:T(1,128)}, u32[]{:S(2)}) copy-start(s32[1,2]{1,0:T(1,128)} %param.14) | copy-start | bytes 28
  3.8 25.0 %collective-permute-start = (f32[64,10]{1,0:T(8,128)}, f32[64,10]{1,0:T(8,128)S(1)}, u32[]{:S(2)}, u32[]{:S(2)}) collective-permute-start(f32[64,10]{1,0:T(8,128)} %get-tuple-element.17), channel_id=1, source_target_pairs={{0,252},{4,0},{8,4},{12,8},{16,12},{20,16},{24,20},{28,24},{32,28}... | collective-permute-start | bytes 7688 | tf_op jit(solution)/shard_map/ppermute | solution.py:428
  13.4 15.5 %collective-permute-start.1 = (f32[64,10]{1,0:T(8,128)}, f32[64,10]{1,0:T(8,128)S(1)}, u32[]{:S(2)}, u32[]{:S(2)}) collective-permute-start(f32[64,10]{1,0:T(8,128)} %get-tuple-element.18), channel_id=1, source_target_pairs={{0,4},{4,8},{8,12},{12,16},{16,20},{20,24},{24,28},{28,32},{32,36}... | collective-permute-start | bytes 7688 | tf_op jit(solution)/shard_map/ppermute | solution.py:429
  13.4 15.5 %collective-permute-start.2 = (f32[10,256]{1,0:T(8,128)}, f32[10,256]{1,0:T(8,128)S(1)}, u32[]{:S(2)}, u32[]{:S(2)}) collective-permute-start(f32[10,256]{1,0:T(8,128)} %get-tuple-element.19), channel_id=1, source_target_pairs={{0,1},{1,0},{2,3},{3,2},{4,5},{5,4},{6,7},{7,6},{8,9},{9,8},{10,11... | collective-permute-start | bytes 30728 | tf_op jit(solution)/shard_map/ppermute | solution.py:430
  14.4 14.5 %collective-permute-start.3 = (f32[10,256]{1,0:T(8,128)}, f32[10,256]{1,0:T(8,128)S(1)}, u32[]{:S(2)}, u32[]{:S(2)}) collective-permute-start(f32[10,256]{1,0:T(8,128)} %get-tuple-element.20), channel_id=1, source_target_pairs={{1,2},{2,1},{3,255},{5,6},{6,5},{7,251},{9,10},{10,9},{11,247},{13... | collective-permute-start | bytes 30728 | tf_op jit(solution)/shard_map/ppermute | solution.py:431
  28.9 0.6 %copy-start = (f32[64,10]{1,0:T(8,128)}, f32[64,10]{1,0:T(8,128)S(1)}, u32[]{:S(2)}) copy-start(f32[64,10]{1,0:T(8,128)S(1)} %collective-permute-done.rest_0_.he_ref) | copy-start | bytes 7684
  28.9 0.6 %copy-start.1 = (f32[64,10]{1,0:T(8,128)}, f32[64,10]{1,0:T(8,128)S(1)}, u32[]{:S(2)}) copy-start(f32[64,10]{1,0:T(8,128)S(1)} %collective-permute-done.1.rest_1_.hw_ref) | copy-start | bytes 7684
  28.9 0.6 %copy-start.2 = (f32[10,256]{1,0:T(8,128)}, f32[10,256]{1,0:T(8,128)S(1)}, u32[]{:S(2)}) copy-start(f32[10,256]{1,0:T(8,128)S(1)} %collective-permute-done.2.rest_2_.ha_ref) | copy-start | bytes 30724
  28.9 0.6 %copy-start.3 = (f32[10,256]{1,0:T(8,128)}, f32[10,256]{1,0:T(8,128)S(1)}, u32[]{:S(2)}) copy-start(f32[10,256]{1,0:T(8,128)S(1)} %collective-permute-done.3.rest_3_.hb_ref) | copy-start | bytes 30724
  35.1 17.2 %collective-permute-start.6 = (f32[10,256]{1,0:T(8,128)}, f32[10,256]{1,0:T(8,128)S(1)}, u32[]{:S(2)}, u32[]{:S(2)}) collective-permute-start(f32[10,256]{1,0:T(8,128)} %get-tuple-element.25), channel_id=1, source_target_pairs={{0,1},{1,0},{2,3},{3,2},{4,5},{5,4},{6,7},{7,6},{8,9},{9,8},{10,11... | collective-permute-start | bytes 30728 | tf_op jit(solution)/shard_map/ppermute | solution.py:430
  35.1 17.2 %collective-permute-start.7 = (f32[10,256]{1,0:T(8,128)}, f32[10,256]{1,0:T(8,128)S(1)}, u32[]{:S(2)}, u32[]{:S(2)}) collective-permute-start(f32[10,256]{1,0:T(8,128)} %get-tuple-element.26), channel_id=1, source_target_pairs={{1,2},{2,1},{3,255},{5,6},{6,5},{7,251},{9,10},{10,9},{11,247},{13... | collective-permute-start | bytes 30728 | tf_op jit(solution)/shard_map/ppermute | solution.py:431
  40.3 11.8 %collective-permute-start.5 = (f32[64,10]{1,0:T(8,128)}, f32[64,10]{1,0:T(8,128)S(1)}, u32[]{:S(2)}, u32[]{:S(2)}) collective-permute-start(f32[64,10]{1,0:T(8,128)} %get-tuple-element.24), channel_id=1, source_target_pairs={{0,4},{4,8},{8,12},{12,16},{16,20},{20,24},{24,28},{28,32},{32,36}... | collective-permute-start | bytes 7688 | tf_op jit(solution)/shard_map/ppermute | solution.py:429
  40.4 11.8 %collective-permute-start.4 = (f32[64,10]{1,0:T(8,128)}, f32[64,10]{1,0:T(8,128)S(1)}, u32[]{:S(2)}, u32[]{:S(2)}) collective-permute-start(f32[64,10]{1,0:T(8,128)} %get-tuple-element.23), channel_id=1, source_target_pairs={{0,252},{4,0},{8,4},{12,8},{16,12},{20,16},{24,20},{28,24},{32,28}... | collective-permute-start | bytes 7688 | tf_op jit(solution)/shard_map/ppermute | solution.py:428

commit v9 on v6

--- a/solution.py
+++ b/solution.py
@@ -49,6 +49,11 @@
         return jnp.dot(part, flip, preferred_element_type=jnp.float32)
 
     return (perm(x1) + perm(x2)) + perm(x3)
+
+
+def lat_position(n_lat):
+    lat = lax.axis_index("lat")
+    return lat % 2 == 0, lat == n_lat - 1
 
 
 class Collector:
@@ -81,15 +86,14 @@
             fold = reverse_lanes(fold)
         pf_ref[...] = fold[:levels]
 
-    def finish_pairs(self, flag_ref, pe_ref, pw_ref, pa_ref, pb_ref):
+    def finish_pairs(self, n_lat, pe_ref, pw_ref, pa_ref, pb_ref):
         levels = self.levels
         pe_ref[...] = self.cols[0][:, :levels]
         pw_ref[...] = self.cols[1][:, :levels]
         north_going = self.rows_acc[0][:levels]
         south_going = self.rows_acc[1][:levels]
         fold = reverse_lanes(self.rows_acc[2])[:levels]
-        even = flag_ref[0] == 0
-        top = flag_ref[1] == 1
+        even, top = lat_position(n_lat)
         pa_ref[...] = jnp.where(even, south_going, north_going)
         pb_ref[...] = jnp.where(top, fold, jnp.where(even, north_going, south_going))
 
@@ -114,16 +118,26 @@
     )
 
 
-def prologue_kernel(si_ref, wt_ref, flag_ref, af_ref, d_ref, u_ref, v_ref, pe_ref, pw_ref, pa_ref, pb_ref):
+def prologue_kernel(n_lat, si_ref, wt_ref, af_ref, d_ref, u_ref, vlo_ref, vhi_ref, pe_ref, pw_ref, pa_ref, pb_ref):
     del si_ref
     levels, rows, width = af_ref.shape
     wet = wet_field(wt_ref, rows, width)
     d = d_ref[...]
+    tile = vhi_ref.shape[1]
     out = Collector(levels, rows, width, True)
     for l in range(levels):
-        coef = coefficients(l, d, u_ref[l], v_ref[l], rows, width)
+        u = u_ref[l]
+        v_first = vlo_ref[l, 0:1, :]
+        v_last = vhi_ref[l, tile - 1:tile, :]
+        coef = (
+            d[:, 0:1] + advect_scale * u[:, 0:1],
+            d[:, width - 1:width] - advect_scale * u[:, width - 1:width],
+            d[0:1, :] + advect_scale * v_first,
+            d[rows - 1:rows, :] - advect_scale * v_last,
+            d[rows - 1:rows, :] + advect_scale * v_last,
+        )
         out.add(l, *edge_values(*coef, af_ref[l] * wet, rows, width))
-    out.finish_pairs(flag_ref, pe_ref, pw_ref, pa_ref, pb_ref)
+    out.finish_pairs(n_lat, pe_ref, pw_ref, pa_ref, pb_ref)
 
 
 def core_kernel(first, emit, si_ref, wt_ref, lm_ref, adj_ref, d_ref, t_ref, u_ref, v_ref, *rest):
@@ -165,7 +179,7 @@
         coef.finish(ce_ref, cw_ref, cn_ref, cs_ref, cf_ref)
 
 
-def fix_kernel(emit, wt_ref, flag_ref, part_ref, he_ref, hw_ref, ha_ref, hb_ref, *rest):
+def fix_kernel(emit, n_lat, wt_ref, part_ref, he_ref, hw_ref, ha_ref, hb_ref, *rest):
     if emit:
         ce_ref, cw_ref, cn_ref, cs_ref, cf_ref, out_ref, pe_ref, pw_ref, pa_ref, pb_ref = rest
     else:
@@ -177,7 +191,7 @@
     lane = lax.broadcasted_iota(jnp.int32, (rows, TLON), 1)
     he = he_ref[...]
     hw = hw_ref[...]
-    even = flag_ref[0] == 0
+    even, _ = lat_position(n_lat)
     if emit:
         ce = ce_ref[...]
         cw = cw_ref[...]
@@ -200,7 +214,7 @@
             coef = (ce[:, l:l + 1], cw[:, l:l + 1], cn_ref[l:l + 1, :], cs_ref[l:l + 1, :], cf_ref[l:l + 1, :])
             out.add(l, *edge_values(*coef, new, rows, width))
     if emit:
-        out.finish_pairs(flag_ref, pe_ref, pw_ref, pa_ref, pb_ref)
+        out.finish_pairs(n_lat, pe_ref, pw_ref, pa_ref, pb_ref)
 
 
 def payload_shapes(levels, rows, width):
@@ -221,22 +235,25 @@
     return pl.BlockSpec((None, levels, rows, width), lambda i, si, *_: (si[k], 0, 0, 0))
 
 
-def run_prologue(k, si, wt, flags, af, d, zonal, merid):
+def run_prologue(k, n_lat, si, wt, af, d, zonal, merid):
     levels, rows, width = af.shape
     shapes = pair_shapes(levels, rows, width)
+    tile = 8
+    last = rows // tile - 1
+    v_lo = pl.BlockSpec((None, levels, tile, width), lambda i, si, *_: (si[k], 0, 0, 0))
+    v_hi = pl.BlockSpec((None, levels, tile, width), lambda i, si, *_: (si[k], 0, last, 0))
     n = levels * rows * width
     return pl.pallas_call(
-        prologue_kernel,
+        functools.partial(prologue_kernel, n_lat),
         out_shape=shapes,
         grid_spec=pltpu.PrefetchScalarGridSpec(
-            num_scalar_prefetch=3,
+            num_scalar_prefetch=2,
             grid=(1,),
-            in_specs=[whole(af.shape), whole(d.shape), state_spec(k, levels, rows, width),
-                      state_spec(k, levels, rows, width)],
+            in_specs=[whole(af.shape), whole(d.shape), state_spec(k, levels, rows, width), v_lo, v_hi],
             out_specs=[whole(s.shape) for s in shapes],
         ),
-        cost_estimate=pl.CostEstimate(flops=2 * n, bytes_accessed=12 * n, transcendentals=0),
-    )(si, wt, flags, af, d, zonal, merid)
+        cost_estimate=pl.CostEstimate(flops=2 * n, bytes_accessed=10 * n, transcendentals=0),
+    )(si, wt, af, d, zonal, merid, merid)
 
 
 def run_core(k, k_next, si, wt, lm, adj, d, tracer, zonal, merid):
@@ -268,20 +285,20 @@
     return outs[0], outs[1:]
 
 
-def run_fix(wt, flags, part, halos, coefs):
+def run_fix(n_lat, wt, part, halos, coefs):
     levels, rows, width = part.shape
     emit = bool(coefs)
-    args = [wt, flags, part, *halos, *coefs]
-    in_specs = [whole(x.shape) for x in args[2:]]
+    args = [wt, part, *halos, *coefs]
+    in_specs = [whole(x.shape) for x in args[1:]]
     out_shape = [jax.ShapeDtypeStruct(part.shape, jnp.float32)]
     if emit:
         out_shape += pair_shapes(levels, rows, width)
     n = levels * rows * width
     outs = pl.pallas_call(
-        functools.partial(fix_kernel, emit),
+        functools.partial(fix_kernel, emit, n_lat),
         out_shape=out_shape,
         grid_spec=pltpu.PrefetchScalarGridSpec(
-            num_scalar_prefetch=2,
+            num_scalar_prefetch=1,
             grid=(1,),
             in_specs=in_specs,
             out_specs=[whole(s.shape) for s in out_shape],
@@ -323,7 +340,6 @@
     n_lon = lax.axis_size("lon")
     wt = wet_tiles.reshape(-1)
     lat_index = lax.axis_index("lat")
-    flags = jnp.stack([lat_index % 2, (lat_index == n_lat - 1).astype(jnp.int32)]).astype(jnp.int32)
 
     to_west = shift_pairs(n_lon, -1, True)
     to_east = shift_pairs(n_lon, 1, True)
@@ -343,7 +359,7 @@
         hb = lax.ppermute(pb, ("lon", "lat"), pairs_b)
         return he, hw, ha, hb
 
-    payloads = run_prologue(STEPS - 1, state_index, wt, flags, adjoint_final, diffusivity,
+    payloads = run_prologue(STEPS - 1, n_lat, state_index, wt, adjoint_final, diffusivity,
                             stored_zonal, stored_meridional)
     adj = adjoint_final
     for back in range(STEPS):
@@ -353,7 +369,7 @@
         part, coefs = run_core(k, k_next, state_index, wt, level_mixing, adj, diffusivity,
                                stored_tracer, stored_zonal, stored_meridional)
         if coefs:
-            adj, payloads = run_fix(wt, flags, part, halos, coefs)
+            adj, payloads = run_fix(n_lat, wt, part, halos, coefs)
         else:
             adj = fix_in_xla(wet_tiles, lat_index, part, halos)
     return adj

time: 53.3 us -> 52.4 us (0.983)
  other arithmetic: 2.9 us -> 2.24 us
    another operation x1 -> x0, other arithmetic: 0.67 us -> none  [shards(): jnp.stack([lat_index % 2, (lat_index == n_lat - 1).astype(jnp.int32)])]
  transfers between devices with their start and end apart: 8 -> 8, of which waited for: 0 -> 0; matrix products, arithmetic and copies ran while one was open for 0% -> 0% of each run, Pallas kernels for 17% -> 18%
where the time goes in v9:
time: 52.4 us; the launch traced here: 52.1 us
  starting transfers between devices  32.5 us (62%)
  Pallas kernels  16.4 us (31%)
  other arithmetic  2.24 us (4%)
  local copies, waits for them, and re-layouts  0.83 us (2%)
    ppermute x2, starting transfers between devices, exchange(): he = lax.ppermute(pe, 'lon', to_west)  16.8 us
    ppermute x2, starting transfers between devices, exchange(): hb = lax.ppermute(pb, ('lon', 'lat'), pairs_b)  14.7 us
    pallas_call x2, Pallas kernels, run_core(): pl.pallas_call(functools.partial(core_kernel, first, emit), out_shape=out...  9.2 us
    pallas_call x1, Pallas kernels, run_fix(): pl.pallas_call(functools.partial(fix_kernel, emit, n_lat), out_shape=out_...  4.08 us
    pallas_call x1, Pallas kernels, run_prologue(): pl.pallas_call(functools.partial(prologue_kernel, n_lat), out_shape=shape...  3.09 us
    add x1, other arithmetic, fix_in_xla(): return part + wet * corr  2.21 us
  transfers between devices with their start and end apart: 8, of which 0 were waited for; matrix products, arithmetic and copies ran while one was open for 0% of the time, Pallas kernels for 18%

profile of v9, /device:TPU:3, one launch (start us, length us, event | category | flops | bytes accessed | tf_op | source)
XLA Modules:
  0.0 52.1 jit_solution(18023474836422163592)
XLA Ops:
  0.0 3.1 %shard_map.83 = (f32[64,10]{1,0:T(8,128)}, f32[64,10]{1,0:T(8,128)}, f32[10,256]{1,0:T(8,128)}, f32[10,256]{1,0:T(8,128)}) custom-call(s32[2]{0:T(128)} %si_ref.5, s32[2]{0:T(128)} %bitcast.8, f32[10,64,256]{2,1,0:T(8,128)} %af_ref.1, f32[64,256]{1,0:T(8,128)} %d_ref.5, f32[4,10,64,256]{3,2,1,0:T(8,128)} %u_ref.5, f32[4,10,64,256]{3,2,1,0:T(8,128)} %v_ref.3, ...), custom_call_target="tpu_custom_call" | custom-call | flops 327680 | bytes 1638400 | tf_op jit(solution)/shard_map/pallas_call | solution.py:246
  3.1 9.6 %collective-permute-start = (f32[64,10]{1,0:T(8,128)}, f32[64,10]{1,0:T(8,128)S(1)}, u32[]{:S(2)}, u32[]{:S(2)}) collective-permute-start(f32[64,10]{1,0:T(8,128)} %get-tuple-element.21), channel_id=1, source_target_pairs={{0,252},{4,0},{8,4},{12,8},{16,12},{20,16},{24,20},{28,24},{32,28}... | collective-permute-start | bytes 7688 | tf_op jit(solution)/shard_map/ppermute | solution.py:356
  12.7 0.0 collective-permute-start.1
  12.7 1.0 %collective-permute-start.2 = (f32[10,256]{1,0:T(8,128)}, f32[10,256]{1,0:T(8,128)S(1)}, u32[]{:S(2)}, u32[]{:S(2)}) collective-permute-start(f32[10,256]{1,0:T(8,128)} %get-tuple-element.23), channel_id=1, source_target_pairs={{0,1},{1,0},{2,3},{3,2},{4,5},{5,4},{6,7},{7,6},{8,9},{9,8},{10,11... | collective-permute-start | bytes 30728 | tf_op jit(solution)/shard_map/ppermute | solution.py:358
  13.6 9.4 %collective-permute-start.3 = (f32[10,256]{1,0:T(8,128)}, f32[10,256]{1,0:T(8,128)S(1)}, u32[]{:S(2)}, u32[]{:S(2)}) collective-permute-start(f32[10,256]{1,0:T(8,128)} %get-tuple-element.24), channel_id=1, source_target_pairs={{1,2},{2,1},{3,255},{5,6},{6,5},{7,251},{9,10},{10,9},{11,247},{13... | collective-permute-start | bytes 30728 | tf_op jit(solution)/shard_map/ppermute | solution.py:359
  23.0 0.1 broadcast_bitcast_fusion
  23.1 4.9 %shard_map.82 = (f32[10,64,256]{2,1,0:T(8,128)}, f32[64,10]{1,0:T(8,128)}, f32[64,10]{1,0:T(8,128)}, f32[10,256]{1,0:T(8,128)}, f32[10,256]{1,0:T(8,128)}, /*index=5*/f32[10,256]{1,0:T(8,128)}) custom-call(s32[2]{0:T(128)} %si_ref.5, s32[2]{0:T(128)} %bitcast.9, f32[10,10]{1,0:T(8,128)} %lm_ref.3, f32[10,64,256]{2,1,0:T(8,128)} %af_ref.1, f32[64,256]{1,0:T(8,128)} %d_ref.5, ...), custom_call_target="tpu_custom_call" | custom-call | flops 9830400 | bytes 5242880 | tf_op jit(solution)/shard_map/pallas_call | solution.py:273
  28.0 0.0 collective-permute-done.he_ref
  28.0 0.0 collective-permute-done.1.hw_ref
  28.0 0.0 collective-permute-done.2.ha_ref
  28.1 0.5 %copy-done = f32[64,10]{1,0:T(8,128)} copy-done((f32[64,10]{1,0:T(8,128)}, f32[64,10]{1,0:T(8,128)S(1)}, u32[]{:S(2)}) %copy-start) | copy-done | bytes 2584
  28.6 0.0 copy-done.1
  28.6 0.0 copy-done.2
  28.6 0.0 copy-done.3
  28.7 4.1 %shard_map.84 = (f32[10,64,256]{2,1,0:T(8,128)}, f32[64,10]{1,0:T(8,128)}, f32[64,10]{1,0:T(8,128)}, f32[10,256]{1,0:T(8,128)}, f32[10,256]{1,0:T(8,128)}) custom-call(s32[2]{0:T(128)} %bitcast.10, f32[10,64,256]{2,1,0:T(8,128)} %get-tuple-element.20.part_ref, f32[64,10]{1,0:T(8,128)} %copy-done, f32[64,10]{1,0:T(8,128)} %copy-done.1, f32[10,256]{1,0:T(8,128)} %copy-done.2, ...), custom_call_target="tpu_custom_call" | custom-call | flops 1638400 | bytes 1310720 | tf_op jit(solution)/shard_map/pallas_call | solution.py:297
  32.7 5.4 %collective-permute-start.7 = (f32[10,256]{1,0:T(8,128)}, f32[10,256]{1,0:T(8,128)S(1)}, u32[]{:S(2)}, u32[]{:S(2)}) collective-permute-start(f32[10,256]{1,0:T(8,128)} %get-tuple-element.34), channel_id=1, source_target_pairs={{1,2},{2,1},{3,255},{5,6},{6,5},{7,251},{9,10},{10,9},{11,247},{13... | collective-permute-start | bytes 30728 | tf_op jit(solution)/shard_map/ppermute | solution.py:359
  38.1 0.1 collective-permute-start.5
  38.2 7.2 %collective-permute-start.4 = (f32[64,10]{1,0:T(8,128)}, f32[64,10]{1,0:T(8,128)S(1)}, u32[]{:S(2)}, u32[]{:S(2)}) collective-permute-start(f32[64,10]{1,0:T(8,128)} %get-tuple-element.31), channel_id=1, source_target_pairs={{0,252},{4,0},{8,4},{12,8},{16,12},{20,16},{24,20},{28,24},{32,28}... | collective-permute-start | bytes 7688 | tf_op jit(solution)/shard_map/ppermute | solution.py:356
  45.4 4.3 %shard_map.85 = f32[10,64,256]{2,1,0:T(8,128)} custom-call(s32[2]{0:T(128)} %si_ref.5, s32[2]{0:T(128)} %bitcast.11, f32[10,10]{1,0:T(8,128)} %lm_ref.3, f32[10,64,256]{2,1,0:T(8,128)} %get-tuple-element.30.adj_ref, f32[64,256]{1,0:T(8,128)} %d_ref.5, f32[4,10,64,256]{3,2,1,0:T(8,128)} %t_ref.3, f32[4,10,64,256]{3,2,1,0:T(8,128)} %u_ref.5, ...), custom_call_target="tpu_custom_call" | custom-call | flops 9830400 | bytes 5242880 | tf_op jit(solution)/shard_map/pallas_call | solution.py:273
  49.7 0.1 copy.10
  49.8 0.0 collective-permute-done.4
  49.8 0.1 copy.9
  49.9 0.0 collective-permute-done.7
  49.9 2.2 %multiply_add_fusion = f32[10,64,256]{2,1,0:T(8,128)} fusion(f32[10,64,256]{2,1,0:T(8,128)} %shard_map.85, f32[10,256]{1,0:T(8,128)S(1)} %get-tuple-element.36, f32[10,256]{1,0:T(8,128)S(1)} %get-tuple-element.35, f32[10,64]{1,0:T(8,128)S(1)} %copy.10, f32[10,64]{1,0:T(8,128)S(1)} %copy.9, f32[256]{0:T(256)S(1)} %broadcast_bitcast_fusion, ...), kind=kLoop, calls=%fused_computation | loop fusion | flops 1474560 | bytes 1337984 | tf_op jit(solution)/shard_map/add | solution.py:326
  (14 shorter events, 0.0 us)
Async XLA Ops:
  0.0 23.0 %copy-start.4 = (s32[1,2]{1,0:T(1,128)S(1)}, s32[1,2]{1,0:T(1,128)}, u32[]{:S(2)}) copy-start(s32[1,2]{1,0:T(1,128)} %param.14) | copy-start | bytes 28
  3.1 24.9 %collective-permute-start = (f32[64,10]{1,0:T(8,128)}, f32[64,10]{1,0:T(8,128)S(1)}, u32[]{:S(2)}, u32[]{:S(2)}) collective-permute-start(f32[64,10]{1,0:T(8,128)} %get-tuple-element.21), channel_id=1, source_target_pairs={{0,252},{4,0},{8,4},{12,8},{16,12},{20,16},{24,20},{28,24},{32,28}... | collective-permute-start | bytes 7688 | tf_op jit(solution)/shard_map/ppermute | solution.py:356
  12.7 15.3 %collective-permute-start.1 = (f32[64,10]{1,0:T(8,128)}, f32[64,10]{1,0:T(8,128)S(1)}, u32[]{:S(2)}, u32[]{:S(2)}) collective-permute-start(f32[64,10]{1,0:T(8,128)} %get-tuple-element.22), channel_id=1, source_target_pairs={{0,4},{4,8},{8,12},{12,16},{16,20},{20,24},{24,28},{28,32},{32,36}... | collective-permute-start | bytes 7688 | tf_op jit(solution)/shard_map/ppermute | solution.py:357
  12.7 15.3 %collective-permute-start.2 = (f32[10,256]{1,0:T(8,128)}, f32[10,256]{1,0:T(8,128)S(1)}, u32[]{:S(2)}, u32[]{:S(2)}) collective-permute-start(f32[10,256]{1,0:T(8,128)} %get-tuple-element.23), channel_id=1, source_target_pairs={{0,1},{1,0},{2,3},{3,2},{4,5},{5,4},{6,7},{7,6},{8,9},{9,8},{10,11... | collective-permute-start | bytes 30728 | tf_op jit(solution)/shard_map/ppermute | solution.py:358
  13.6 14.4 %collective-permute-start.3 = (f32[10,256]{1,0:T(8,128)}, f32[10,256]{1,0:T(8,128)S(1)}, u32[]{:S(2)}, u32[]{:S(2)}) collective-permute-start(f32[10,256]{1,0:T(8,128)} %get-tuple-element.24), channel_id=1, source_target_pairs={{1,2},{2,1},{3,255},{5,6},{6,5},{7,251},{9,10},{10,9},{11,247},{13... | collective-permute-start | bytes 30728 | tf_op jit(solution)/shard_map/ppermute | solution.py:359
  28.0 0.6 %copy-start = (f32[64,10]{1,0:T(8,128)}, f32[64,10]{1,0:T(8,128)S(1)}, u32[]{:S(2)}) copy-start(f32[64,10]{1,0:T(8,128)S(1)} %collective-permute-done.he_ref) | copy-start | bytes 7684
  28.0 0.6 %copy-start.1 = (f32[64,10]{1,0:T(8,128)}, f32[64,10]{1,0:T(8,128)S(1)}, u32[]{:S(2)}) copy-start(f32[64,10]{1,0:T(8,128)S(1)} %collective-permute-done.1.hw_ref) | copy-start | bytes 7684
  28.0 0.6 %copy-start.2 = (f32[10,256]{1,0:T(8,128)}, f32[10,256]{1,0:T(8,128)S(1)}, u32[]{:S(2)}) copy-start(f32[10,256]{1,0:T(8,128)S(1)} %collective-permute-done.2.ha_ref) | copy-start | bytes 30724
  28.0 0.6 %copy-start.3 = (f32[10,256]{1,0:T(8,128)}, f32[10,256]{1,0:T(8,128)S(1)}, u32[]{:S(2)}) copy-start(f32[10,256]{1,0:T(8,128)S(1)} %collective-permute-done.3.hb_ref) | copy-start | bytes 30724
  32.7 17.2 %collective-permute-start.6 = (f32[10,256]{1,0:T(8,128)}, f32[10,256]{1,0:T(8,128)S(1)}, u32[]{:S(2)}, u32[]{:S(2)}) collective-permute-start(f32[10,256]{1,0:T(8,128)} %get-tuple-element.33), channel_id=1, source_target_pairs={{0,1},{1,0},{2,3},{3,2},{4,5},{5,4},{6,7},{7,6},{8,9},{9,8},{10,11... | collective-permute-start | bytes 30728 | tf_op jit(solution)/shard_map/ppermute | solution.py:358
  32.7 17.2 %collective-permute-start.7 = (f32[10,256]{1,0:T(8,128)}, f32[10,256]{1,0:T(8,128)S(1)}, u32[]{:S(2)}, u32[]{:S(2)}) collective-permute-start(f32[10,256]{1,0:T(8,128)} %get-tuple-element.34), channel_id=1, source_target_pairs={{1,2},{2,1},{3,255},{5,6},{6,5},{7,251},{9,10},{10,9},{11,247},{13... | collective-permute-start | bytes 30728 | tf_op jit(solution)/shard_map/ppermute | solution.py:359
  38.1 11.6 %collective-permute-start.5 = (f32[64,10]{1,0:T(8,128)}, f32[64,10]{1,0:T(8,128)S(1)}, u32[]{:S(2)}, u32[]{:S(2)}) collective-permute-start(f32[64,10]{1,0:T(8,128)} %get-tuple-element.32), channel_id=1, source_target_pairs={{0,4},{4,8},{8,12},{12,16},{16,20},{20,24},{24,28},{28,32},{32,36}... | collective-permute-start | bytes 7688 | tf_op jit(solution)/shard_map/ppermute | solution.py:357
  38.2 11.6 %collective-permute-start.4 = (f32[64,10]{1,0:T(8,128)}, f32[64,10]{1,0:T(8,128)S(1)}, u32[]{:S(2)}, u32[]{:S(2)}) collective-permute-start(f32[64,10]{1,0:T(8,128)} %get-tuple-element.31), channel_id=1, source_target_pairs={{0,252},{4,0},{8,4},{12,8},{16,12},{20,16},{24,20},{28,24},{32,28}... | collective-permute-start | bytes 7688 | tf_op jit(solution)/shard_map/ppermute | solution.py:356

commit v10 on v9

--- a/solution.py
+++ b/solution.py
@@ -6,6 +6,7 @@
 from jax.experimental import pallas as pl
 from jax.experimental.pallas import tpu as pltpu
 from jax.sharding import PartitionSpec as P
+
 
 TLON = 128
 STEPS = 2
@@ -98,7 +99,7 @@
         pb_ref[...] = jnp.where(top, fold, jnp.where(even, north_going, south_going))
 
 
-def coefficients(l, d, u, v, rows, width):
+def coefficients(d, u, v, rows, width):
     return (
         d[:, 0:1] + advect_scale * u[:, 0:1],
         d[:, width - 1:width] - advect_scale * u[:, width - 1:width],
@@ -174,7 +175,7 @@
         t = t_ref[l]
         out_ref[l] = wet * (a - 4.0 * s + east + west + north + south + vertical - damping * t * t * a)
         if emit:
-            coef.add(l, *coefficients(l, d, u2_ref[l], v2_ref[l], rows, width))
+            coef.add(l, *coefficients(d, u2_ref[l], v2_ref[l], rows, width))
     if emit:
         coef.finish(ce_ref, cw_ref, cn_ref, cs_ref, cf_ref)
 
@@ -309,7 +310,7 @@
 
 
 def fix_in_xla(wet_tiles, lat_index, part, halos):
-    levels, rows, width = part.shape
+    _, rows, width = part.shape
     he, hw, ha, hb = halos
     even = lat_index % 2 == 0
     north = jnp.where(even, ha, hb)
@@ -353,10 +354,10 @@
 
     def exchange(payloads):
         pe, pw, pa, pb = payloads
+        hb = lax.ppermute(pb, ("lon", "lat"), pairs_b)
+        ha = lax.ppermute(pa, "lat", pairs_a)
         he = lax.ppermute(pe, "lon", to_west)
         hw = lax.ppermute(pw, "lon", to_east)
-        ha = lax.ppermute(pa, "lat", pairs_a)
-        hb = lax.ppermute(pb, ("lon", "lat"), pairs_b)
         return he, hw, ha, hb
 
     payloads = run_prologue(STEPS - 1, n_lat, state_index, wt, adjoint_final, diffusivity,

time: 52.4 us -> 52.4 us (level)
  no operation moved by 1% of the time
where the time goes in v10:
time: 52.4 us; the launch traced here: 52.1 us
  starting transfers between devices  32.5 us (62%)
  Pallas kernels  16.4 us (31%)
  other arithmetic  2.24 us (4%)
  local copies, waits for them, and re-layouts  0.83 us (2%)
    ppermute x2, starting transfers between devices, exchange(): he = lax.ppermute(pe, 'lon', to_west)  16.8 us
    ppermute x2, starting transfers between devices, exchange(): hb = lax.ppermute(pb, ('lon', 'lat'), pairs_b)  14.7 us
    pallas_call x2, Pallas kernels, run_core(): pl.pallas_call(functools.partial(core_kernel, first, emit), out_shape=out...  9.2 us
    pallas_call x1, Pallas kernels, run_fix(): pl.pallas_call(functools.partial(fix_kernel, emit, n_lat), out_shape=out_...  4.08 us
    pallas_call x1, Pallas kernels, run_prologue(): pl.pallas_call(functools.partial(prologue_kernel, n_lat), out_shape=shape...  3.09 us
    add x1, other arithmetic, fix_in_xla(): return part + wet * corr  2.21 us
  transfers between devices with their start and end apart: 8, of which 0 were waited for; matrix products, arithmetic and copies ran while one was open for 0% of the time, Pallas kernels for 18%

profile of v10, /device:TPU:3, one launch (start us, length us, event | category | flops | bytes accessed | tf_op | source)
XLA Modules:
  0.0 52.1 jit_solution(18023474836422163592)
XLA Ops:
  0.0 3.1 %shard_map.83 = (f32[64,10]{1,0:T(8,128)}, f32[64,10]{1,0:T(8,128)}, f32[10,256]{1,0:T(8,128)}, f32[10,256]{1,0:T(8,128)}) custom-call(s32[2]{0:T(128)} %si_ref.5, s32[2]{0:T(128)} %bitcast.8, f32[10,64,256]{2,1,0:T(8,128)} %af_ref.1, f32[64,256]{1,0:T(8,128)} %d_ref.5, f32[4,10,64,256]{3,2,1,0:T(8,128)} %u_ref.5, f32[4,10,64,256]{3,2,1,0:T(8,128)} %v_ref.3, ...), custom_call_target="tpu_custom_call" | custom-call | flops 327680 | bytes 1638400 | tf_op jit(solution)/shard_map/pallas_call | solution.py:247
  3.1 9.6 %collective-permute-start = (f32[64,10]{1,0:T(8,128)}, f32[64,10]{1,0:T(8,128)S(1)}, u32[]{:S(2)}, u32[]{:S(2)}) collective-permute-start(f32[64,10]{1,0:T(8,128)} %get-tuple-element.21), channel_id=1, source_target_pairs={{0,252},{4,0},{8,4},{12,8},{16,12},{20,16},{24,20},{28,24},{32,28}... | collective-permute-start | bytes 7688 | tf_op jit(solution)/shard_map/ppermute | solution.py:359
  12.7 0.0 collective-permute-start.1
  12.7 1.0 %collective-permute-start.2 = (f32[10,256]{1,0:T(8,128)}, f32[10,256]{1,0:T(8,128)S(1)}, u32[]{:S(2)}, u32[]{:S(2)}) collective-permute-start(f32[10,256]{1,0:T(8,128)} %get-tuple-element.23), channel_id=1, source_target_pairs={{0,1},{1,0},{2,3},{3,2},{4,5},{5,4},{6,7},{7,6},{8,9},{9,8},{10,11... | collective-permute-start | bytes 30728 | tf_op jit(solution)/shard_map/ppermute | solution.py:358
  13.6 9.4 %collective-permute-start.3 = (f32[10,256]{1,0:T(8,128)}, f32[10,256]{1,0:T(8,128)S(1)}, u32[]{:S(2)}, u32[]{:S(2)}) collective-permute-start(f32[10,256]{1,0:T(8,128)} %get-tuple-element.24), channel_id=1, source_target_pairs={{1,2},{2,1},{3,255},{5,6},{6,5},{7,251},{9,10},{10,9},{11,247},{13... | collective-permute-start | bytes 30728 | tf_op jit(solution)/shard_map/ppermute | solution.py:357
  23.0 0.1 broadcast_bitcast_fusion
  23.1 4.9 %shard_map.82 = (f32[10,64,256]{2,1,0:T(8,128)}, f32[64,10]{1,0:T(8,128)}, f32[64,10]{1,0:T(8,128)}, f32[10,256]{1,0:T(8,128)}, f32[10,256]{1,0:T(8,128)}, /*index=5*/f32[10,256]{1,0:T(8,128)}) custom-call(s32[2]{0:T(128)} %si_ref.5, s32[2]{0:T(128)} %bitcast.9, f32[10,10]{1,0:T(8,128)} %lm_ref.3, f32[10,64,256]{2,1,0:T(8,128)} %af_ref.1, f32[64,256]{1,0:T(8,128)} %d_ref.5, ...), custom_call_target="tpu_custom_call" | custom-call | flops 9830400 | bytes 5242880 | tf_op jit(solution)/shard_map/pallas_call | solution.py:274
  28.0 0.0 collective-permute-done.he_ref
  28.0 0.0 collective-permute-done.2.ha_ref
  28.0 0.0 collective-permute-done.3.hb_ref
  28.1 0.5 %copy-done = f32[64,10]{1,0:T(8,128)} copy-done((f32[64,10]{1,0:T(8,128)}, f32[64,10]{1,0:T(8,128)S(1)}, u32[]{:S(2)}) %copy-start) | copy-done | bytes 2584
  28.6 0.0 copy-done.1
  28.6 0.0 copy-done.3
  28.7 4.1 %shard_map.84 = (f32[10,64,256]{2,1,0:T(8,128)}, f32[64,10]{1,0:T(8,128)}, f32[64,10]{1,0:T(8,128)}, f32[10,256]{1,0:T(8,128)}, f32[10,256]{1,0:T(8,128)}) custom-call(s32[2]{0:T(128)} %bitcast.10, f32[10,64,256]{2,1,0:T(8,128)} %get-tuple-element.20.part_ref, f32[64,10]{1,0:T(8,128)} %copy-done, f32[64,10]{1,0:T(8,128)} %copy-done.1, f32[10,256]{1,0:T(8,128)} %copy-done.2, ...), custom_call_target="tpu_custom_call" | custom-call | flops 1638400 | bytes 1310720 | tf_op jit(solution)/shard_map/pallas_call | solution.py:298
  32.7 0.0 collective-permute-start.6
  32.7 5.4 %collective-permute-start.7 = (f32[10,256]{1,0:T(8,128)}, f32[10,256]{1,0:T(8,128)S(1)}, u32[]{:S(2)}, u32[]{:S(2)}) collective-permute-start(f32[10,256]{1,0:T(8,128)} %get-tuple-element.34), channel_id=1, source_target_pairs={{1,2},{2,1},{3,255},{5,6},{6,5},{7,251},{9,10},{10,9},{11,247},{13... | collective-permute-start | bytes 30728 | tf_op jit(solution)/shard_map/ppermute | solution.py:357
  38.1 0.1 collective-permute-start.5
  38.2 7.2 %collective-permute-start.4 = (f32[64,10]{1,0:T(8,128)}, f32[64,10]{1,0:T(8,128)S(1)}, u32[]{:S(2)}, u32[]{:S(2)}) collective-permute-start(f32[64,10]{1,0:T(8,128)} %get-tuple-element.31), channel_id=1, source_target_pairs={{0,252},{4,0},{8,4},{12,8},{16,12},{20,16},{24,20},{28,24},{32,28}... | collective-permute-start | bytes 7688 | tf_op jit(solution)/shard_map/ppermute | solution.py:359
  45.4 4.3 %shard_map.85 = f32[10,64,256]{2,1,0:T(8,128)} custom-call(s32[2]{0:T(128)} %si_ref.5, s32[2]{0:T(128)} %bitcast.11, f32[10,10]{1,0:T(8,128)} %lm_ref.3, f32[10,64,256]{2,1,0:T(8,128)} %get-tuple-element.30.adj_ref, f32[64,256]{1,0:T(8,128)} %d_ref.5, f32[4,10,64,256]{3,2,1,0:T(8,128)} %t_ref.3, f32[4,10,64,256]{3,2,1,0:T(8,128)} %u_ref.5, ...), custom_call_target="tpu_custom_call" | custom-call | flops 9830400 | bytes 5242880 | tf_op jit(solution)/shard_map/pallas_call | solution.py:274
  49.7 0.0 collective-permute-done.5
  49.7 0.1 copy.10
  49.8 0.1 copy.9
  49.9 0.0 collective-permute-done.7
  49.9 2.2 %multiply_add_fusion = f32[10,64,256]{2,1,0:T(8,128)} fusion(f32[10,64,256]{2,1,0:T(8,128)} %shard_map.85, f32[10,256]{1,0:T(8,128)S(1)} %get-tuple-element.36, f32[10,256]{1,0:T(8,128)S(1)} %get-tuple-element.35, f32[10,64]{1,0:T(8,128)S(1)} %copy.10, f32[10,64]{1,0:T(8,128)S(1)} %copy.9, f32[256]{0:T(256)S(1)} %broadcast_bitcast_fusion, ...), kind=kLoop, calls=%fused_computation | loop fusion | flops 1474560 | bytes 1337984 | tf_op jit(solution)/shard_map/add | solution.py:327
  (14 shorter events, 0.0 us)
Async XLA Ops:
  0.0 23.0 %copy-start.4 = (s32[1,2]{1,0:T(1,128)S(1)}, s32[1,2]{1,0:T(1,128)}, u32[]{:S(2)}) copy-start(s32[1,2]{1,0:T(1,128)} %param.14) | copy-start | bytes 28
  3.1 24.9 %collective-permute-start = (f32[64,10]{1,0:T(8,128)}, f32[64,10]{1,0:T(8,128)S(1)}, u32[]{:S(2)}, u32[]{:S(2)}) collective-permute-start(f32[64,10]{1,0:T(8,128)} %get-tuple-element.21), channel_id=1, source_target_pairs={{0,252},{4,0},{8,4},{12,8},{16,12},{20,16},{24,20},{28,24},{32,28}... | collective-permute-start | bytes 7688 | tf_op jit(solution)/shard_map/ppermute | solution.py:359
  12.7 15.3 %collective-permute-start.1 = (f32[64,10]{1,0:T(8,128)}, f32[64,10]{1,0:T(8,128)S(1)}, u32[]{:S(2)}, u32[]{:S(2)}) collective-permute-start(f32[64,10]{1,0:T(8,128)} %get-tuple-element.22), channel_id=1, source_target_pairs={{0,4},{4,8},{8,12},{12,16},{16,20},{20,24},{24,28},{28,32},{32,36}... | collective-permute-start | bytes 7688 | tf_op jit(solution)/shard_map/ppermute | solution.py:360
  12.7 15.3 %collective-permute-start.2 = (f32[10,256]{1,0:T(8,128)}, f32[10,256]{1,0:T(8,128)S(1)}, u32[]{:S(2)}, u32[]{:S(2)}) collective-permute-start(f32[10,256]{1,0:T(8,128)} %get-tuple-element.23), channel_id=1, source_target_pairs={{0,1},{1,0},{2,3},{3,2},{4,5},{5,4},{6,7},{7,6},{8,9},{9,8},{10,11... | collective-permute-start | bytes 30728 | tf_op jit(solution)/shard_map/ppermute | solution.py:358
  13.6 14.4 %collective-permute-start.3 = (f32[10,256]{1,0:T(8,128)}, f32[10,256]{1,0:T(8,128)S(1)}, u32[]{:S(2)}, u32[]{:S(2)}) collective-permute-start(f32[10,256]{1,0:T(8,128)} %get-tuple-element.24), channel_id=1, source_target_pairs={{1,2},{2,1},{3,255},{5,6},{6,5},{7,251},{9,10},{10,9},{11,247},{13... | collective-permute-start | bytes 30728 | tf_op jit(solution)/shard_map/ppermute | solution.py:357
  28.0 0.6 %copy-start = (f32[64,10]{1,0:T(8,128)}, f32[64,10]{1,0:T(8,128)S(1)}, u32[]{:S(2)}) copy-start(f32[64,10]{1,0:T(8,128)S(1)} %collective-permute-done.he_ref) | copy-start | bytes 7684
  28.0 0.6 %copy-start.1 = (f32[64,10]{1,0:T(8,128)}, f32[64,10]{1,0:T(8,128)S(1)}, u32[]{:S(2)}) copy-start(f32[64,10]{1,0:T(8,128)S(1)} %collective-permute-done.1.hw_ref) | copy-start | bytes 7684
  28.0 0.6 %copy-start.2 = (f32[10,256]{1,0:T(8,128)}, f32[10,256]{1,0:T(8,128)S(1)}, u32[]{:S(2)}) copy-start(f32[10,256]{1,0:T(8,128)S(1)} %collective-permute-done.2.ha_ref) | copy-start | bytes 30724
  28.0 0.6 %copy-start.3 = (f32[10,256]{1,0:T(8,128)}, f32[10,256]{1,0:T(8,128)S(1)}, u32[]{:S(2)}) copy-start(f32[10,256]{1,0:T(8,128)S(1)} %collective-permute-done.3.hb_ref) | copy-start | bytes 30724
  32.7 17.2 %collective-permute-start.6 = (f32[10,256]{1,0:T(8,128)}, f32[10,256]{1,0:T(8,128)S(1)}, u32[]{:S(2)}, u32[]{:S(2)}) collective-permute-start(f32[10,256]{1,0:T(8,128)} %get-tuple-element.33), channel_id=1, source_target_pairs={{0,1},{1,0},{2,3},{3,2},{4,5},{5,4},{6,7},{7,6},{8,9},{9,8},{10,11... | collective-permute-start | bytes 30728 | tf_op jit(solution)/shard_map/ppermute | solution.py:358
  32.7 17.2 %collective-permute-start.7 = (f32[10,256]{1,0:T(8,128)}, f32[10,256]{1,0:T(8,128)S(1)}, u32[]{:S(2)}, u32[]{:S(2)}) collective-permute-start(f32[10,256]{1,0:T(8,128)} %get-tuple-element.34), channel_id=1, source_target_pairs={{1,2},{2,1},{3,255},{5,6},{6,5},{7,251},{9,10},{10,9},{11,247},{13... | collective-permute-start | bytes 30728 | tf_op jit(solution)/shard_map/ppermute | solution.py:357
  38.1 11.6 %collective-permute-start.5 = (f32[64,10]{1,0:T(8,128)}, f32[64,10]{1,0:T(8,128)S(1)}, u32[]{:S(2)}, u32[]{:S(2)}) collective-permute-start(f32[64,10]{1,0:T(8,128)} %get-tuple-element.32), channel_id=1, source_target_pairs={{0,4},{4,8},{8,12},{12,16},{16,20},{20,24},{24,28},{28,32},{32,36}... | collective-permute-start | bytes 7688 | tf_op jit(solution)/shard_map/ppermute | solution.py:360
  38.2 11.6 %collective-permute-start.4 = (f32[64,10]{1,0:T(8,128)}, f32[64,10]{1,0:T(8,128)S(1)}, u32[]{:S(2)}, u32[]{:S(2)}) collective-permute-start(f32[64,10]{1,0:T(8,128)} %get-tuple-element.31), channel_id=1, source_target_pairs={{0,252},{4,0},{8,4},{12,8},{16,12},{20,16},{24,20},{28,24},{32,28}... | collective-permute-start | bytes 7688 | tf_op jit(solution)/shard_map/ppermute | solution.py:359
